TPU v7x, 512 devices: a whole 4x4x16 slice. The times are simulated.
512 devices in a mesh: smp: 16 (over z), par: 32 (over x, y, core).
Axes of the slice: x: 4, y: 4, z: 16, core: 2. Of those that a mesh axis runs over, the one named last changes fastest.
Arguments:
- jacobian: bfloat16 [4096, 16384], P('smp', 'par'), may hold values from -52 to 52
Outputs:
- panel_factor: float32 [4096, 512], P('smp')
- schur_part: float32 [4096, 4096], P('smp', 'par')
All inputs are finite; a program needn't handle non-finite values.
Results may differ from a plain program's by a relative error of at most 0.0022.
Values may be sent and summed in bfloat16 or wider, within the bound.
No kernel may reach another device: no remote copies, remote signals or barrier semaphores. Data moves between devices by JAX's collectives and lax.ppermute only.
A program may use at most 64 MiB of HBM per device.

v0:
```python
import jax
import jax.numpy as jnp
from jax import lax
from jax.sharding import PartitionSpec as P

PANEL = 512


shift_scale = 0.01


def shards(jacobian):
    row_count, par_width = jacobian.shape
    par_count = lax.axis_size("par")
    smp_count = lax.axis_size("smp")
    sample_total = row_count * smp_count
    param_total = par_width * par_count
    col_width = sample_total // par_count
    row_index = lax.axis_index("smp")
    col_index = lax.axis_index("par")
    widened = jacobian.astype(jnp.float32)
    col_mean = lax.psum(jnp.sum(widened, axis=0), "smp") / sample_total
    centered = (widened - col_mean).astype(jnp.bfloat16)
    gathered = lax.all_gather(centered, "smp", axis=0, tiled=True)
    gram_tile = lax.psum_scatter(
        lax.dot_general(
            gathered, centered, (((1,), (1,)), ((), ())), preferred_element_type=jnp.float32
        )
        / param_total,
        "par",
        scatter_dimension=0,
        tiled=True,
    ).T
    global_rows = row_index * row_count + jnp.arange(row_count, dtype=jnp.int32)
    global_cols = col_index * col_width + jnp.arange(col_width, dtype=jnp.int32)
    diag_mask = global_rows[:, None] == global_cols[None, :]
    trace_total = lax.psum(jnp.sum(jnp.where(diag_mask, gram_tile, 0.0)), ("smp", "par"))
    shift_value = shift_scale * trace_total / sample_total
    shifted = gram_tile + jnp.where(diag_mask, shift_value, 0.0)
    col_keep = (col_index < PANEL // col_width).astype(jnp.float32)
    start_col = jnp.minimum(col_index, PANEL // col_width - 1) * col_width
    placed_rows = lax.dynamic_update_slice(
        jnp.zeros((row_count, PANEL), jnp.float32), shifted * col_keep, (jnp.int32(0), start_col)
    )
    panel_rows = lax.psum(placed_rows, "par")
    row_keep = (row_index < PANEL // row_count).astype(jnp.float32)
    start_row = jnp.minimum(row_index, PANEL // row_count - 1) * row_count
    top_square = lax.dynamic_update_slice(
        jnp.zeros((PANEL, PANEL), jnp.float32), panel_rows * row_keep, (start_row, jnp.int32(0))
    )
    top_band = lax.dynamic_update_slice(
        jnp.zeros((PANEL, col_width), jnp.float32), shifted * row_keep, (start_row, jnp.int32(0))
    )
    square, band_rows = lax.psum((top_square, top_band), "smp")
    factor = jnp.linalg.cholesky(square)
    panel_out = jax.scipy.linalg.solve_triangular(factor, panel_rows.T, lower=True).T
    band_factor = jax.scipy.linalg.solve_triangular(factor, band_rows, lower=True)
    schur_tile = shifted - jnp.dot(panel_out, band_factor, precision=lax.Precision.HIGHEST)
    return (panel_out, schur_tile)


def solution(mesh):
    placed = (P("smp", "par"),)
    return jax.shard_map(
        shards,
        mesh=mesh,
        in_specs=placed,
        out_specs=(P("smp", None), P("smp", "par")),
        check_vma=False,
    )
```

profile of v0, /device:TPU:1, one launch (start us, length us, event | category | flops | bytes accessed | tf_op | source)
XLA Modules:
  0.0 748.8 jit_solution(15600301314958486580)
XLA Ops:
  7.2 1.0 convert_reduce_fusion
  8.2 30.3 %psum.35 = f32[512]{0:T(512)S(1)} all-reduce(f32[512]{0:T(512)S(1)} %convert_reduce_fusion), channel_id=1, replica_groups=mesh['smp'=16,'par'=32] {'smp'}, use_global_device_ids=true, to_apply=%region_1.0 | all-reduce | flops 512 | bytes 4096 | tf_op jit(solution)/shard_map/psum | solution.py:22
  38.6 1.7 fusion.1
  40.3 73.0 %all-gather.2.cloned.1.call-done = bf16[4096,512]{1,0:T(8,128)(2,1)} async-done(((bf16[256,512]{1,0:T(8,128)(2,1)}), bf16[4096,512]{1,0:T(8,128)(2,1)}) %all-gather.2.cloned.1.call-update) | async-done | bytes 4194320 | tf_op jit(solution)/shard_map/all_gather | solution.py:24
  113.4 5.4 convolution_multiply_fusion
  118.9 108.8 %reduce-scatter.2.cloned.1.call-done = f32[128,256]{1,0:T(8,128)} async-done(((f32[4096,256]{1,0:T(8,128)}), f32[128,256]{1,0:T(8,128)}) %reduce-scatter.2.cloned.1.call-update) | async-done | bytes 131088 | tf_op jit(solution)/shard_map/reduce_scatter | solution.py:25
  227.7 1.6 fusion.29
  229.3 105.3 %psum.36 = f32[]{:T(128)} all-reduce(f32[]{:T(128)} %fusion.29), channel_id=1, replica_groups=mesh['smp'=16,'par'=32] {'smp','par'}, use_global_device_ids=true, to_apply=%region_4.5 | all-reduce | flops 1 | bytes 8 | tf_op jit(solution)/shard_map/psum | solution.py:37
  335.4 1.0 multiply_dynamic-update-slice_fusion.1
  336.4 0.8 copy-done.2
  337.2 0.2 all-reduce.7.cloned.1.call-start
  337.4 128.6 %all-reduce.5.cloned.1.call-done = f32[256,512]{0,1:T(8,128)} async-done(((f32[256,512]{0,1:T(8,128)}), f32[256,512]{0,1:T(8,128)}) %all-reduce.5.cloned.1.call-update) | async-done | bytes 524304 | tf_op jit(solution)/shard_map/psum | solution.py:45
  466.1 0.1 broadcast_in_dim.24
  466.2 1.1 multiply_dynamic-update-slice_fusion
  467.3 1.0 copy-done
  468.4 130.8 %all-reduce.7.cloned.1.call-done = (f32[512,512]{0,1:T(8,128)}, f32[512,128]{0,1:T(8,128)}) async-done(((f32[512,512]{0,1:T(8,128)}, f32[512,128]{0,1:T(8,128)}), (f32[512,512]{0,1:T(8,128)}, f32[512,128]{0,1:T(8,128)})) %all-reduce.7.cloned.1.call-update) | async-done | bytes 1310736 | tf_op jit(solution)/shard_map/psum | solution.py:54
  599.2 1.6 copy.3
  600.7 1.4 fusion
  602.2 11.7 %cholesky.103 = f32[128,128]{1,0:T(8,128)S(1)} custom-call(f32[128,128]{1,0:T(8,128)S(1)} %cholesky.263), custom_call_target="Cholesky" | custom-call | tf_op jit(solution)/shard_map/jit(cholesky)/cholesky | solution.py:55
  614.0 9.8 %custom-call.34 = f32[1,128,128]{1,2,0:T(8,128)S(1)} custom-call(f32[1,128,128]{2,1,0:T(8,128)S(1)} %get-tuple-element.35), custom_call_target="InvertDiagBlocksLowerTriangular" | custom-call | tf_op jit(solution)/shard_map/jit(cholesky)/cholesky | solution.py:55
  623.8 0.3 fusion.20
  624.1 0.3 convolution_subtract_fusion
  624.4 11.7 %cholesky.215 = f32[128,128]{1,0:T(8,128)S(1)} custom-call(f32[128,128]{1,0:T(8,128)S(1)} %cholesky.267), custom_call_target="Cholesky" | custom-call | tf_op jit(solution)/shard_map/jit(cholesky)/cholesky | solution.py:55
  636.3 0.1 copy.5
  636.5 0.1 cholesky.222
  636.7 10.0 %custom-call.35 = f32[1,128,128]{1,2,0:T(8,128)S(1)} custom-call(f32[1,128,128]{2,1,0:T(8,128)S(1)} %get-tuple-element.33), custom_call_target="InvertDiagBlocksLowerTriangular" | custom-call | tf_op jit(solution)/shard_map/jit(cholesky)/cholesky | solution.py:55
  646.7 0.3 convolution_dynamic-update-slice_fusion
  647.0 0.6 convolution_subtract_fusion.4
  647.6 11.7 %cholesky.236 = f32[128,128]{1,0:T(8,128)S(1)} custom-call(f32[128,128]{1,0:T(8,128)S(1)} %cholesky.272), custom_call_target="Cholesky" | custom-call | tf_op jit(solution)/shard_map/jit(cholesky)/cholesky | solution.py:55
  659.5 9.8 %custom-call.36 = f32[1,128,128]{1,2,0:T(8,128)S(1)} custom-call(f32[1,128,128]{2,1,0:T(8,128)S(1)} %get-tuple-element.31), custom_call_target="InvertDiagBlocksLowerTriangular" | custom-call | tf_op jit(solution)/shard_map/jit(cholesky)/cholesky | solution.py:55
  669.3 0.3 convolution_dynamic-update-slice_fusion.1
  669.6 0.5 convolution_subtract_fusion.9
  670.1 11.9 %cholesky.253 = f32[128,128]{1,0:T(8,128)S(1)} custom-call(f32[128,128]{1,0:T(8,128)S(1)} %convolution_subtract_fusion.9), custom_call_target="Cholesky" | custom-call | tf_op jit(solution)/shard_map/jit(cholesky)/cholesky | solution.py:55
  682.2 0.7 compare_reduce_fusion.1
  682.9 0.6 compare_reduce_fusion
  683.5 0.7 compare_reduce_fusion.2
  686.7 0.1 select_select_fusion
  686.8 8.8 %while.1 = (s32[]{:T(128)}, f32[512,512]{0,1:T(8,128)S(1)}, s32[4,2]{0,1:T(2,128)S(1)}, f32[4,128,128]{2,1,0:T(8,128)S(1)}, s32[]{:T(128)}) while((s32[]{:T(128)}, f32[512,512]{0,1:T(8,128)S(1)}, s32[4,2]{0,1:T(2,128)S(1)}, f32[4,128,128]{2,1,0:T(8,128)S(1)}, s32[]{:T(128)}) %tuple.30), condition=%wide.while_cond, body=%wide.while_body.sunk | while | flops 2 | bytes 393321 | solution.py:56
  686.9 0.6 fusion.73
  687.5 1.4 dynamic-slice.7
  689.1 0.6 fusion.73
  689.7 1.4 dynamic-slice.7
  691.3 0.6 fusion.73
  691.9 1.4 dynamic-slice.7
  693.5 0.6 fusion.73
  694.1 1.4 dynamic-slice.7
  695.6 39.3 %custom-call.37 = f32[4,128,128]{1,2,0:T(8,128)S(1)} custom-call(f32[4,128,128]{2,1,0:T(8,128)S(1)} %get-tuple-element.9), custom_call_target="InvertDiagBlocksLowerTriangular" | custom-call | tf_op jit(solution)/shard_map/jit(_solve_triangular)/triangular_solve | solution.py:56
  735.0 0.3 fusion.40
  735.3 0.3 convolution_subtract_fusion.7
  735.6 0.3 fusion.47
  735.9 0.4 convolution_subtract_fusion.6
  736.3 0.3 fusion.49
  736.5 0.5 convolution_subtract_fusion.8
  737.0 0.3 fusion.51
  737.3 0.3 fusion.31
  737.7 0.3 convolution_subtract_fusion.5
  738.0 0.3 fusion.48
  738.3 0.4 convolution_subtract_fusion.3
  738.7 0.3 fusion.50
  739.0 0.5 convolution_subtract_fusion.2
  739.5 0.3 fusion.52
  739.9 0.6 convolution_subtract_fusion.1
  740.5 0.8 copy.14
  741.3 1.0 copy.13
  (53 shorter events, 1.6 us)
Async XLA Ops:
  7.2 106.2 %all-gather.2.cloned.1.call-start = ((), (), s32[]{:S(2)}) async-start(), calls=%async_computation.1 | async-start | bytes 4456448 | tf_op jit(solution)/shard_map/all_gather | solution.py:24
  40.3 187.4 %reduce-scatter.2.cloned.1.call-start = ((), (), s32[]{:S(2)}) async-start(), calls=%async_computation.2 | async-start | bytes 4325376 | tf_op jit(solution)/shard_map/reduce_scatter | solution.py:25
  118.8 347.2 %all-reduce.5.cloned.1.call-start = ((), (), s32[]{:S(2)}) async-start(), calls=%async_computation.3 | async-start | bytes 1048576 | tf_op jit(solution)/shard_map/psum | solution.py:45
  336.4 0.8 copy-start.2
  336.4 130.9 %copy-start.3 = (f32[512,128]{0,1:T(8,128)}, f32[512,128]{0,1:T(8,128)S(1)}, u32[]{:S(2)}) copy-start(f32[512,128]{0,1:T(8,128)S(1)} %get-tuple-element.28) | copy-start | bytes 786436
  337.2 262.0 %all-reduce.7.cloned.1.call-start = ((), (), s32[]{:S(2)}) async-start(), calls=%async_computation.4 | async-start | bytes 2621440 | tf_op jit(solution)/shard_map/psum | solution.py:54
  467.3 1.0 copy-start
  636.4 98.5 %copy-start.5 = (f32[512,128]{0,1:T(8,128)S(1)}, f32[512,128]{0,1:T(8,128)}, u32[]{:S(2)}) copy-start(f32[512,128]{0,1:T(8,128)} %get-tuple-element.25) | copy-start | bytes 786436
  647.0 90.3 %copy-start.1 = (f32[256,512]{0,1:T(8,128)S(1)}, f32[256,512]{0,1:T(8,128)}, u32[]{:S(2)}) copy-start(f32[256,512]{0,1:T(8,128)} %all-reduce.5.cloned.1.call-done) | copy-start | bytes 1572868
  686.8 53.0 %copy-start.4 = (f32[128,256]{1,0:T(8,128)S(1)}, f32[128,256]{1,0:T(8,128)}, u32[]{:S(2)}) copy-start(f32[128,256]{1,0:T(8,128)} %reduce-scatter.2.cloned.1.call-done) | copy-start | bytes 393220
Sparse Core Ops, SparseCore 0:
  40.4 72.9 all-gather.1
  118.9 108.7 reduce-scatter.1
  337.3 128.6 all-reduce.4
  468.5 130.6 all-reduce.6
where the time goes:
time: 758 us; the launch traced here: 749 us
  waiting for transfers between devices  441 us (58%)
  blocking collectives  136 us (18%)
  other arithmetic  126 us (17%)
  between operations  17.4 us (2%)
  local copies, waits for them, and re-layouts  14.6 us (2%)
  matrix products  13.1 us (2%)
    psum x1, waiting for transfers between devices, shards(): square, band_rows = lax.psum((top_square, top_band), 'smp')  131 us
    psum x1, waiting for transfers between devices, shards(): panel_rows = lax.psum(placed_rows, 'par')  129 us
    reduce_scatter x1, waiting for transfers between devices, shards(): lax.psum_scatter(lax.dot_general(gathered, centered, (((1,), (1,)), ((),...  109 us
    psum x1, blocking collectives, shards(): lax.psum(jnp.sum(jnp.where(diag_mask, gram_tile, 0.0)), ('smp', 'par'))  105 us
    another operation x14, other arithmetic, shards(): factor = jnp.linalg.cholesky(square)  78.8 us
    all_gather x1, waiting for transfers between devices, shards(): gathered = lax.all_gather(centered, 'smp', axis=0, tiled=True)  73 us
    another operation x3, other arithmetic, shards(): jax.scipy.linalg.solve_triangular(factor, panel_rows.T, lower=True)  39.4 us
    psum x1, blocking collectives, shards(): col_mean = lax.psum(jnp.sum(widened, axis=0), 'smp') / sample_total  30.3 us
  transfers between devices with their start and end apart: 4, of which 4 were waited for; matrix products, arithmetic and copies ran while one was open for 0% of the time, Pallas kernels for 0%

commit v1 on v0

v1 whole, which is shorter than its diff:
```python
import jax
import jax.numpy as jnp
from jax import lax
from jax.sharding import PartitionSpec as P

PANEL = 512


shift_scale = 0.01


def shards(jacobian):
    row_count, par_width = jacobian.shape
    par_count = lax.axis_size("par")
    smp_count = lax.axis_size("smp")
    sample_total = row_count * smp_count
    param_total = par_width * par_count
    col_width = sample_total // par_count
    panel_piece = PANEL // par_count
    band_piece = col_width // smp_count
    row_index = lax.axis_index("smp")
    col_index = lax.axis_index("par")
    f32 = jnp.float32

    gathered = lax.all_gather(jacobian, "smp", axis=0, tiled=True)
    widened = gathered.astype(f32)
    col_mean = jnp.sum(widened, axis=0) / sample_total
    centered = (widened - col_mean).astype(jnp.bfloat16)
    mine = lax.dynamic_slice_in_dim(centered, row_index * row_count, row_count, 0)
    head = centered[:PANEL]
    contract = (((1,), (1,)), ((), ()))

    main = lax.dot_general(centered, mine, contract, preferred_element_type=f32)
    square = lax.dot_general(head, head, contract, preferred_element_type=f32)
    band_rows = lax.dynamic_index_in_dim(
        centered.reshape(par_count, smp_count, band_piece, par_width), row_index, 1, False
    ).reshape(par_count * band_piece, par_width)
    band = lax.dot_general(band_rows, head, contract, preferred_element_type=f32)
    sq = centered.astype(f32)
    sumsq = jnp.sum(sq * sq)

    width = row_count
    pieces = [
        main.reshape(par_count, col_width, width),
        main[:PANEL].reshape(par_count, panel_piece, width),
        square.reshape(par_count, panel_piece * PANEL // width, width),
        jnp.broadcast_to(sumsq, (par_count, 8, width)),
        band.reshape(par_count, band_piece * PANEL // width, width),
    ]
    stacked = jnp.concatenate(pieces, axis=1)
    chunk = stacked.shape[1]
    reduced = lax.psum_scatter(
        stacked.reshape(par_count * chunk, width), "par", scatter_dimension=0, tiled=True
    ) / param_total

    o1 = col_width
    o2 = o1 + panel_piece
    o3 = o2 + panel_piece * PANEL // width
    o4 = o3 + 8
    tile = reduced[:o1].T
    shared = lax.all_gather(reduced[o1:o4], "par", axis=0, tiled=False)
    band_mine = lax.all_gather(
        reduced[o4:].reshape(band_piece, PANEL), "smp", axis=0, tiled=True
    )
    panel_t = shared[:, : o2 - o1].reshape(PANEL, width)
    square_g = shared[:, o2 - o1 : o3 - o1].reshape(PANEL, PANEL)
    trace_total = shared[0, o3 - o1, 0]
    shift_value = shift_scale * trace_total / sample_total

    eye = jnp.arange(PANEL, dtype=jnp.int32)
    global_rows = row_index * row_count + jnp.arange(row_count, dtype=jnp.int32)
    global_cols = col_index * col_width + jnp.arange(col_width, dtype=jnp.int32)
    square_s = square_g + jnp.where(eye[:, None] == eye[None, :], shift_value, 0.0)
    panel_s = panel_t.T + jnp.where(global_rows[:, None] == eye[None, :], shift_value, 0.0)
    band_s = band_mine + jnp.where(global_cols[:, None] == eye[None, :], shift_value, 0.0)
    tile_s = tile + jnp.where(global_rows[:, None] == global_cols[None, :], shift_value, 0.0)

    factor = jnp.linalg.cholesky(square_s)
    panel_out = jax.scipy.linalg.solve_triangular(factor, panel_s.T, lower=True).T
    band_factor = jax.scipy.linalg.solve_triangular(factor, band_s.T, lower=True)
    schur_tile = tile_s - jnp.dot(panel_out, band_factor, precision=lax.Precision.HIGHEST)
    return (panel_out, schur_tile)


def solution(mesh):
    placed = (P("smp", "par"),)
    return jax.shard_map(
        shards,
        mesh=mesh,
        in_specs=placed,
        out_specs=(P("smp", None), P("smp", "par")),
        check_vma=False,
    )
```

time: 758 us -> 451 us (0.59)
  waiting for transfers between devices: 441 us -> 227 us
  blocking collectives: 136 us -> 25.6 us
  local copies, waits for them, and re-layouts: 14.6 us -> 33.8 us
    psum x2 -> x0, waiting for transfers between devices: 259 us -> none  [the longest x1 131 us: shards(): square, band_rows = lax.psum((top_square, top_band), 'smp')]
    psum x2 -> x0, blocking collectives: 136 us -> none  [the longest x1 105 us: shards(): lax.psum(jnp.sum(jnp.where(diag_mask, gram_tile, 0.0)), ('smp', 'par'))]
    unnamed x4, waiting for transfers between devices: 0.07 us -> 114 us
    reduce_scatter x1 -> x0, waiting for transfers between devices: 109 us -> none  [shards(): lax.psum_scatter(lax.dot_general(gathered, centered, (((1,), (1,)), ((),...]
    all_gather x1 -> x2, waiting for transfers between devices: 73 us -> 113 us  [the longest x1 77.4 us: shards(): gathered = lax.all_gather(jacobian, 'smp', axis=0, tiled=True)]
    all_gather x0 -> x1, blocking collectives: none -> 25.6 us  [shards(): lax.all_gather(reduced[o4:].reshape(band_piece, PANEL), 'smp', axis=0, ti...]
    unnamed x14 -> x16, local copies, waits for them, and re-layouts: 3.57 us -> 12 us
  transfers between devices with their start and end apart: 4 -> 3, of which waited for: 4 -> 3; matrix products, arithmetic and copies ran while one was open for 0% -> 0% of each run, Pallas kernels for 0% -> 0%
where the time goes in v1:
time: 451 us; the launch traced here: 446 us
  waiting for transfers between devices  227 us (50%)
  other arithmetic  126 us (28%)
  local copies, waits for them, and re-layouts  33.8 us (7%)
  blocking collectives  25.6 us (6%)
  between operations  17.6 us (4%)
  matrix products  15.9 us (4%)
    unnamed x4, waiting for transfers between devices  114 us
    another operation x14, other arithmetic, shards(): factor = jnp.linalg.cholesky(square_s)  78.8 us
    all_gather x1, waiting for transfers between devices, shards(): gathered = lax.all_gather(jacobian, 'smp', axis=0, tiled=True)  77.4 us
    another operation x3, other arithmetic, shards(): jax.scipy.linalg.solve_triangular(factor, panel_s.T, lower=True)  40.8 us
    all_gather x1, waiting for transfers between devices, shards(): shared = lax.all_gather(reduced[o1:o4], 'par', axis=0, tiled=False)  35.2 us
    all_gather x1, blocking collectives, shards(): lax.all_gather(reduced[o4:].reshape(band_piece, PANEL), 'smp', axis=0, ti...  25.6 us
    unnamed x16, local copies, waits for them, and re-layouts  12 us
    another operation x20, local copies, waits for them, and re-layouts  11.2 us
  transfers between devices with their start and end apart: 3, of which 3 were waited for; matrix products, arithmetic and copies ran while one was open for 0% of the time, Pallas kernels for 0%

profile of v1, /device:TPU:1, one launch (start us, length us, event | category | flops | bytes accessed | tf_op | source)
XLA Modules:
  0.0 445.8 jit_solution(17912938375229908624)
XLA Ops:
  7.2 0.7 all-gather.4.cloned.1.call-update
  7.9 77.4 %all-gather.4.cloned.1.call-done = bf16[4096,512]{1,0:T(8,128)(2,1)} async-done(((bf16[256,512]{1,0:T(8,128)(2,1)}), bf16[4096,512]{1,0:T(8,128)(2,1)}) %all-gather.4.cloned.1.call-update) | async-done | bytes 4194320 | tf_op jit(solution)/shard_map/all_gather | solution.py:25
  85.3 3.0 convert_reduce_fusion
  88.3 0.5 copy-done.1
  88.8 2.8 multiply_reduce_fusion
  91.6 0.5 fusion.4
  92.0 1.5 copy-done
  93.5 0.3 fusion.2
  93.9 5.5 %fusion.25 = f32[4096,256]{1,0:T(8,128)} fusion(bf16[4096,512]{1,0:T(8,128)(2,1)} %copy-done, s32[]{:T(128)S(6)} %select_n.28), kind=kOutput, calls=%fused_computation.52 | convolution fusion | flops 1073741824 | bytes 8650756 | tf_op jit(solution)/shard_map/dot_general | solution.py:33
  99.6 1.1 slice.190
  100.7 4.7 %constant_dynamic-update-slice_fusion.3 = f32[32,200,256]{2,1,0:T(8,128)} fusion(f32[32,128,256]{2,1,0:T(8,128)} %bitcast.78), kind=kLoop, calls=%fused_computation.108 | loop fusion | bytes 8388608
  105.4 0.9 constant_dynamic-update-slice_fusion.2
  106.3 1.1 constant_dynamic-update-slice_fusion.1
  107.3 1.4 broadcast_dynamic-update-slice_fusion
  108.7 0.9 constant_dynamic-update-slice_fusion
  109.7 113.6 %reduce-scatter.4.cloned.1.call-done = f32[200,256]{1,0:T(8,128)} async-done(((f32[6400,256]{1,0:T(8,128)}), f32[200,256]{1,0:T(8,128)}) %reduce-scatter.4.cloned.1.call-update) | async-done | bytes 204816
  223.2 1.1 copy.61
  224.4 0.7 copy.44
  225.1 0.5 iota_multiply_fusion
  225.8 25.6 %all_gather.15 = f32[128,512]{1,0:T(8,128)S(1)} all-gather(f32[8,512]{1,0:T(8,128)S(1)} %reshape.112), channel_id=1, replica_groups=mesh['smp'=16,'par'=32] {'smp'}, dimensions={0}, use_global_device_ids=true | all-gather | bytes 278528 | tf_op jit(solution)/shard_map/all_gather | solution.py:62
  251.4 0.8 copy.56
  252.3 35.2 %all-gather.6.cloned.1.call-done = f32[1792,256]{1,0:T(8,128)} async-done(((f32[56,256]{1,0:T(8,128)}), f32[1792,256]{1,0:T(8,128)}) %all-gather.6.cloned.1.call-update) | async-done | bytes 1835024 | tf_op jit(solution)/shard_map/all_gather | solution.py:61
  287.4 1.2 slice.194
  288.6 1.9 slice.195
  290.5 1.3 slice.193
  292.1 0.3 copy.45
  293.2 0.3 copy.46
  293.8 11.7 %cholesky.103 = f32[128,128]{1,0:T(8,128)S(1)} custom-call(f32[128,128]{1,0:T(8,128)S(1)} %cholesky.263), custom_call_target="Cholesky" | custom-call | tf_op jit(solution)/shard_map/jit(cholesky)/cholesky | solution.py:78
  305.7 9.8 %custom-call.34 = f32[1,128,128]{1,2,0:T(8,128)S(1)} custom-call(f32[1,128,128]{2,1,0:T(8,128)S(1)} %get-tuple-element.51), custom_call_target="InvertDiagBlocksLowerTriangular" | custom-call | tf_op jit(solution)/shard_map/jit(cholesky)/cholesky | solution.py:78
  315.5 0.3 fusion.28
  315.8 0.3 convolution_subtract_fusion
  316.3 11.7 %cholesky.215 = f32[128,128]{1,0:T(8,128)S(1)} custom-call(f32[128,128]{1,0:T(8,128)S(1)} %cholesky.267), custom_call_target="Cholesky" | custom-call | tf_op jit(solution)/shard_map/jit(cholesky)/cholesky | solution.py:78
  328.1 9.9 %custom-call.35 = f32[1,128,128]{1,2,0:T(8,128)S(1)} custom-call(f32[1,128,128]{2,1,0:T(8,128)S(1)} %get-tuple-element.49), custom_call_target="InvertDiagBlocksLowerTriangular" | custom-call | tf_op jit(solution)/shard_map/jit(cholesky)/cholesky | solution.py:78
  338.3 1.2 convolution_dynamic-update-slice_fusion
  339.5 0.6 convolution_subtract_fusion.4
  340.1 11.7 %cholesky.236 = f32[128,128]{1,0:T(8,128)S(1)} custom-call(f32[128,128]{1,0:T(8,128)S(1)} %cholesky.272), custom_call_target="Cholesky" | custom-call | tf_op jit(solution)/shard_map/jit(cholesky)/cholesky | solution.py:78
  352.0 9.8 %custom-call.36 = f32[1,128,128]{1,2,0:T(8,128)S(1)} custom-call(f32[1,128,128]{2,1,0:T(8,128)S(1)} %get-tuple-element.47), custom_call_target="InvertDiagBlocksLowerTriangular" | custom-call | tf_op jit(solution)/shard_map/jit(cholesky)/cholesky | solution.py:78
  362.1 0.5 convolution_subtract_fusion.9
  362.6 11.9 %cholesky.253 = f32[128,128]{1,0:T(8,128)S(1)} custom-call(f32[128,128]{1,0:T(8,128)S(1)} %convolution_subtract_fusion.9), custom_call_target="Cholesky" | custom-call | tf_op jit(solution)/shard_map/jit(cholesky)/cholesky | solution.py:78
  374.6 0.7 compare_reduce_fusion.1
  375.3 0.6 compare_reduce_fusion
  376.0 0.7 compare_reduce_fusion.2
  379.3 0.6 triangular_solve.124
  379.9 11.3 %while.1 = (s32[]{:T(128)}, f32[512,512]{0,1:T(8,128)S(1)}, s32[4,2]{0,1:T(2,128)S(1)}, f32[4,128,128]{2,1,0:T(8,128)}, s32[]{:T(128)}) while((s32[]{:T(128)}, f32[512,512]{0,1:T(8,128)S(1)}, s32[4,2]{0,1:T(2,128)S(1)}, f32[4,128,128]{2,1,0:T(8,128)}, s32[]{:T(128)}) %tuple.36), condition=%wide.while_cond, body=%wide.while_body.sunk | while | flops 2 | bytes 393329 | solution.py:79
  380.0 0.6 fusion.82
  380.6 1.4 dynamic-slice.7
  382.1 0.6 bitcast_dynamic-update-slice_fusion.2
  382.8 0.6 fusion.82
  383.4 1.4 dynamic-slice.7
  384.9 0.6 bitcast_dynamic-update-slice_fusion.2
  385.6 0.6 fusion.82
  386.2 1.4 dynamic-slice.7
  387.7 0.6 bitcast_dynamic-update-slice_fusion.2
  388.4 0.6 fusion.82
  389.0 1.4 dynamic-slice.7
  390.6 0.6 bitcast_dynamic-update-slice_fusion.2
  391.2 40.1 %custom-call.37 = f32[4,128,128]{1,2,0:T(8,128)S(1)} custom-call(f32[4,128,128]{2,1,0:T(8,128)} %get-tuple-element.9), custom_call_target="InvertDiagBlocksLowerTriangular" | custom-call | tf_op jit(solution)/shard_map/jit(_solve_triangular)/triangular_solve | solution.py:79
  432.3 0.4 convolution_subtract_fusion.6
  432.9 0.5 convolution_subtract_fusion.8
  434.4 0.3 fusion.55
  434.8 0.4 convolution_subtract_fusion.3
  435.5 0.5 convolution_subtract_fusion.2
  436.3 1.7 convolution_subtract_fusion.1
  438.0 1.0 copy.57
  (66 shorter events, 5.9 us)
Async XLA Ops:
  7.2 78.2 %all-gather.4.cloned.1.call-start = ((), (), s32[]{:S(2)}) async-start(), calls=%async_computation.1 | async-start | bytes 4456448 | tf_op jit(solution)/shard_map/all_gather | solution.py:25
  7.9 215.3 %reduce-scatter.4.cloned.1.call-start = ((), (), s32[]{:S(2)}) async-start(), calls=%async_computation.3 | async-start | bytes 6758400
  85.3 3.4 copy-start.1
  91.6 1.9 copy-start
  109.6 177.8 %all-gather.6.cloned.1.call-start = ((), (), s32[]{:S(2)}) async-start(), calls=%async_computation.2 | async-start | bytes 1892352 | tf_op jit(solution)/shard_map/all_gather | solution.py:61
  293.8 137.6 %copy-start.3 = (f32[128,512]{0,1:T(8,128)S(1)}, f32[128,512]{0,1:T(8,128)}, u32[]{:S(2)}) copy-start(f32[128,512]{0,1:T(8,128)} %copy.56) | copy-start | bytes 786436
  293.8 140.0 %copy-start.2 = (f32[32,16,256]{2,1,0:T(8,128)S(1)}, f32[32,16,256]{2,1,0:T(8,128)}, u32[]{:S(2)}) copy-start(f32[32,16,256]{2,1,0:T(8,128)} %slice.195) | copy-start | bytes 1572868
  316.1 12.0 %copy-start.4 = (f32[384,128]{1,0:T(8,128)}, f32[384,128]{1,0:T(8,128)S(1)}, u32[]{:S(2)}) copy-start(f32[384,128]{1,0:T(8,128)S(1)} %convolution_subtract_fusion) | copy-start | bytes 589828
Sparse Core Ops, SparseCore 0:
  10.1 75.2 all-gather.3
  109.7 113.4 reduce-scatter.3
  227.0 60.4 all-gather.5

commit v2 on v1

--- a/solution.py
+++ b/solution.py
@@ -17,7 +17,6 @@
     param_total = par_width * par_count
     col_width = sample_total // par_count
     panel_piece = PANEL // par_count
-    band_piece = col_width // smp_count
     row_index = lax.axis_index("smp")
     col_index = lax.axis_index("par")
     f32 = jnp.float32
@@ -32,39 +31,45 @@
 
     main = lax.dot_general(centered, mine, contract, preferred_element_type=f32)
     square = lax.dot_general(head, head, contract, preferred_element_type=f32)
-    band_rows = lax.dynamic_index_in_dim(
-        centered.reshape(par_count, smp_count, band_piece, par_width), row_index, 1, False
-    ).reshape(par_count * band_piece, par_width)
-    band = lax.dot_general(band_rows, head, contract, preferred_element_type=f32)
+    band = lax.dot_general(centered, head, contract, preferred_element_type=f32)
     sq = centered.astype(f32)
     sumsq = jnp.sum(sq * sq)
 
     width = row_count
-    pieces = [
-        main.reshape(par_count, col_width, width),
-        main[:PANEL].reshape(par_count, panel_piece, width),
-        square.reshape(par_count, panel_piece * PANEL // width, width),
-        jnp.broadcast_to(sumsq, (par_count, 8, width)),
-        band.reshape(par_count, band_piece * PANEL // width, width),
-    ]
-    stacked = jnp.concatenate(pieces, axis=1)
-    chunk = stacked.shape[1]
+    panel_parts = jnp.concatenate(
+        [
+            main[:PANEL].reshape(par_count, panel_piece, width),
+            square.reshape(par_count, panel_piece * PANEL // width, width),
+            jnp.broadcast_to(sumsq, (par_count, 8, width)),
+        ],
+        axis=1,
+    )
+    chunk = panel_parts.shape[1]
     reduced = lax.psum_scatter(
-        stacked.reshape(par_count * chunk, width), "par", scatter_dimension=0, tiled=True
+        panel_parts.reshape(par_count * chunk, width), "par", scatter_dimension=0, tiled=True
     ) / param_total
+    shared = lax.all_gather(reduced, "par", axis=0, tiled=False)
 
-    o1 = col_width
-    o2 = o1 + panel_piece
+    main_parts = jnp.concatenate(
+        [
+            main.reshape(par_count, col_width, width),
+            band.reshape(par_count, col_width * PANEL // width, width),
+        ],
+        axis=1,
+    )
+    main_parts, shared = lax.optimization_barrier((main_parts, shared))
+    main_chunk = main_parts.shape[1]
+    reduced_main = lax.psum_scatter(
+        main_parts.reshape(par_count * main_chunk, width), "par", scatter_dimension=0, tiled=True
+    ) / param_total
+    tile = reduced_main[:col_width].T
+    band_mine = reduced_main[col_width:].reshape(col_width, PANEL)
+
+    o2 = panel_piece
     o3 = o2 + panel_piece * PANEL // width
-    o4 = o3 + 8
-    tile = reduced[:o1].T
-    shared = lax.all_gather(reduced[o1:o4], "par", axis=0, tiled=False)
-    band_mine = lax.all_gather(
-        reduced[o4:].reshape(band_piece, PANEL), "smp", axis=0, tiled=True
-    )
-    panel_t = shared[:, : o2 - o1].reshape(PANEL, width)
-    square_g = shared[:, o2 - o1 : o3 - o1].reshape(PANEL, PANEL)
-    trace_total = shared[0, o3 - o1, 0]
+    panel_t = shared[:, :o2].reshape(PANEL, width)
+    square_g = shared[:, o2:o3].reshape(PANEL, PANEL)
+    trace_total = shared[0, o3, 0]
     shift_value = shift_scale * trace_total / sample_total
 
     eye = jnp.arange(PANEL, dtype=jnp.int32)

time: 451 us -> 444 us (0.984)
  blocking collectives: 25.6 us -> 0 us
  other arithmetic: 126 us -> 139 us
  waiting for transfers between devices: 227 us -> 218 us
  local copies, waits for them, and re-layouts: 33.8 us -> 41.5 us
  matrix products: 15.9 us -> 20.7 us
    unnamed x4, waiting for transfers between devices: 114 us -> 0.73 us
    reduce_scatter x0 -> x2, waiting for transfers between devices: none -> 105 us  [the longest x1 105 us: shards(): lax.psum_scatter(panel_parts.reshape(par_count * chunk, width), 'par', sc...]
    all_gather x1 -> x0, blocking collectives: 25.6 us -> none  [shards(): lax.all_gather(reduced[o4:].reshape(band_piece, PANEL), 'smp', axis=0, ti...]
    reshape x4 -> x5, local copies, waits for them, and re-layouts: 0.71 us -> 23.1 us  [the longest x1 13.1 us: shards(): main_parts.reshape(par_count * main_chunk, width)]
    concatenate x0 -> x2, other arithmetic: none -> 12.1 us  [the longest x1 10.5 us: shards(): jnp.concatenate([main.reshape(par_count, col_width, width), band.reshape(...]
    dot_general x1, matrix products: 0.33 us -> 7.97 us  [shards(): band = lax.dot_general(centered, head, contract, preferred_element_type=f32)]
    unnamed x16 -> x11, local copies, waits for them, and re-layouts: 12 us -> 6.81 us
  transfers between devices with their start and end apart: 3 -> 4, of which waited for: 3 -> 3; matrix products, arithmetic and copies ran while one was open for 0% -> 37% of each run, Pallas kernels for 0% -> 0%
where the time goes in v2:
time: 444 us; the launch traced here: 437 us
  waiting for transfers between devices  218 us (49%)
  other arithmetic  139 us (31%)
  local copies, waits for them, and re-layouts  41.5 us (9%)
  matrix products  20.7 us (5%)
  between operations  17.7 us (4%)
    reduce_scatter x1, waiting for transfers between devices, shards(): lax.psum_scatter(panel_parts.reshape(par_count * chunk, width), 'par', sc...  105 us
    another operation x14, other arithmetic, shards(): factor = jnp.linalg.cholesky(square_s)  78.7 us
    all_gather x1, waiting for transfers between devices, shards(): gathered = lax.all_gather(jacobian, 'smp', axis=0, tiled=True)  77.4 us
    another operation x3, other arithmetic, shards(): jax.scipy.linalg.solve_triangular(factor, panel_s.T, lower=True)  39.5 us
    all_gather x1, waiting for transfers between devices, shards(): shared = lax.all_gather(reduced, 'par', axis=0, tiled=False)  34.7 us
    reshape x1, local copies, waits for them, and re-layouts, shards(): main_parts.reshape(par_count * main_chunk, width)  13.1 us
    concatenate x1, other arithmetic, shards(): jnp.concatenate([main.reshape(par_count, col_width, width), band.reshape(...  10.5 us
    reshape x1, local copies, waits for them, and re-layouts, shards(): band.reshape(par_count, col_width * PANEL // width, width)  9.33 us
  transfers between devices with their start and end apart: 4, of which 3 were waited for; matrix products, arithmetic and copies ran while one was open for 37% of the time, Pallas kernels for 0%

profile of v2, /device:TPU:1, one launch (start us, length us, event | category | flops | bytes accessed | tf_op | source)
XLA Modules:
  0.0 437.3 jit_solution(6986741140144333234)
XLA Ops:
  7.2 0.7 all-gather.4.cloned.1.call-update
  7.9 77.4 %all-gather.4.cloned.1.call-done = bf16[4096,512]{1,0:T(8,128)(2,1)} async-done(((bf16[256,512]{1,0:T(8,128)(2,1)}), bf16[4096,512]{1,0:T(8,128)(2,1)}) %all-gather.4.cloned.1.call-update) | async-done | bytes 4194320 | tf_op jit(solution)/shard_map/all_gather | solution.py:24
  85.3 3.0 convert_reduce_fusion
  88.3 0.5 copy-done.2
  88.8 2.8 multiply_reduce_fusion
  91.6 2.0 copy-done
  93.5 0.5 fusion.2
  94.2 3.5 fusion.23
  97.7 1.9 copy-done.1
  99.7 0.6 broadcast_in_dim.46
  100.4 1.5 maximum_maximum_fusion
  102.0 105.5 %reduce-scatter.3.cloned.1.call-done = f32[56,256]{1,0:T(8,128)} async-done(((f32[1792,256]{1,0:T(8,128)}), f32[56,256]{1,0:T(8,128)}) %reduce-scatter.3.cloned.1.call-update) | async-done | bytes 57360 | tf_op jit(solution)/shard_map/reduce_scatter | solution.py:48
  207.5 1.4 broadcast_multiply_fusion.1
  209.0 8.0 %fusion.4 = f32[4096,512]{1,0:T(8,128)} fusion(bf16[4096,512]{1,0:T(8,128)(2,1)} %copy-done), kind=kOutput, calls=%fused_computation.31 | convolution fusion | flops 2147483648 | bytes 13107200 | tf_op jit(solution)/shard_map/dot_general | solution.py:34
  217.0 9.3 %reshape.100 = f32[32,256,256]{2,1,0:T(8,128)} reshape(f32[4096,512]{1,0:T(8,128)} %fusion.4) | data formatting | bytes 16777216 | tf_op jit(solution)/shard_map/reshape | solution.py:56
  226.3 10.5 %pad_maximum_fusion = f32[32,384,256]{2,1,0:T(8,128)} fusion(f32[32,256,256]{2,1,0:T(8,128)} %reshape.100, f32[32,128,256]{2,1,0:T(8,128)} %bitcast.75), kind=kLoop, calls=%fused_computation.2 | loop fusion | flops 3145728 | bytes 25165824 | tf_op jit(solution)/shard_map/concatenate | solution.py:53
  236.8 34.7 %all-gather.6.cloned.1.call-done = f32[1792,256]{1,0:T(8,128)} async-done(((f32[56,256]{1,0:T(8,128)}), f32[1792,256]{1,0:T(8,128)}) %all-gather.6.cloned.1.call-update) | async-done | bytes 1835024 | tf_op jit(solution)/shard_map/all_gather | solution.py:51
  271.5 13.1 %copy.29 = f32[12288,256]{0,1:T(8,128)} copy(f32[12288,256]{1,0:T(8,128)} %bitcast.74) | data formatting | bytes 25165824 | tf_op jit(solution)/shard_map/reshape | solution.py:63
  284.7 1.4 copy-done.4
  286.1 0.5 slice.171
  286.6 0.9 slice.172
  287.6 0.3 reshape.104
  287.9 0.3 copy.14
  289.0 0.3 copy.15
  289.6 11.7 %cholesky.103 = f32[128,128]{1,0:T(8,128)S(1)} custom-call(f32[128,128]{1,0:T(8,128)S(1)} %cholesky.263), custom_call_target="Cholesky" | custom-call | tf_op jit(solution)/shard_map/jit(cholesky)/cholesky | solution.py:83
  301.5 9.8 %custom-call.34 = f32[1,128,128]{1,2,0:T(8,128)S(1)} custom-call(f32[1,128,128]{2,1,0:T(8,128)S(1)} %get-tuple-element.43), custom_call_target="InvertDiagBlocksLowerTriangular" | custom-call | tf_op jit(solution)/shard_map/jit(cholesky)/cholesky | solution.py:83
  311.3 0.3 fusion.26
  311.7 0.3 convolution_subtract_fusion
  312.1 11.7 %cholesky.215 = f32[128,128]{1,0:T(8,128)S(1)} custom-call(f32[128,128]{1,0:T(8,128)S(1)} %cholesky.267), custom_call_target="Cholesky" | custom-call | tf_op jit(solution)/shard_map/jit(cholesky)/cholesky | solution.py:83
  323.9 9.9 %custom-call.35 = f32[1,128,128]{1,2,0:T(8,128)S(1)} custom-call(f32[1,128,128]{2,1,0:T(8,128)S(1)} %get-tuple-element.41), custom_call_target="InvertDiagBlocksLowerTriangular" | custom-call | tf_op jit(solution)/shard_map/jit(cholesky)/cholesky | solution.py:83
  334.1 0.3 convolution_dynamic-update-slice_fusion
  334.4 0.6 convolution_subtract_fusion.4
  335.0 11.7 %cholesky.236 = f32[128,128]{1,0:T(8,128)S(1)} custom-call(f32[128,128]{1,0:T(8,128)S(1)} %cholesky.272), custom_call_target="Cholesky" | custom-call | tf_op jit(solution)/shard_map/jit(cholesky)/cholesky | solution.py:83
  346.8 9.8 %custom-call.36 = f32[1,128,128]{1,2,0:T(8,128)S(1)} custom-call(f32[1,128,128]{2,1,0:T(8,128)S(1)} %get-tuple-element.39), custom_call_target="InvertDiagBlocksLowerTriangular" | custom-call | tf_op jit(solution)/shard_map/jit(cholesky)/cholesky | solution.py:83
  356.7 0.3 convolution_dynamic-update-slice_fusion.1
  357.0 0.5 convolution_subtract_fusion.9
  357.5 11.9 %cholesky.253 = f32[128,128]{1,0:T(8,128)S(1)} custom-call(f32[128,128]{1,0:T(8,128)S(1)} %convolution_subtract_fusion.9), custom_call_target="Cholesky" | custom-call | tf_op jit(solution)/shard_map/jit(cholesky)/cholesky | solution.py:83
  369.5 0.6 compare_reduce_fusion.2
  371.3 0.6 compare_reduce_fusion.1
  372.7 0.6 compare_reduce_fusion
  374.1 8.1 %while.1 = (s32[]{:T(128)}, f32[512,512]{0,1:T(8,128)S(1)}, s32[4,2]{0,1:T(2,128)S(1)}, f32[4,128,128]{2,1,0:T(8,128)S(1)}, s32[]{:T(128)}) while((s32[]{:T(128)}, f32[512,512]{0,1:T(8,128)S(1)}, s32[4,2]{0,1:T(2,128)S(1)}, f32[4,128,128]{2,1,0:T(8,128)S(1)}, s32[]{:T(128)}) %tuple.34), condition=%wide.while_cond, body=%wide.while_body.sunk | while | flops 2 | bytes 393329 | solution.py:84
  374.2 0.5 fusion.80
  374.7 1.3 dynamic-slice.7
  376.2 0.5 fusion.80
  376.8 1.3 dynamic-slice.7
  378.3 0.5 fusion.80
  378.8 1.3 dynamic-slice.7
  380.3 0.5 fusion.80
  380.8 1.3 dynamic-slice.7
  382.2 39.3 %custom-call.37 = f32[4,128,128]{1,2,0:T(8,128)S(1)} custom-call(f32[4,128,128]{2,1,0:T(8,128)S(1)} %get-tuple-element.13), custom_call_target="InvertDiagBlocksLowerTriangular" | custom-call | tf_op jit(solution)/shard_map/jit(_solve_triangular)/triangular_solve | solution.py:84
  421.6 0.3 fusion.36
  422.0 0.3 convolution_subtract_fusion.5
  422.3 0.3 fusion.53
  422.6 0.4 convolution_subtract_fusion.3
  423.0 0.3 fusion.55
  423.3 0.5 convolution_subtract_fusion.2
  423.8 0.3 fusion.57
  424.2 1.0 copy.26
  425.2 1.0 broadcast_multiply_fusion
  426.8 0.3 convolution_subtract_fusion.7
  427.4 0.4 convolution_subtract_fusion.6
  428.1 0.5 convolution_subtract_fusion.8
  428.6 0.3 fusion.56
  428.9 1.7 convolution_subtract_fusion.1
  (65 shorter events, 3.9 us)
Async XLA Ops:
  7.2 78.2 %all-gather.4.cloned.1.call-start = ((), (), s32[]{:S(2)}) async-start(), calls=%async_computation.2 | async-start | bytes 4456448 | tf_op jit(solution)/shard_map/all_gather | solution.py:24
  7.9 199.6 %reduce-scatter.3.cloned.1.call-start = ((), (), s32[]{:S(2)}) async-start(), calls=%async_computation.3 | async-start | bytes 1892352 | tf_op jit(solution)/shard_map/reduce_scatter | solution.py:48
  85.3 3.4 copy-start.2
  91.6 2.0 copy-start
  97.7 1.9 copy-start.1
  101.9 169.6 %all-gather.6.cloned.1.call-start = ((), (), s32[]{:S(2)}) async-start(), calls=%async_computation.5 | async-start | bytes 1892352 | tf_op jit(solution)/shard_map/all_gather | solution.py:51
  208.9 216.2 %reduce-scatter.5.cloned.1.call-start = ((), (), s32[]{:S(2)}) async-start(), calls=%async_computation.4 | async-start | bytes 12976128 | tf_op jit(solution)/shard_map/reduce_scatter | solution.py:62
  284.6 1.5 copy-start.4
  323.9 97.7 %copy-start.3 = (f32[32,16,256]{2,1,0:T(8,128)S(1)}, f32[32,16,256]{2,1,0:T(8,128)}, u32[]{:S(2)}) copy-start(f32[32,16,256]{2,1,0:T(8,128)} %slice.172) | copy-start | bytes 1572868
Sparse Core Ops, SparseCore 0:
  10.1 75.2 all-gather.3
  102.1 105.3 reduce-scatter.2
  211.2 60.3 all-gather.5
  284.8 125.7 reduce-scatter.4

commit v3 on v1

v3 whole, which is shorter than its diff:
```python
import jax
import jax.numpy as jnp
from jax import lax
from jax.sharding import Mesh, PartitionSpec as P

PANEL = 512


shift_scale = 0.01

PAR_PARTS = ("px", "py", "pc")


def reduce_in_steps(x, axes):
    for n, axis in enumerate(axes):
        if n:
            x = lax.optimization_barrier(x)
        x = lax.psum(x, axis)
    return x


def shards(jacobian):
    row_count, par_width = jacobian.shape
    sizes = [lax.axis_size(a) for a in PAR_PARTS]
    par_count = sizes[0] * sizes[1] * sizes[2]
    smp_count = lax.axis_size("smp")
    sample_total = row_count * smp_count
    param_total = par_width * par_count
    col_width = sample_total // par_count
    row_index = lax.axis_index("smp")
    col_index = (
        lax.axis_index("px") * (sizes[1] * sizes[2]) + lax.axis_index("py") * sizes[2] + lax.axis_index("pc")
    )
    f32 = jnp.float32

    gathered = lax.all_gather(jacobian, "smp", axis=0, tiled=True)
    widened = gathered.astype(f32)
    col_mean = jnp.sum(widened, axis=0) / sample_total
    centered = (widened - col_mean).astype(jnp.bfloat16)
    mine = lax.dynamic_slice_in_dim(centered, row_index * row_count, row_count, 0)
    head = centered[:PANEL]
    lhs = jnp.concatenate([mine, head], axis=0)
    contract = (((1,), (1,)), ((), ()))

    sq = centered.astype(f32)
    sumsq = jnp.sum(sq * sq)
    panel_all = lax.dot_general(lhs, head, contract, preferred_element_type=f32)
    panel_in = jnp.concatenate([panel_all, jnp.broadcast_to(sumsq, (8, PANEL))], axis=0)
    panel_red = reduce_in_steps(panel_in, ("pc", "py", "px")) / param_total

    big = lax.dot_general(lhs, centered, contract, preferred_element_type=f32)
    big, panel_red = lax.optimization_barrier((big, panel_red))
    big = lax.psum_scatter(big, PAR_PARTS, scatter_dimension=1, tiled=True)
    big = big / param_total
    tile = big[:row_count]
    band_t = big[row_count:]

    panel_g = panel_red[:row_count]
    square_g = panel_red[row_count : row_count + PANEL]
    trace_total = panel_red[row_count + PANEL, 0]
    shift_value = shift_scale * trace_total / sample_total

    eye = jnp.arange(PANEL, dtype=jnp.int32)
    global_rows = row_index * row_count + jnp.arange(row_count, dtype=jnp.int32)
    global_cols = col_index * col_width + jnp.arange(col_width, dtype=jnp.int32)
    square_s = square_g + jnp.where(eye[:, None] == eye[None, :], shift_value, 0.0)
    panel_s = panel_g + jnp.where(global_rows[:, None] == eye[None, :], shift_value, 0.0)
    band_s = band_t + jnp.where(eye[:, None] == global_cols[None, :], shift_value, 0.0)
    tile_s = tile + jnp.where(global_rows[:, None] == global_cols[None, :], shift_value, 0.0)

    factor = jnp.linalg.cholesky(square_s)
    panel_out = jax.scipy.linalg.solve_triangular(factor, panel_s.T, lower=True).T
    band_factor = jax.scipy.linalg.solve_triangular(factor, band_s, lower=True)
    schur_tile = tile_s - jnp.dot(panel_out, band_factor, precision=lax.Precision.HIGHEST)
    return (panel_out, schur_tile)


def solution(mesh):
    smp_count = mesh.shape["smp"]
    split = Mesh(mesh.devices.reshape(smp_count, 4, 4, -1), ("smp",) + PAR_PARTS)
    return jax.shard_map(
        shards,
        mesh=split,
        in_specs=(P("smp", PAR_PARTS),),
        out_specs=(P("smp", None), P("smp", PAR_PARTS)),
        check_vma=False,
    )
```

time: 451 us -> 459 us (1.018)
  waiting for transfers between devices: 227 us -> 262 us
  blocking collectives: 25.6 us -> 0 us
  local copies, waits for them, and re-layouts: 33.8 us -> 22.3 us
  matrix products: 15.9 us -> 21.2 us
  other arithmetic: 126 us -> 131 us
    psum x0 -> x3, waiting for transfers between devices: none -> 184 us  [reduce_in_steps(): x = lax.psum(x, axis)]
    unnamed x4 -> x5, waiting for transfers between devices: 114 us -> 0.75 us
    all_gather x1 -> x0, waiting for transfers between devices: 35.2 us -> none  [shards(): shared = lax.all_gather(reduced[o1:o4], 'par', axis=0, tiled=False)]
    all_gather x1 -> x0, blocking collectives: 25.6 us -> none  [shards(): lax.all_gather(reduced[o4:].reshape(band_piece, PANEL), 'smp', axis=0, ti...]
    unnamed x16 -> x11, local copies, waits for them, and re-layouts: 12 us -> 2.77 us
    slice x8 -> x2, local copies, waits for them, and re-layouts: 6.31 us -> 0.55 us  [the longest x1 0.51 us: shards(): trace_total = panel_red[row_count + PANEL, 0]]
    dot_general x3 -> x2, matrix products: 6.33 us -> 9.88 us  [the longest x1 9.27 us: shards(): big = lax.dot_general(lhs, centered, contract, preferred_element_type=f32)]
  transfers between devices with their start and end apart: 3 -> 5, of which waited for: 3 -> 4; matrix products, arithmetic and copies ran while one was open for 0% -> 35% of each run, Pallas kernels for 0% -> 0%
where the time goes in v3:
time: 459 us; the launch traced here: 454 us
  waiting for transfers between devices  262 us (57%)
  other arithmetic  131 us (29%)
  local copies, waits for them, and re-layouts  22.3 us (5%)
  matrix products  21.2 us (5%)
  between operations  17.6 us (4%)
    psum x3, waiting for transfers between devices, reduce_in_steps(): x = lax.psum(x, axis)  184 us
    another operation x14, other arithmetic, shards(): factor = jnp.linalg.cholesky(square_s)  78.7 us
    all_gather x1, waiting for transfers between devices, shards(): gathered = lax.all_gather(jacobian, 'smp', axis=0, tiled=True)  77.4 us
    another operation x3, other arithmetic, shards(): jax.scipy.linalg.solve_triangular(factor, panel_s.T, lower=True)  42 us
    another operation x20, local copies, waits for them, and re-layouts  14.9 us
    dot_general x1, matrix products, shards(): big = lax.dot_general(lhs, centered, contract, preferred_element_type=f32)  9.27 us
  transfers between devices with their start and end apart: 5, of which 4 were waited for; matrix products, arithmetic and copies ran while one was open for 35% of the time, Pallas kernels for 0%

profile of v3, /device:TPU:1, one launch (start us, length us, event | category | flops | bytes accessed | tf_op | source)
XLA Modules:
  0.0 454.0 jit_solution(1238047846994950883)
XLA Ops:
  7.2 0.7 all-gather.2.cloned.1.call-update
  7.9 77.4 %all-gather.2.cloned.1.call-done = bf16[4096,512]{1,0:T(8,128)(2,1)} async-done(((bf16[256,512]{1,0:T(8,128)(2,1)}), bf16[4096,512]{1,0:T(8,128)(2,1)}) %all-gather.2.cloned.1.call-update) | async-done | bytes 4194320 | tf_op jit(solution)/shard_map/all_gather | solution.py:36
  85.3 3.0 convert_reduce_fusion
  88.3 0.5 copy-done
  88.8 2.8 multiply_reduce_fusion
  91.6 0.6 fusion.2
  92.2 1.3 copy-done.1
  93.5 2.0 concatenate.29
  95.6 48.8 %all-reduce.6.cloned.1.call-done = f32[776,512]{0,1:T(8,128)} async-done(((f32[776,512]{0,1:T(8,128)}), f32[776,512]{0,1:T(8,128)}) %all-reduce.6.cloned.1.call-update) | async-done | bytes 1589264 | tf_op jit(solution)/shard_map/psum | solution.py:18
  144.5 72.2 %all-reduce.8.cloned.1.call-done = f32[776,512]{0,1:T(8,128)} async-done(((f32[776,512]{0,1:T(8,128)}), f32[776,512]{0,1:T(8,128)}) %all-reduce.8.cloned.1.call-update) | async-done | bytes 1589264 | tf_op jit(solution)/shard_map/psum | solution.py:18
  216.8 9.3 %fusion.3 = f32[768,4096]{1,0:T(8,128)} fusion(bf16[4096,512]{1,0:T(8,128)(2,1)} %copy-done.1, bf16[512,512]{1,0:T(8,128)(2,1)S(1)} %slice.182, bf16[256,512]{1,0:T(8,128)(2,1)S(1)} %constant_dynamic-slice_fusion.1), kind=kOutput, calls=%fused_computation.27 | convolution fusion | flops 3222798336 | bytes 17563648 | tf_op jit(solution)/shard_map/dot_general | solution.py:51
  226.1 62.7 %all-reduce.10.cloned.1.call-done = f32[776,512]{0,1:T(8,128)} async-done(((f32[776,512]{0,1:T(8,128)}), f32[776,512]{0,1:T(8,128)}) %all-reduce.10.cloned.1.call-update) | async-done | bytes 1589264 | tf_op jit(solution)/shard_map/psum | solution.py:18
  288.8 1.6 broadcast_multiply_fusion
  290.4 0.6 iota_multiply_fusion
  291.0 0.5 slice.167
  292.3 1.4 copy.4
  293.7 1.4 fusion.1
  295.1 11.7 %cholesky.103 = f32[128,128]{1,0:T(8,128)S(1)} custom-call(f32[128,128]{1,0:T(8,128)S(1)} %cholesky.263), custom_call_target="Cholesky" | custom-call | tf_op jit(solution)/shard_map/jit(cholesky)/cholesky | solution.py:71
  307.0 9.8 %custom-call.34 = f32[1,128,128]{1,2,0:T(8,128)S(1)} custom-call(f32[1,128,128]{2,1,0:T(8,128)S(1)} %get-tuple-element.37), custom_call_target="InvertDiagBlocksLowerTriangular" | custom-call | tf_op jit(solution)/shard_map/jit(cholesky)/cholesky | solution.py:71
  316.8 0.3 fusion.22
  317.2 0.3 convolution_subtract_fusion
  317.6 11.7 %cholesky.215 = f32[128,128]{1,0:T(8,128)S(1)} custom-call(f32[128,128]{1,0:T(8,128)S(1)} %cholesky.267), custom_call_target="Cholesky" | custom-call | tf_op jit(solution)/shard_map/jit(cholesky)/cholesky | solution.py:71
  329.5 10.0 %custom-call.35 = f32[1,128,128]{1,2,0:T(8,128)S(1)} custom-call(f32[1,128,128]{2,1,0:T(8,128)S(1)} %get-tuple-element.35), custom_call_target="InvertDiagBlocksLowerTriangular" | custom-call | tf_op jit(solution)/shard_map/jit(cholesky)/cholesky | solution.py:71
  339.6 0.3 convolution_dynamic-update-slice_fusion
  339.9 1.5 convolution_subtract_fusion.4
  341.4 11.7 %cholesky.236 = f32[128,128]{1,0:T(8,128)S(1)} custom-call(f32[128,128]{1,0:T(8,128)S(1)} %cholesky.272), custom_call_target="Cholesky" | custom-call | tf_op jit(solution)/shard_map/jit(cholesky)/cholesky | solution.py:71
  353.3 9.8 %custom-call.36 = f32[1,128,128]{1,2,0:T(8,128)S(1)} custom-call(f32[1,128,128]{2,1,0:T(8,128)S(1)} %get-tuple-element.33), custom_call_target="InvertDiagBlocksLowerTriangular" | custom-call | tf_op jit(solution)/shard_map/jit(cholesky)/cholesky | solution.py:71
  363.1 0.3 convolution_dynamic-update-slice_fusion.1
  363.4 1.3 convolution_subtract_fusion.9
  364.8 11.9 %cholesky.253 = f32[128,128]{1,0:T(8,128)S(1)} custom-call(f32[128,128]{1,0:T(8,128)S(1)} %convolution_subtract_fusion.9), custom_call_target="Cholesky" | custom-call | tf_op jit(solution)/shard_map/jit(cholesky)/cholesky | solution.py:71
  376.8 0.7 compare_reduce_fusion.2
  378.7 0.6 compare_reduce_fusion.1
  380.0 0.6 compare_reduce_fusion
  381.3 1.2 select_select_fusion
  382.5 14.9 %while.1 = (s32[]{:T(128)}, f32[512,512]{0,1:T(8,128)}, s32[4,2]{0,1:T(2,128)S(1)}, f32[4,128,128]{2,1,0:T(8,128)}, s32[]{:T(128)}) while((s32[]{:T(128)}, f32[512,512]{0,1:T(8,128)}, s32[4,2]{0,1:T(2,128)S(1)}, f32[4,128,128]{2,1,0:T(8,128)}, s32[]{:T(128)}) %tuple.32), condition=%wide.while_cond, body=%wide.while_body.sunk | while | flops 2 | bytes 393829 | solution.py:72
  382.6 0.6 fusion.76
  383.2 2.3 dynamic-slice.7
  385.6 0.6 bitcast_dynamic-update-slice_fusion.2
  386.3 0.6 fusion.76
  386.9 2.4 dynamic-slice.7
  389.4 0.6 bitcast_dynamic-update-slice_fusion.2
  390.1 0.6 fusion.76
  390.7 2.3 dynamic-slice.7
  393.1 0.6 bitcast_dynamic-update-slice_fusion.2
  393.8 0.6 fusion.76
  394.4 2.3 dynamic-slice.7
  396.8 0.6 bitcast_dynamic-update-slice_fusion.2
  397.5 40.2 %custom-call.37 = f32[4,128,128]{1,2,0:T(8,128)S(1)} custom-call(f32[4,128,128]{2,1,0:T(8,128)} %get-tuple-element.13), custom_call_target="InvertDiagBlocksLowerTriangular" | custom-call | tf_op jit(solution)/shard_map/jit(_solve_triangular)/triangular_solve | solution.py:72
  437.7 0.3 fusion.31
  438.1 1.1 convolution_subtract_fusion.5
  439.2 0.3 fusion.48
  439.5 0.4 convolution_subtract_fusion.3
  439.9 0.3 fusion.50
  440.3 0.5 convolution_subtract_fusion.2
  440.8 0.3 fusion.52
  441.1 1.0 copy.13
  442.1 1.0 broadcast_multiply_fusion.1
  443.5 0.3 convolution_subtract_fusion.7
  443.8 0.3 fusion.47
  444.1 0.4 convolution_subtract_fusion.6
  444.5 0.3 fusion.49
  444.8 0.5 convolution_subtract_fusion.8
  445.3 0.3 fusion.51
  445.5 1.7 convolution_subtract_fusion.1
  (55 shorter events, 2.4 us)
Async XLA Ops:
  7.2 78.2 %all-gather.2.cloned.1.call-start = ((), (), s32[]{:S(2)}) async-start(), calls=%async_computation.1 | async-start | bytes 4456448 | tf_op jit(solution)/shard_map/all_gather | solution.py:36
  7.9 136.5 %all-reduce.6.cloned.1.call-start = ((), (), s32[]{:S(2)}) async-start(), calls=%async_computation.2 | async-start | bytes 3670016 | tf_op jit(solution)/shard_map/psum | solution.py:18
  85.3 3.4 copy-start
  91.6 2.0 copy-start.1
  95.5 121.2 %all-reduce.8.cloned.1.call-start = ((), (), s32[]{:S(2)}) async-start(), calls=%async_computation.3 | async-start | bytes 3670016 | tf_op jit(solution)/shard_map/psum | solution.py:18
  144.4 144.3 %all-reduce.10.cloned.1.call-start = ((), (), s32[]{:S(2)}) async-start(), calls=%async_computation.4 | async-start | bytes 3670016 | tf_op jit(solution)/shard_map/psum | solution.py:18
  216.7 225.4 %reduce-scatter.2.cloned.1.call-start = ((), (), s32[]{:S(2)}) async-start(), calls=%async_computation.5 | async-start | bytes 12976128 | tf_op jit(solution)/shard_map/reduce_scatter | solution.py:53
  295.1 34.4 %copy-start.3 = (f32[512,512]{1,0:T(8,128)}, f32[512,512]{1,0:T(8,128)S(1)}, u32[]{:S(2)}) copy-start(f32[512,512]{1,0:T(8,128)S(1)} %fusion.1) | copy-start | bytes 3145732
  341.4 41.1 %copy-start.4 = (s32[4]{0:T(128)S(1)}, s32[4]{0:T(128)}, u32[]{:S(2)}) copy-start(s32[4]{0:T(128)} %iota_multiply_fusion) | copy-start | bytes 52
  397.5 42.1 %copy-start.2 = (f32[512,512]{0,1:T(8,128)S(1)}, f32[512,512]{0,1:T(8,128)}, u32[]{:S(2)}) copy-start(f32[512,512]{0,1:T(8,128)} %get-tuple-element.94) | copy-start | bytes 3145732
Sparse Core Ops, SparseCore 0:
  10.1 75.2 all-gather.1
  95.7 48.7 all-reduce.5
  146.9 69.7 all-reduce.7
  219.0 69.6 all-reduce.9
  294.0 126.3 reduce-scatter.1

commit v4 on v2

--- a/solution.py
+++ b/solution.py
@@ -1,12 +1,93 @@
+import functools
+
 import jax
 import jax.numpy as jnp
 from jax import lax
+from jax.experimental import pallas as pl
+from jax.experimental.pallas import tpu as pltpu
 from jax.sharding import PartitionSpec as P
 
 PANEL = 512
 
 
 shift_scale = 0.01
+
+
+HI = lax.Precision.HIGHEST
+NT = (((1,), (1,)), ((), ()))
+
+
+def _chol_kernel(a_ref, l_ref, w_ref, s_ref, blk_a, blk_b, blk_lt, blk_w, *, n, b):
+    nb = n // b
+    f32 = jnp.float32
+    s_ref[...] = a_ref[...]
+    l_ref[...] = jnp.zeros((n, n), f32)
+    w_ref[...] = jnp.zeros((n, n), f32)
+    rows = lax.broadcasted_iota(jnp.int32, (b, b), 0)
+    cols = lax.broadcasted_iota(jnp.int32, (b, b), 1)
+    lane = lax.broadcasted_iota(jnp.int32, (1, b), 1)
+    for k in range(nb):
+        ks = pl.ds(k * b, b)
+        blk_a[...] = s_ref[ks, ks]
+        blk_b[...] = jnp.where(rows == cols, 1.0, 0.0).astype(f32)
+
+        def step(j, carry):
+            row = blk_a[pl.ds(j, 1), :]
+            d = jnp.sum(jnp.where(lane == j, row, 0.0), axis=1, keepdims=True)
+            s = jnp.sqrt(d)
+            v_row = jnp.where(lane >= j, row / s, 0.0)
+            v_col = jnp.transpose(jnp.broadcast_to(v_row, (8, b)))[:, 0:1]
+            blk_a[...] = blk_a[...] - v_col * v_row
+            x = blk_b[pl.ds(j, 1), :] / s
+            blk_b[...] = blk_b[...] - v_col * x
+            blk_lt[pl.ds(j, 1), :] = v_row
+            blk_w[pl.ds(j, 1), :] = x
+            return carry
+
+        lax.fori_loop(0, b, step, 0)
+        w_kk = blk_w[...]
+        l_ref[ks, ks] = jnp.transpose(blk_lt[...])
+        w_ref[ks, ks] = w_kk
+        if k < nb - 1:
+            rest = pl.ds((k + 1) * b, n - (k + 1) * b)
+            below = lax.dot_general(s_ref[rest, ks], w_kk, NT, precision=HI, preferred_element_type=f32)
+            l_ref[rest, ks] = below
+            s_ref[rest, rest] = s_ref[rest, rest] - lax.dot_general(
+                below, below, NT, precision=HI, preferred_element_type=f32
+            )
+    for i in range(1, nb):
+        w_ii = w_ref[pl.ds(i * b, b), pl.ds(i * b, b)]
+        for j in range(i):
+            acc = jnp.zeros((b, b), f32)
+            for m in range(j, i):
+                acc = acc + jnp.dot(
+                    l_ref[pl.ds(i * b, b), pl.ds(m * b, b)],
+                    w_ref[pl.ds(m * b, b), pl.ds(j * b, b)],
+                    precision=HI,
+                    preferred_element_type=f32,
+                )
+            w_ref[pl.ds(i * b, b), pl.ds(j * b, b)] = -jnp.dot(
+                w_ii, acc, precision=HI, preferred_element_type=f32
+            )
+
+
+def chol_and_inverse(a, block=128):
+    n = a.shape[0]
+    f32 = jnp.float32
+    return pl.pallas_call(
+        functools.partial(_chol_kernel, n=n, b=block),
+        out_shape=(jax.ShapeDtypeStruct((n, n), f32), jax.ShapeDtypeStruct((n, n), f32)),
+        in_specs=[pl.BlockSpec(memory_space=pltpu.VMEM)],
+        out_specs=(pl.BlockSpec(memory_space=pltpu.VMEM), pl.BlockSpec(memory_space=pltpu.VMEM)),
+        scratch_shapes=[
+            pltpu.VMEM((n, n), f32),
+            pltpu.VMEM((block, block), f32),
+            pltpu.VMEM((block, block), f32),
+            pltpu.VMEM((block, block), f32),
+            pltpu.VMEM((block, block), f32),
+        ],
+        cost_estimate=pl.CostEstimate(flops=2 * n * n * n, bytes_accessed=3 * n * n * 4, transcendentals=n),
+    )(a)
 
 
 def shards(jacobian):
@@ -80,9 +161,9 @@
     band_s = band_mine + jnp.where(global_cols[:, None] == eye[None, :], shift_value, 0.0)
     tile_s = tile + jnp.where(global_rows[:, None] == global_cols[None, :], shift_value, 0.0)
 
-    factor = jnp.linalg.cholesky(square_s)
-    panel_out = jax.scipy.linalg.solve_triangular(factor, panel_s.T, lower=True).T
-    band_factor = jax.scipy.linalg.solve_triangular(factor, band_s.T, lower=True)
+    _, inverse = chol_and_inverse(square_s)
+    panel_out = lax.dot_general(panel_s, inverse, NT, precision=HI, preferred_element_type=f32)
+    band_factor = lax.dot_general(inverse, band_s, NT, precision=HI, preferred_element_type=f32)
     schur_tile = tile_s - jnp.dot(panel_out, band_factor, precision=lax.Precision.HIGHEST)
     return (panel_out, schur_tile)
 

time: 444 us -> 447 us (level); the launches traced: 437 us -> 446 us
  Pallas kernels: 0 us -> 143 us
  other arithmetic: 139 us -> 21.5 us
  local copies, waits for them, and re-layouts: 41.5 us -> 31.4 us
    pallas_call x0 -> x1, Pallas kernels: none -> 143 us  [chol_and_inverse(): pl.pallas_call(functools.partial(_chol_kernel, n=n, b=block), out_shape=(...]
    another operation x17 -> x0, other arithmetic: 118 us -> none  [the longest x14 78.7 us: shards(): factor = jnp.linalg.cholesky(square_s)]
    another operation x34 -> x0, local copies, waits for them, and re-layouts: 8.66 us -> none
    another operation x20 -> x0, matrix products: 7.06 us -> none  [the longest x7 2.43 us: shards(): jax.scipy.linalg.solve_triangular(factor, panel_s.T, lower=True)]
  transfers between devices with their start and end apart: 4 -> 4, of which waited for: 3 -> 3; matrix products, arithmetic and copies ran while one was open for 37% -> 8% of each run, Pallas kernels for 0% -> 32%
where the time goes in v4:
time: 447 us; the launch traced here: 446 us
  waiting for transfers between devices  218 us (49%)
  Pallas kernels  143 us (32%)
  local copies, waits for them, and re-layouts  31.4 us (7%)
  other arithmetic  21.5 us (5%)
  matrix products  17.3 us (4%)
  between operations  14.6 us (3%)
    pallas_call x1, Pallas kernels, chol_and_inverse(): pl.pallas_call(functools.partial(_chol_kernel, n=n, b=block), out_shape=(...  143 us
    reduce_scatter x1, waiting for transfers between devices, shards(): lax.psum_scatter(panel_parts.reshape(par_count * chunk, width), 'par', sc...  105 us
    all_gather x1, waiting for transfers between devices, shards(): gathered = lax.all_gather(jacobian, 'smp', axis=0, tiled=True)  77.4 us
    all_gather x1, waiting for transfers between devices, shards(): shared = lax.all_gather(reduced, 'par', axis=0, tiled=False)  34.7 us
    reshape x1, local copies, waits for them, and re-layouts, shards(): main_parts.reshape(par_count * main_chunk, width)  12.6 us
    concatenate x1, other arithmetic, shards(): jnp.concatenate([main.reshape(par_count, col_width, width), band.reshape(...  10.4 us
    reshape x1, local copies, waits for them, and re-layouts, shards(): band.reshape(par_count, col_width * PANEL // width, width)  9.36 us
  transfers between devices with their start and end apart: 4, of which 3 were waited for; matrix products, arithmetic and copies ran while one was open for 8% of the time, Pallas kernels for 32%

profile of v4, /device:TPU:1, one launch (start us, length us, event | category | flops | bytes accessed | tf_op | source)
XLA Modules:
  0.0 445.9 jit_solution(2289494533051944216)
XLA Ops:
  7.2 0.0 all-gather.4.cloned.1.call-start
  7.2 0.7 all-gather.4.cloned.1.call-update
  7.9 0.0 reduce-scatter.3.cloned.1.call-start
  7.9 77.4 %all-gather.4.cloned.1.call-done = bf16[4096,512]{1,0:T(8,128)(2,1)} async-done(((bf16[256,512]{1,0:T(8,128)(2,1)}), bf16[4096,512]{1,0:T(8,128)(2,1)}) %all-gather.4.cloned.1.call-update) | async-done | bytes 4194320 | tf_op jit(solution)/shard_map/all_gather | solution.py:105
  85.3 0.0 copy-start.2
  85.3 3.0 convert_reduce_fusion
  88.3 0.5 copy-done.2
  88.8 2.8 multiply_reduce_fusion
  91.6 0.0 copy-start
  91.6 1.9 copy-done
  93.5 0.5 fusion.1
  94.0 0.2 reshape.51
  94.1 3.5 fusion.8
  97.7 0.0 copy-start.1
  97.7 2.0 copy-done.1
  99.7 0.6 broadcast_in_dim.44
  100.3 0.1 pad.2.clone
  100.4 1.5 maximum_maximum_fusion
  101.9 0.0 reduce-scatter.3.cloned.1.call-update
  101.9 0.0 all-gather.6.cloned.1.call-start
  102.0 105.4 %reduce-scatter.3.cloned.1.call-done = f32[56,256]{1,0:T(8,128)} async-done(((f32[1792,256]{1,0:T(8,128)}), f32[56,256]{1,0:T(8,128)}) %reduce-scatter.3.cloned.1.call-update) | async-done | bytes 57360 | tf_op jit(solution)/shard_map/reduce_scatter | solution.py:129
  207.4 1.4 broadcast_multiply_fusion.1
  208.8 0.0 all-gather.6.cloned.1.call-update
  208.8 0.2 reduce-scatter.5.cloned.1.call-start
  209.1 7.9 %fusion.3 = f32[4096,512]{1,0:T(8,128)} fusion(bf16[4096,512]{1,0:T(8,128)(2,1)} %copy-done), kind=kOutput, calls=%fused_computation.13 | convolution fusion | flops 2147483648 | bytes 13107200 | tf_op jit(solution)/shard_map/dot_general | solution.py:115
  217.0 9.4 %reshape.49 = f32[32,256,256]{2,1,0:T(8,128)} reshape(f32[4096,512]{1,0:T(8,128)} %fusion.3) | data formatting | bytes 16777216 | tf_op jit(solution)/shard_map/reshape | solution.py:137
  226.3 10.4 %pad_maximum_fusion = f32[32,384,256]{2,1,0:T(8,128)} fusion(f32[32,256,256]{2,1,0:T(8,128)} %reshape.49, f32[32,128,256]{2,1,0:T(8,128)} %bitcast.24), kind=kLoop, calls=%fused_computation | loop fusion | flops 3145728 | bytes 25165824 | tf_op jit(solution)/shard_map/concatenate | solution.py:134
  236.8 34.7 %all-gather.6.cloned.1.call-done = f32[1792,256]{1,0:T(8,128)} async-done(((f32[56,256]{1,0:T(8,128)}), f32[1792,256]{1,0:T(8,128)}) %all-gather.6.cloned.1.call-update) | async-done | bytes 1835024 | tf_op jit(solution)/shard_map/all_gather | solution.py:132
  271.5 12.6 %copy.6 = f32[12288,256]{0,1:T(8,128)} copy(f32[12288,256]{1,0:T(8,128)} %bitcast.23) | data formatting | bytes 25165824 | tf_op jit(solution)/shard_map/reshape | solution.py:144
  284.0 0.0 reduce-scatter.5.cloned.1.call-update
  284.1 1.2 slice.24
  285.3 1.1 slice.23
  286.4 1.3 slice.25
  287.7 0.3 reshape.54
  288.6 1.1 select_add_fusion.a_ref
  289.7 142.6 %shard_map.30 = (f32[512,512]{1,0:T(8,128)}, f32[512,512]{1,0:T(8,128)}) custom-call(f32[512,512]{1,0:T(8,128)} %select_add_fusion.a_ref), custom_call_target="tpu_custom_call" | custom-call | flops 268435456 | bytes 3145728 | tf_op jit(solution)/shard_map/pallas_call | solution.py:77
  432.4 0.0 copy-start.3
  432.4 0.1 bitcast_add_fusion
  432.4 3.2 fusion.17
  435.6 0.0 copy-start.4
  435.6 0.0 reduce-scatter.5.cloned.1.call-done
  435.6 1.2 broadcast_multiply_fusion
  436.9 0.1 copy.5
  437.0 0.1 reshape.56
  437.1 0.0 copy-done.3
  437.1 1.1 fusion.5
  438.2 1.2 convolution_subtract_fusion
  439.4 0.0 copy-done.4
  (5 shorter events, 0.1 us)
Async XLA Ops:
  7.2 78.2 %all-gather.4.cloned.1.call-start = ((), (), s32[]{:S(2)}) async-start(), calls=%async_computation.2 | async-start | bytes 4456448 | tf_op jit(solution)/shard_map/all_gather | solution.py:105
  7.9 199.5 %reduce-scatter.3.cloned.1.call-start = ((), (), s32[]{:S(2)}) async-start(), calls=%async_computation.3 | async-start | bytes 1892352 | tf_op jit(solution)/shard_map/reduce_scatter | solution.py:129
  85.3 3.4 copy-start.2
  91.6 1.9 copy-start
  97.7 2.0 copy-start.1
  101.9 169.5 %all-gather.6.cloned.1.call-start = ((), (), s32[]{:S(2)}) async-start(), calls=%async_computation.5 | async-start | bytes 1892352 | tf_op jit(solution)/shard_map/all_gather | solution.py:132
  208.8 226.8 %reduce-scatter.5.cloned.1.call-start = ((), (), s32[]{:S(2)}) async-start(), calls=%async_computation.4 | async-start | bytes 12976128 | tf_op jit(solution)/shard_map/reduce_scatter | solution.py:143
  432.4 4.7 %copy-start.3 = (f32[512,512]{1,0:T(8,128)S(1)}, f32[512,512]{1,0:T(8,128)}, u32[]{:S(2)}) copy-start(f32[512,512]{1,0:T(8,128)} %get-tuple-element.6) | copy-start | bytes 3145732
  435.6 3.8 copy-start.4
Sparse Core Ops, SparseCore 0:
  10.1 75.2 all-gather.3
  102.0 105.3 reduce-scatter.2
  211.1 60.3 all-gather.5
  284.2 125.6 reduce-scatter.4

commit v5 on v4

--- a/solution.py
+++ b/solution.py
@@ -110,16 +110,15 @@
     head = centered[:PANEL]
     contract = (((1,), (1,)), ((), ()))
 
-    main = lax.dot_general(centered, mine, contract, preferred_element_type=f32)
+    main_t = lax.dot_general(mine, head, contract, preferred_element_type=f32)
     square = lax.dot_general(head, head, contract, preferred_element_type=f32)
-    band = lax.dot_general(centered, head, contract, preferred_element_type=f32)
     sq = centered.astype(f32)
     sumsq = jnp.sum(sq * sq)
 
     width = row_count
     panel_parts = jnp.concatenate(
         [
-            main[:PANEL].reshape(par_count, panel_piece, width),
+            main_t.T.reshape(par_count, panel_piece, width),
             square.reshape(par_count, panel_piece * PANEL // width, width),
             jnp.broadcast_to(sumsq, (par_count, 8, width)),
         ],
@@ -131,20 +130,12 @@
     ) / param_total
     shared = lax.all_gather(reduced, "par", axis=0, tiled=False)
 
-    main_parts = jnp.concatenate(
-        [
-            main.reshape(par_count, col_width, width),
-            band.reshape(par_count, col_width * PANEL // width, width),
-        ],
-        axis=1,
-    )
-    main_parts, shared = lax.optimization_barrier((main_parts, shared))
-    main_chunk = main_parts.shape[1]
-    reduced_main = lax.psum_scatter(
-        main_parts.reshape(par_count * main_chunk, width), "par", scatter_dimension=0, tiled=True
-    ) / param_total
-    tile = reduced_main[:col_width].T
-    band_mine = reduced_main[col_width:].reshape(col_width, PANEL)
+    lhs = jnp.concatenate([mine, head], axis=0)
+    big = lax.dot_general(lhs, centered, contract, preferred_element_type=f32)
+    big, shared = lax.optimization_barrier((big, shared))
+    big = lax.psum_scatter(big, "par", scatter_dimension=1, tiled=True) / param_total
+    tile = big[:row_count]
+    band_t = big[row_count:]
 
     o2 = panel_piece
     o3 = o2 + panel_piece * PANEL // width
@@ -158,12 +149,12 @@
     global_cols = col_index * col_width + jnp.arange(col_width, dtype=jnp.int32)
     square_s = square_g + jnp.where(eye[:, None] == eye[None, :], shift_value, 0.0)
     panel_s = panel_t.T + jnp.where(global_rows[:, None] == eye[None, :], shift_value, 0.0)
-    band_s = band_mine + jnp.where(global_cols[:, None] == eye[None, :], shift_value, 0.0)
+    band_s = band_t + jnp.where(eye[:, None] == global_cols[None, :], shift_value, 0.0)
     tile_s = tile + jnp.where(global_rows[:, None] == global_cols[None, :], shift_value, 0.0)
 
     _, inverse = chol_and_inverse(square_s)
     panel_out = lax.dot_general(panel_s, inverse, NT, precision=HI, preferred_element_type=f32)
-    band_factor = lax.dot_general(inverse, band_s, NT, precision=HI, preferred_element_type=f32)
+    band_factor = jnp.dot(inverse, band_s, precision=HI, preferred_element_type=f32)
     schur_tile = tile_s - jnp.dot(panel_out, band_factor, precision=lax.Precision.HIGHEST)
     return (panel_out, schur_tile)
 

time: 447 us -> 429 us (0.960)
  local copies, waits for them, and re-layouts: 31.4 us -> 7.82 us
  waiting for transfers between devices: 218 us -> 236 us
  other arithmetic: 21.5 us -> 11 us
    reshape x3 -> x0, local copies, waits for them, and re-layouts: 22 us -> none  [the longest x1 12.6 us: shards(): main_parts.reshape(par_count * main_chunk, width)]
    all_gather x1, waiting for transfers between devices: 34.7 us -> 52.4 us  [shards(): shared = lax.all_gather(reduced, 'par', axis=0, tiled=False)]
    concatenate x2 -> x1, other arithmetic: 11.9 us -> 1.47 us  [shards(): jnp.concatenate([main_t.T.reshape(par_count, panel_piece, width), square....]
  transfers between devices with their start and end apart: 4 -> 4, of which waited for: 3 -> 3; matrix products, arithmetic and copies ran while one was open for 8% -> 4% of each run, Pallas kernels for 32% -> 33%
where the time goes in v5:
time: 429 us
  waiting for transfers between devices  236 us (55%)
  Pallas kernels  143 us (33%)
  matrix products  16.1 us (4%)
  between operations  14.5 us (3%)
  other arithmetic  11 us (3%)
  local copies, waits for them, and re-layouts  7.82 us (2%)
    pallas_call x1, Pallas kernels, chol_and_inverse(): pl.pallas_call(functools.partial(_chol_kernel, n=n, b=block), out_shape=(...  143 us
    reduce_scatter x1, waiting for transfers between devices, shards(): lax.psum_scatter(panel_parts.reshape(par_count * chunk, width), 'par', sc...  106 us
    all_gather x1, waiting for transfers between devices, shards(): gathered = lax.all_gather(jacobian, 'smp', axis=0, tiled=True)  77.4 us
    all_gather x1, waiting for transfers between devices, shards(): shared = lax.all_gather(reduced, 'par', axis=0, tiled=False)  52.4 us
    dot_general x1, matrix products, shards(): big = lax.dot_general(lhs, centered, contract, preferred_element_type=f32)  8.83 us
  transfers between devices with their start and end apart: 4, of which 3 were waited for; matrix products, arithmetic and copies ran while one was open for 4% of the time, Pallas kernels for 33%

profile of v5, /device:TPU:1, one launch (start us, length us, event | category | flops | bytes accessed | tf_op | source)
XLA Modules:
  0.0 428.5 jit_solution(11888937416438935903)
XLA Ops:
  7.2 0.0 all-gather.4.cloned.1.call-start
  7.2 0.7 all-gather.4.cloned.1.call-update
  7.9 0.0 reduce-scatter.3.cloned.1.call-start
  7.9 77.4 %all-gather.4.cloned.1.call-done = bf16[4096,512]{1,0:T(8,128)(2,1)} async-done(((bf16[256,512]{1,0:T(8,128)(2,1)}), bf16[4096,512]{1,0:T(8,128)(2,1)}) %all-gather.4.cloned.1.call-update) | async-done | bytes 4194320 | tf_op jit(solution)/shard_map/all_gather | solution.py:105
  85.3 0.0 copy-start
  85.3 3.0 convert_reduce_fusion
  88.3 0.5 copy-done
  88.8 2.8 multiply_reduce_fusion
  91.6 0.0 copy-start.1
  91.6 0.5 fusion.12
  92.0 1.5 copy-done.1
  93.5 0.2 reshape.33
  93.7 1.4 fusion.14
  95.1 0.6 broadcast_in_dim.44
  95.7 0.1 pad.2.clone
  95.8 1.5 maximum_maximum_fusion
  97.3 0.0 reduce-scatter.3.cloned.1.call-update
  97.3 0.0 all-gather.6.cloned.1.call-start
  97.4 105.5 %reduce-scatter.3.cloned.1.call-done = f32[56,256]{1,0:T(8,128)} async-done(((f32[1792,256]{1,0:T(8,128)}), f32[56,256]{1,0:T(8,128)}) %reduce-scatter.3.cloned.1.call-update) | async-done | bytes 57360 | tf_op jit(solution)/shard_map/reduce_scatter | solution.py:128
  202.9 1.4 broadcast_multiply_fusion.1
  204.3 0.0 all-gather.6.cloned.1.call-update
  204.3 0.2 reduce-scatter.5.cloned.1.call-start
  204.6 1.1 slice.24
  205.6 8.8 %fusion.1 = f32[768,4096]{1,0:T(8,128)} fusion(bf16[4096,512]{1,0:T(8,128)(2,1)} %copy-done.1, bf16[512,512]{1,0:T(8,128)(2,1)S(1)} %slice.24, bf16[256,512]{1,0:T(8,128)(2,1)S(1)} %constant_dynamic-slice_fusion), kind=kOutput, calls=%fused_computation.8 | convolution fusion | flops 3222798336 | bytes 17563648 | tf_op jit(solution)/shard_map/dot_general | solution.py:134
  214.5 52.4 %all-gather.6.cloned.1.call-done = f32[1792,256]{1,0:T(8,128)} async-done(((f32[56,256]{1,0:T(8,128)}), f32[1792,256]{1,0:T(8,128)}) %all-gather.6.cloned.1.call-update) | async-done | bytes 1835024 | tf_op jit(solution)/shard_map/all_gather | solution.py:131
  266.9 0.0 reduce-scatter.5.cloned.1.call-update
  267.0 1.1 slice.19
  268.1 1.2 slice.20
  269.2 1.3 slice.21
  270.6 0.3 reshape.36
  271.5 1.1 select_add_fusion.a_ref
  272.6 142.6 %shard_map.30 = (f32[512,512]{1,0:T(8,128)}, f32[512,512]{1,0:T(8,128)}) custom-call(f32[512,512]{1,0:T(8,128)} %select_add_fusion.a_ref), custom_call_target="tpu_custom_call" | custom-call | flops 268435456 | bytes 3145728 | tf_op jit(solution)/shard_map/pallas_call | solution.py:77
  415.2 0.0 copy-start.2
  415.2 0.1 bitcast_add_fusion
  415.3 3.2 fusion.17
  418.5 0.0 copy-start.3
  418.5 0.0 reduce-scatter.5.cloned.1.call-done
  418.5 1.2 broadcast_multiply_fusion
  419.7 0.0 copy-done.2
  419.7 1.0 fusion.5
  420.7 1.2 convolution_subtract_fusion
  422.0 0.0 copy-done.3
  (4 shorter events, 0.0 us)
Async XLA Ops:
  7.2 78.2 %all-gather.4.cloned.1.call-start = ((), (), s32[]{:S(2)}) async-start(), calls=%async_computation.2 | async-start | bytes 4456448 | tf_op jit(solution)/shard_map/all_gather | solution.py:105
  7.9 195.0 %reduce-scatter.3.cloned.1.call-start = ((), (), s32[]{:S(2)}) async-start(), calls=%async_computation.3 | async-start | bytes 1892352 | tf_op jit(solution)/shard_map/reduce_scatter | solution.py:128
  85.3 3.4 copy-start
  91.6 1.9 copy-start.1
  97.3 169.6 %all-gather.6.cloned.1.call-start = ((), (), s32[]{:S(2)}) async-start(), calls=%async_computation.5 | async-start | bytes 1892352 | tf_op jit(solution)/shard_map/all_gather | solution.py:131
  204.3 214.2 %reduce-scatter.5.cloned.1.call-start = ((), (), s32[]{:S(2)}) async-start(), calls=%async_computation.4 | async-start | bytes 12976128 | tf_op jit(solution)/shard_map/reduce_scatter | solution.py:136
  415.2 4.5 %copy-start.2 = (f32[512,512]{1,0:T(8,128)S(1)}, f32[512,512]{1,0:T(8,128)}, u32[]{:S(2)}) copy-start(f32[512,512]{1,0:T(8,128)} %get-tuple-element.6) | copy-start | bytes 3145732
  418.5 3.5 copy-start.3
Sparse Core Ops, SparseCore 0:
  10.1 75.2 all-gather.3
  97.4 105.3 reduce-scatter.2
  206.6 60.3 all-gather.5
  271.5 125.7 reduce-scatter.4

commit v6 on v5

--- a/solution.py
+++ b/solution.py
@@ -90,6 +90,27 @@
     )(a)
 
 
+def reduce_by_halving(x, axis, count):
+    index = lax.axis_index(axis)
+    masks = [1 << k for k in range(count.bit_length() - 1)]
+    masks = masks[:2] + masks[3:4] + masks[2:3] + masks[4:]
+    size = x.shape[0]
+    for mask in masks:
+        half = size // 2
+        bit = (index // mask) % 2
+        keep = lax.dynamic_slice_in_dim(x, bit * half, half, 0)
+        send = lax.dynamic_slice_in_dim(x, (1 - bit) * half, half, 0)
+        x = keep + lax.ppermute(send, axis, [(i, i ^ mask) for i in range(count)])
+        size = half
+    for mask in reversed(masks):
+        bit = (index // mask) % 2
+        other = lax.ppermute(x, axis, [(i, i ^ mask) for i in range(count)])
+        low = jnp.where(bit == 0, x, other)
+        high = jnp.where(bit == 0, other, x)
+        x = jnp.concatenate([low, high], axis=0)
+    return x
+
+
 def shards(jacobian):
     row_count, par_width = jacobian.shape
     par_count = lax.axis_size("par")
@@ -115,20 +136,9 @@
     sq = centered.astype(f32)
     sumsq = jnp.sum(sq * sq)
 
-    width = row_count
-    panel_parts = jnp.concatenate(
-        [
-            main_t.T.reshape(par_count, panel_piece, width),
-            square.reshape(par_count, panel_piece * PANEL // width, width),
-            jnp.broadcast_to(sumsq, (par_count, 8, width)),
-        ],
-        axis=1,
-    )
-    chunk = panel_parts.shape[1]
-    reduced = lax.psum_scatter(
-        panel_parts.reshape(par_count * chunk, width), "par", scatter_dimension=0, tiled=True
-    ) / param_total
-    shared = lax.all_gather(reduced, "par", axis=0, tiled=False)
+    fill = jnp.broadcast_to(sumsq, (row_count, PANEL))
+    panel_in = jnp.concatenate([main_t, square, fill], axis=0)
+    shared = reduce_by_halving(panel_in, "par", par_count) / param_total
 
     lhs = jnp.concatenate([mine, head], axis=0)
     big = lax.dot_general(lhs, centered, contract, preferred_element_type=f32)
@@ -137,18 +147,16 @@
     tile = big[:row_count]
     band_t = big[row_count:]
 
-    o2 = panel_piece
-    o3 = o2 + panel_piece * PANEL // width
-    panel_t = shared[:, :o2].reshape(PANEL, width)
-    square_g = shared[:, o2:o3].reshape(PANEL, PANEL)
-    trace_total = shared[0, o3, 0]
+    panel_g = shared[:row_count]
+    square_g = shared[row_count : row_count + PANEL]
+    trace_total = shared[row_count + PANEL, 0]
     shift_value = shift_scale * trace_total / sample_total
 
     eye = jnp.arange(PANEL, dtype=jnp.int32)
     global_rows = row_index * row_count + jnp.arange(row_count, dtype=jnp.int32)
     global_cols = col_index * col_width + jnp.arange(col_width, dtype=jnp.int32)
     square_s = square_g + jnp.where(eye[:, None] == eye[None, :], shift_value, 0.0)
-    panel_s = panel_t.T + jnp.where(global_rows[:, None] == eye[None, :], shift_value, 0.0)
+    panel_s = panel_g + jnp.where(global_rows[:, None] == eye[None, :], shift_value, 0.0)
     band_s = band_t + jnp.where(eye[:, None] == global_cols[None, :], shift_value, 0.0)
     tile_s = tile + jnp.where(global_rows[:, None] == global_cols[None, :], shift_value, 0.0)
 

time: 429 us -> 358 us (0.83)
  waiting for transfers between devices: 236 us -> 117 us
  starting transfers between devices: 0.34 us -> 53.5 us
  local copies, waits for them, and re-layouts: 7.82 us -> 3.07 us
    reduce_scatter x1 -> x0, waiting for transfers between devices: 106 us -> none  [shards(): lax.psum_scatter(panel_parts.reshape(par_count * chunk, width), 'par', sc...]
    ppermute x0 -> x10, starting transfers between devices: none -> 53.4 us  [the longest x5 26.9 us: reduce_by_halving(): x = keep + lax.ppermute(send, axis, [(i, i ^ mask) for i in range(count)])]
    all_gather x1 -> x0, waiting for transfers between devices: 52.4 us -> none  [shards(): shared = lax.all_gather(reduced, 'par', axis=0, tiled=False)]
    ppermute x0 -> x10, waiting for transfers between devices: none -> 39.3 us  [the longest x5 24 us: reduce_by_halving(): x = keep + lax.ppermute(send, axis, [(i, i ^ mask) for i in range(count)])]
  transfers between devices with their start and end apart: 4 -> 12, of which waited for: 3 -> 10; matrix products, arithmetic and copies ran while one was open for 4% -> 4% of each run, Pallas kernels for 33% -> 40%
where the time goes in v6:
time: 358 us
  Pallas kernels  143 us (40%)
  waiting for transfers between devices  117 us (33%)
  starting transfers between devices  53.5 us (15%)
  matrix products  15.4 us (4%)
  between operations  15.2 us (4%)
  other arithmetic  10.6 us (3%)
    pallas_call x1, Pallas kernels, chol_and_inverse(): pl.pallas_call(functools.partial(_chol_kernel, n=n, b=block), out_shape=(...  143 us
    all_gather x1, waiting for transfers between devices, shards(): gathered = lax.all_gather(jacobian, 'smp', axis=0, tiled=True)  77.4 us
    ppermute x5, starting transfers between devices, reduce_by_halving(): x = keep + lax.ppermute(send, axis, [(i, i ^ mask) for i in range(count)])  26.9 us
    ppermute x5, starting transfers between devices, reduce_by_halving(): other = lax.ppermute(x, axis, [(i, i ^ mask) for i in range(count)])  26.5 us
    ppermute x5, waiting for transfers between devices, reduce_by_halving(): x = keep + lax.ppermute(send, axis, [(i, i ^ mask) for i in range(count)])  24 us
    ppermute x5, waiting for transfers between devices, reduce_by_halving(): other = lax.ppermute(x, axis, [(i, i ^ mask) for i in range(count)])  15.3 us
    dot_general x1, matrix products, shards(): big = lax.dot_general(lhs, centered, contract, preferred_element_type=f32)  8.83 us
  transfers between devices with their start and end apart: 12, of which 10 were waited for; matrix products, arithmetic and copies ran while one was open for 4% of the time, Pallas kernels for 40%

profile of v6, /device:TPU:1, one launch (start us, length us, event | category | flops | bytes accessed | tf_op | source)
XLA Modules:
  0.0 357.8 jit_solution(5100116967935026091)
XLA Ops:
  7.2 0.0 all-gather.2.cloned.1.call-start
  7.2 0.7 all-gather.2.cloned.1.call-update
  7.9 0.0 reduce-scatter.2.cloned.1.call-start
  8.0 77.4 %all-gather.2.cloned.1.call-done = bf16[4096,512]{1,0:T(8,128)(2,1)} async-done(((bf16[256,512]{1,0:T(8,128)(2,1)}), bf16[4096,512]{1,0:T(8,128)(2,1)}) %all-gather.2.cloned.1.call-update) | async-done | bytes 4194320 | tf_op jit(solution)/shard_map/all_gather | solution.py:126
  85.3 0.0 copy-start
  85.3 3.0 convert_reduce_fusion
  88.3 0.5 copy-done
  88.8 2.8 multiply_reduce_fusion
  91.6 0.0 copy-start.1
  91.6 0.5 fusion.20
  92.1 0.3 fusion.22
  92.4 0.7 broadcast_in_dim.44
  93.1 0.2 maximum_maximum_fusion
  93.3 0.1 constant_dynamic-slice_fusion.4
  93.4 0.1 copy-done.1
  93.5 11.4 %collective-permute-start = (f32[512,512]{1,0:T(8,128)S(1)}, f32[512,512]{1,0:T(8,128)}, u32[]{:S(2)}, u32[]{:S(2)}) collective-permute-start(f32[512,512]{1,0:T(8,128)S(1)} %constant_dynamic-slice_fusion.4), channel_id=1, source_target_pairs={{0,1},{1,0},{2,3},{3,2},{4,5},{5,4},{6,7},{7,6},{8,9},{9,8},{10,11... | collective-permute-start | bytes 3145736 | tf_op jit(solution)/shard_map/ppermute | solution.py:103
  105.0 2.4 collective-permute-done
  107.3 1.4 dynamic-slice_add_fusion
  108.8 3.1 collective-permute-start.1
  112.0 11.9 %collective-permute-done.1 = f32[256,512]{1,0:T(8,128)S(1)} collective-permute-done((f32[256,512]{1,0:T(8,128)S(1)}, f32[256,512]{1,0:T(8,128)S(1)}, u32[]{:S(2)}, u32[]{:S(2)}) %collective-permute-start.1) | collective-permute-done | bytes 524320 | tf_op jit(solution)/shard_map/ppermute | solution.py:103
  123.9 0.1 dynamic-slice_add_fusion.1
  124.0 3.1 collective-permute-start.2
  127.1 5.4 %collective-permute-done.2 = f32[128,512]{1,0:T(8,128)S(1)} collective-permute-done((f32[128,512]{1,0:T(8,128)S(1)}, f32[128,512]{1,0:T(8,128)S(1)}, u32[]{:S(2)}, u32[]{:S(2)}) %collective-permute-start.2) | collective-permute-done | bytes 262176 | tf_op jit(solution)/shard_map/ppermute | solution.py:103
  132.5 4.6 %collective-permute-start.3 = (f32[64,512]{1,0:T(8,128)S(1)}, f32[64,512]{1,0:T(8,128)S(1)}, u32[]{:S(2)}, u32[]{:S(2)}) collective-permute-start(f32[64,512]{1,0:T(8,128)S(1)} %constant_dynamic-slice_fusion.1), channel_id=1, source_target_pairs={{0,4},{1,5},{2,6},{3,7},{4,0},{5,1},{6,2},{7,3},{8,12},{9,13},{10,... | collective-permute-start | bytes 393224 | tf_op jit(solution)/shard_map/ppermute | solution.py:103
  137.2 2.5 collective-permute-done.3
  139.8 4.6 %collective-permute-start.4 = (f32[32,512]{1,0:T(8,128)S(1)}, f32[32,512]{1,0:T(8,128)S(1)}, u32[]{:S(2)}, u32[]{:S(2)}) collective-permute-start(f32[32,512]{1,0:T(8,128)S(1)} %constant_dynamic-slice_fusion), channel_id=1, source_target_pairs={{0,16},{1,17},{2,18},{3,19},{4,20},{5,21},{6,22},{7,23},{8,24},{9,... | collective-permute-start | bytes 196616 | tf_op jit(solution)/shard_map/ppermute | solution.py:103
  144.4 1.9 collective-permute-done.4
  146.3 4.6 %collective-permute-start.5 = (f32[32,512]{1,0:T(8,128)S(1)}, f32[32,512]{1,0:T(8,128)S(1)}, u32[]{:S(2)}, u32[]{:S(2)}) collective-permute-start(f32[32,512]{1,0:T(8,128)S(1)} %dynamic-slice_add_fusion.4), channel_id=1, source_target_pairs={{0,16},{1,17},{2,18},{3,19},{4,20},{5,21},{6,22},{7,23},{8,24},{9,... | collective-permute-start | bytes 196616 | tf_op jit(solution)/shard_map/ppermute | solution.py:107
  151.0 1.9 collective-permute-done.5
  152.9 4.6 %collective-permute-start.6 = (f32[64,512]{1,0:T(8,128)S(1)}, f32[64,512]{1,0:T(8,128)S(1)}, u32[]{:S(2)}, u32[]{:S(2)}) collective-permute-start(f32[64,512]{1,0:T(8,128)S(1)} %pad_maximum_fusion.3), channel_id=1, source_target_pairs={{0,4},{1,5},{2,6},{3,7},{4,0},{5,1},{6,2},{7,3},{8,12},{9,13},{10,... | collective-permute-start | bytes 393224 | tf_op jit(solution)/shard_map/ppermute | solution.py:107
  157.5 2.6 collective-permute-done.6
  160.1 3.1 collective-permute-start.7
  163.2 4.0 %collective-permute-done.7 = f32[128,512]{1,0:T(8,128)S(1)} collective-permute-done((f32[128,512]{1,0:T(8,128)S(1)}, f32[128,512]{1,0:T(8,128)S(1)}, u32[]{:S(2)}, u32[]{:S(2)}) %collective-permute-start.7) | collective-permute-done | bytes 262176 | tf_op jit(solution)/shard_map/ppermute | solution.py:107
  167.4 3.1 collective-permute-start.8
  170.5 6.8 %collective-permute-done.8 = f32[256,512]{1,0:T(8,128)S(1)} collective-permute-done((f32[256,512]{1,0:T(8,128)S(1)}, f32[256,512]{1,0:T(8,128)S(1)}, u32[]{:S(2)}, u32[]{:S(2)}) %collective-permute-start.8) | collective-permute-done | bytes 524320 | tf_op jit(solution)/shard_map/ppermute | solution.py:107
  177.3 0.1 broadcast_select_fusion.3
  177.4 0.1 pad_maximum_fusion
  177.5 11.1 %collective-permute-start.9 = (f32[512,512]{1,0:T(8,128)S(1)}, f32[512,512]{1,0:T(8,128)S(1)}, u32[]{:S(2)}, u32[]{:S(2)}) collective-permute-start(f32[512,512]{1,0:T(8,128)S(1)} %pad_maximum_fusion), channel_id=1, source_target_pairs={{0,1},{1,0},{2,3},{3,2},{4,5},{5,4},{6,7},{7,6},{8,9},{9,8},{10,11... | collective-permute-start | bytes 3145736 | tf_op jit(solution)/shard_map/ppermute | solution.py:107
  188.6 1.1 slice.24
  189.7 8.8 %fusion.1 = f32[768,4096]{1,0:T(8,128)} fusion(bf16[4096,512]{1,0:T(8,128)(2,1)} %copy-done.1, bf16[512,512]{1,0:T(8,128)(2,1)S(1)} %slice.24, bf16[256,512]{1,0:T(8,128)(2,1)S(1)} %constant_dynamic-slice_fusion.5), kind=kOutput, calls=%fused_computation.11 | convolution fusion | flops 3222798336 | bytes 17563648 | tf_op jit(solution)/shard_map/dot_general | solution.py:144
  198.5 0.0 collective-permute-done.9
  198.5 0.2 broadcast_select_fusion.1
  198.7 0.2 maximum_multiply_fusion
  199.0 0.0 reduce-scatter.2.cloned.1.call-update
  199.0 0.5 slice.20
  200.2 1.1 select_add_fusion.a_ref
  201.3 142.6 %shard_map.30 = (f32[512,512]{1,0:T(8,128)}, f32[512,512]{1,0:T(8,128)}) custom-call(f32[512,512]{1,0:T(8,128)} %select_add_fusion.a_ref), custom_call_target="tpu_custom_call" | custom-call | flops 268435456 | bytes 3145728 | tf_op jit(solution)/shard_map/pallas_call | solution.py:77
  343.9 2.4 fusion.5
  346.3 0.0 copy-start.2
  346.3 0.0 reduce-scatter.2.cloned.1.call-done
  346.3 1.2 broadcast_multiply_fusion
  347.5 2.2 fusion.9
  349.7 1.2 convolution_subtract_fusion
  351.0 0.0 copy-done.2
  (18 shorter events, 0.4 us)
Async XLA Ops:
  7.2 78.2 %all-gather.2.cloned.1.call-start = ((), (), s32[]{:S(2)}) async-start(), calls=%async_computation.1 | async-start | bytes 4456448 | tf_op jit(solution)/shard_map/all_gather | solution.py:126
  7.9 338.4 %reduce-scatter.2.cloned.1.call-start = ((), (), s32[]{:S(2)}) async-start(), calls=%async_computation.2 | async-start | bytes 12976128 | tf_op jit(solution)/shard_map/reduce_scatter | solution.py:146
  85.3 3.4 copy-start
  91.6 1.9 copy-start.1
  93.5 13.9 %collective-permute-start = (f32[512,512]{1,0:T(8,128)S(1)}, f32[512,512]{1,0:T(8,128)}, u32[]{:S(2)}, u32[]{:S(2)}) collective-permute-start(f32[512,512]{1,0:T(8,128)S(1)} %constant_dynamic-slice_fusion.4), channel_id=1, source_target_pairs={{0,1},{1,0},{2,3},{3,2},{4,5},{5,4},{6,7},{7,6},{8,9},{9,8},{10,11... | collective-permute-start | bytes 3145736 | tf_op jit(solution)/shard_map/ppermute | solution.py:103
  108.8 15.0 %collective-permute-start.1 = (f32[256,512]{1,0:T(8,128)S(1)}, f32[256,512]{1,0:T(8,128)S(1)}, u32[]{:S(2)}, u32[]{:S(2)}) collective-permute-start(f32[256,512]{1,0:T(8,128)S(1)} %constant_dynamic-slice_fusion.3), channel_id=1, source_target_pairs={{0,2},{1,3},{2,0},{3,1},{4,6},{5,7},{6,4},{7,5},{8,10},{9,11},{10,... | collective-permute-start | bytes 1572872 | tf_op jit(solution)/shard_map/ppermute | solution.py:103
  124.0 8.5 %collective-permute-start.2 = (f32[128,512]{1,0:T(8,128)S(1)}, f32[128,512]{1,0:T(8,128)S(1)}, u32[]{:S(2)}, u32[]{:S(2)}) collective-permute-start(f32[128,512]{1,0:T(8,128)S(1)} %constant_dynamic-slice_fusion.2), channel_id=1, source_target_pairs={{0,8},{1,9},{2,10},{3,11},{4,12},{5,13},{6,14},{7,15},{8,0},{9,1},... | collective-permute-start | bytes 786440 | tf_op jit(solution)/shard_map/ppermute | solution.py:103
  132.5 7.2 %collective-permute-start.3 = (f32[64,512]{1,0:T(8,128)S(1)}, f32[64,512]{1,0:T(8,128)S(1)}, u32[]{:S(2)}, u32[]{:S(2)}) collective-permute-start(f32[64,512]{1,0:T(8,128)S(1)} %constant_dynamic-slice_fusion.1), channel_id=1, source_target_pairs={{0,4},{1,5},{2,6},{3,7},{4,0},{5,1},{6,2},{7,3},{8,12},{9,13},{10,... | collective-permute-start | bytes 393224 | tf_op jit(solution)/shard_map/ppermute | solution.py:103
  139.8 6.5 %collective-permute-start.4 = (f32[32,512]{1,0:T(8,128)S(1)}, f32[32,512]{1,0:T(8,128)S(1)}, u32[]{:S(2)}, u32[]{:S(2)}) collective-permute-start(f32[32,512]{1,0:T(8,128)S(1)} %constant_dynamic-slice_fusion), channel_id=1, source_target_pairs={{0,16},{1,17},{2,18},{3,19},{4,20},{5,21},{6,22},{7,23},{8,24},{9,... | collective-permute-start | bytes 196616 | tf_op jit(solution)/shard_map/ppermute | solution.py:103
  146.3 6.5 %collective-permute-start.5 = (f32[32,512]{1,0:T(8,128)S(1)}, f32[32,512]{1,0:T(8,128)S(1)}, u32[]{:S(2)}, u32[]{:S(2)}) collective-permute-start(f32[32,512]{1,0:T(8,128)S(1)} %dynamic-slice_add_fusion.4), channel_id=1, source_target_pairs={{0,16},{1,17},{2,18},{3,19},{4,20},{5,21},{6,22},{7,23},{8,24},{9,... | collective-permute-start | bytes 196616 | tf_op jit(solution)/shard_map/ppermute | solution.py:107
  152.9 7.2 %collective-permute-start.6 = (f32[64,512]{1,0:T(8,128)S(1)}, f32[64,512]{1,0:T(8,128)S(1)}, u32[]{:S(2)}, u32[]{:S(2)}) collective-permute-start(f32[64,512]{1,0:T(8,128)S(1)} %pad_maximum_fusion.3), channel_id=1, source_target_pairs={{0,4},{1,5},{2,6},{3,7},{4,0},{5,1},{6,2},{7,3},{8,12},{9,13},{10,... | collective-permute-start | bytes 393224 | tf_op jit(solution)/shard_map/ppermute | solution.py:107
  160.1 7.1 %collective-permute-start.7 = (f32[128,512]{1,0:T(8,128)S(1)}, f32[128,512]{1,0:T(8,128)S(1)}, u32[]{:S(2)}, u32[]{:S(2)}) collective-permute-start(f32[128,512]{1,0:T(8,128)S(1)} %pad_maximum_fusion.2), channel_id=1, source_target_pairs={{0,8},{1,9},{2,10},{3,11},{4,12},{5,13},{6,14},{7,15},{8,0},{9,1},... | collective-permute-start | bytes 786440 | tf_op jit(solution)/shard_map/ppermute | solution.py:107
  167.4 9.9 %collective-permute-start.8 = (f32[256,512]{1,0:T(8,128)S(1)}, f32[256,512]{1,0:T(8,128)S(1)}, u32[]{:S(2)}, u32[]{:S(2)}) collective-permute-start(f32[256,512]{1,0:T(8,128)S(1)} %pad_maximum_fusion.1), channel_id=1, source_target_pairs={{0,2},{1,3},{2,0},{3,1},{4,6},{5,7},{6,4},{7,5},{8,10},{9,11},{10,... | collective-permute-start | bytes 1572872 | tf_op jit(solution)/shard_map/ppermute | solution.py:107
  177.5 21.0 %collective-permute-start.9 = (f32[512,512]{1,0:T(8,128)S(1)}, f32[512,512]{1,0:T(8,128)S(1)}, u32[]{:S(2)}, u32[]{:S(2)}) collective-permute-start(f32[512,512]{1,0:T(8,128)S(1)} %pad_maximum_fusion), channel_id=1, source_target_pairs={{0,1},{1,0},{2,3},{3,2},{4,5},{5,4},{6,7},{7,6},{8,9},{9,8},{10,11... | collective-permute-start | bytes 3145736 | tf_op jit(solution)/shard_map/ppermute | solution.py:107
  346.3 4.7 %copy-start.2 = (f32[256,512]{1,0:T(8,128)}, f32[256,512]{1,0:T(8,128)S(1)}, u32[]{:S(2)}) copy-start(f32[256,512]{1,0:T(8,128)S(1)} %fusion.5) | copy-start | bytes 1572868
Sparse Core Ops, SparseCore 0:
  10.1 75.2 all-gather.1
  199.1 122.8 reduce-scatter.1

commit v7 on v6

--- a/solution.py
+++ b/solution.py
@@ -26,19 +26,22 @@
     rows = lax.broadcasted_iota(jnp.int32, (b, b), 0)
     cols = lax.broadcasted_iota(jnp.int32, (b, b), 1)
     lane = lax.broadcasted_iota(jnp.int32, (1, b), 1)
+    sub = lax.broadcasted_iota(jnp.int32, (b, 1), 0)
     for k in range(nb):
         ks = pl.ds(k * b, b)
         blk_a[...] = s_ref[ks, ks]
         blk_b[...] = jnp.where(rows == cols, 1.0, 0.0).astype(f32)
 
         def step(j, carry):
+            whole = blk_a[...]
             row = blk_a[pl.ds(j, 1), :]
+            col = jnp.sum(jnp.where(cols == j, whole, 0.0), axis=1, keepdims=True)
             d = jnp.sum(jnp.where(lane == j, row, 0.0), axis=1, keepdims=True)
-            s = jnp.sqrt(d)
-            v_row = jnp.where(lane >= j, row / s, 0.0)
-            v_col = jnp.transpose(jnp.broadcast_to(v_row, (8, b)))[:, 0:1]
-            blk_a[...] = blk_a[...] - v_col * v_row
-            x = blk_b[pl.ds(j, 1), :] / s
+            r = 1.0 / jnp.sqrt(d)
+            v_row = jnp.where(lane >= j, row * r, 0.0)
+            v_col = jnp.where(sub >= j, col * r, 0.0)
+            blk_a[...] = whole - v_col * v_row
+            x = blk_b[pl.ds(j, 1), :] * r
             blk_b[...] = blk_b[...] - v_col * x
             blk_lt[pl.ds(j, 1), :] = v_row
             blk_w[pl.ds(j, 1), :] = x
@@ -142,7 +145,6 @@
 
     lhs = jnp.concatenate([mine, head], axis=0)
     big = lax.dot_general(lhs, centered, contract, preferred_element_type=f32)
-    big, shared = lax.optimization_barrier((big, shared))
     big = lax.psum_scatter(big, "par", scatter_dimension=1, tiled=True) / param_total
     tile = big[:row_count]
     band_t = big[row_count:]

time: 358 us -> 300 us (0.84)
  Pallas kernels: 143 us -> 65 us
  waiting for transfers between devices: 117 us -> 139 us
    pallas_call x1, Pallas kernels: 143 us -> 65 us  [chol_and_inverse(): pl.pallas_call(functools.partial(_chol_kernel, n=n, b=block), out_shape=(...]
    ppermute x5, waiting for transfers between devices: 15.3 us -> 37.2 us  [reduce_by_halving(): other = lax.ppermute(x, axis, [(i, i ^ mask) for i in range(count)])]
  transfers between devices with their start and end apart: 12 -> 12, of which waited for: 10 -> 11; matrix products, arithmetic and copies ran while one was open for 4% -> 3% of each run, Pallas kernels for 40% -> 22%
where the time goes in v7:
time: 300 us; the launch traced here: 299 us
  waiting for transfers between devices  139 us (46%)
  Pallas kernels  65 us (22%)
  starting transfers between devices  50 us (17%)
  matrix products  15.2 us (5%)
  between operations  15.2 us (5%)
  other arithmetic  10.6 us (4%)
  local copies, waits for them, and re-layouts  3.77 us (1%)
    all_gather x1, waiting for transfers between devices, shards(): gathered = lax.all_gather(jacobian, 'smp', axis=0, tiled=True)  77.4 us
    pallas_call x1, Pallas kernels, chol_and_inverse(): pl.pallas_call(functools.partial(_chol_kernel, n=n, b=block), out_shape=(...  65 us
    ppermute x5, waiting for transfers between devices, reduce_by_halving(): other = lax.ppermute(x, axis, [(i, i ^ mask) for i in range(count)])  37.2 us
    ppermute x5, starting transfers between devices, reduce_by_halving(): x = keep + lax.ppermute(send, axis, [(i, i ^ mask) for i in range(count)])  26.9 us
    ppermute x5, waiting for transfers between devices, reduce_by_halving(): x = keep + lax.ppermute(send, axis, [(i, i ^ mask) for i in range(count)])  24 us
    ppermute x5, starting transfers between devices, reduce_by_halving(): other = lax.ppermute(x, axis, [(i, i ^ mask) for i in range(count)])  23.1 us
    dot_general x1, matrix products, shards(): big = lax.dot_general(lhs, centered, contract, preferred_element_type=f32)  6.39 us
  transfers between devices with their start and end apart: 12, of which 11 were waited for; matrix products, arithmetic and copies ran while one was open for 3% of the time, Pallas kernels for 22%

profile of v7, /device:TPU:1, one launch (start us, length us, event | category | flops | bytes accessed | tf_op | source)
XLA Modules:
  0.0 299.3 jit_solution(15072165238959011505)
XLA Ops:
  7.2 0.0 all-gather.2.cloned.1.call-start
  7.2 0.7 all-gather.2.cloned.1.call-update
  7.9 0.0 reduce-scatter.2.cloned.1.call-start
  7.9 77.4 %all-gather.2.cloned.1.call-done = bf16[4096,512]{1,0:T(8,128)(2,1)} async-done(((bf16[256,512]{1,0:T(8,128)(2,1)}), bf16[4096,512]{1,0:T(8,128)(2,1)}) %all-gather.2.cloned.1.call-update) | async-done | bytes 4194320 | tf_op jit(solution)/shard_map/all_gather | solution.py:129
  85.3 0.0 copy-start
  85.3 3.0 convert_reduce_fusion
  88.3 0.5 copy-done
  88.8 2.8 multiply_reduce_fusion
  91.6 0.0 copy-start.1
  91.7 1.9 copy-done.1
  93.5 6.4 %fusion.1 = f32[768,4096]{1,0:T(8,128)} fusion(bf16[4096,512]{1,0:T(8,128)(2,1)S(1)} %get-tuple-element.5, bf16[512,512]{1,0:T(8,128)(2,1)S(1)} %slice.24, bf16[256,512]{1,0:T(8,128)(2,1)S(1)} %constant_dynamic-slice_fusion.5), kind=kOutput, calls=%fused_computation.11 | convolution fusion | flops 3222798336 | bytes 17563648 | tf_op jit(solution)/shard_map/dot_general | solution.py:147
  99.9 0.0 reduce-scatter.2.cloned.1.call-update
  100.0 0.6 broadcast_in_dim.44
  100.6 1.4 fusion.20
  102.0 1.7 fusion.18
  103.7 0.2 maximum_maximum_fusion
  103.9 0.1 constant_dynamic-slice_fusion.4
  104.0 11.5 %collective-permute-start = (f32[512,512]{1,0:T(8,128)S(1)}, f32[512,512]{1,0:T(8,128)}, u32[]{:S(2)}, u32[]{:S(2)}) collective-permute-start(f32[512,512]{1,0:T(8,128)S(1)} %constant_dynamic-slice_fusion.4), channel_id=1, source_target_pairs={{0,1},{1,0},{2,3},{3,2},{4,5},{5,4},{6,7},{7,6},{8,9},{9,8},{10,11... | collective-permute-start | bytes 3145736 | tf_op jit(solution)/shard_map/ppermute | solution.py:106
  115.5 2.4 collective-permute-done
  117.9 1.4 dynamic-slice_add_fusion
  119.3 3.1 %collective-permute-start.1 = (f32[256,512]{1,0:T(8,128)S(1)}, f32[256,512]{1,0:T(8,128)S(1)}, u32[]{:S(2)}, u32[]{:S(2)}) collective-permute-start(f32[256,512]{1,0:T(8,128)S(1)} %constant_dynamic-slice_fusion.3), channel_id=1, source_target_pairs={{0,2},{1,3},{2,0},{3,1},{4,6},{5,7},{6,4},{7,5},{8,10},{9,11},{10,... | collective-permute-start | bytes 1572872 | tf_op jit(solution)/shard_map/ppermute | solution.py:106
  122.5 11.9 %collective-permute-done.1 = f32[256,512]{1,0:T(8,128)S(1)} collective-permute-done((f32[256,512]{1,0:T(8,128)S(1)}, f32[256,512]{1,0:T(8,128)S(1)}, u32[]{:S(2)}, u32[]{:S(2)}) %collective-permute-start.1) | collective-permute-done | bytes 524320 | tf_op jit(solution)/shard_map/ppermute | solution.py:106
  134.4 0.1 dynamic-slice_add_fusion.1
  134.5 3.1 %collective-permute-start.2 = (f32[128,512]{1,0:T(8,128)S(1)}, f32[128,512]{1,0:T(8,128)S(1)}, u32[]{:S(2)}, u32[]{:S(2)}) collective-permute-start(f32[128,512]{1,0:T(8,128)S(1)} %constant_dynamic-slice_fusion.2), channel_id=1, source_target_pairs={{0,8},{1,9},{2,10},{3,11},{4,12},{5,13},{6,14},{7,15},{8,0},{9,1},... | collective-permute-start | bytes 786440 | tf_op jit(solution)/shard_map/ppermute | solution.py:106
  137.6 5.4 %collective-permute-done.2 = f32[128,512]{1,0:T(8,128)S(1)} collective-permute-done((f32[128,512]{1,0:T(8,128)S(1)}, f32[128,512]{1,0:T(8,128)S(1)}, u32[]{:S(2)}, u32[]{:S(2)}) %collective-permute-start.2) | collective-permute-done | bytes 262176 | tf_op jit(solution)/shard_map/ppermute | solution.py:106
  143.0 4.6 %collective-permute-start.3 = (f32[64,512]{1,0:T(8,128)S(1)}, f32[64,512]{1,0:T(8,128)S(1)}, u32[]{:S(2)}, u32[]{:S(2)}) collective-permute-start(f32[64,512]{1,0:T(8,128)S(1)} %constant_dynamic-slice_fusion.1), channel_id=1, source_target_pairs={{0,4},{1,5},{2,6},{3,7},{4,0},{5,1},{6,2},{7,3},{8,12},{9,13},{10,... | collective-permute-start | bytes 393224 | tf_op jit(solution)/shard_map/ppermute | solution.py:106
  147.7 2.5 collective-permute-done.3
  150.3 4.6 %collective-permute-start.4 = (f32[32,512]{1,0:T(8,128)S(1)}, f32[32,512]{1,0:T(8,128)S(1)}, u32[]{:S(2)}, u32[]{:S(2)}) collective-permute-start(f32[32,512]{1,0:T(8,128)S(1)} %constant_dynamic-slice_fusion), channel_id=1, source_target_pairs={{0,16},{1,17},{2,18},{3,19},{4,20},{5,21},{6,22},{7,23},{8,24},{9,... | collective-permute-start | bytes 196616 | tf_op jit(solution)/shard_map/ppermute | solution.py:106
  154.9 1.9 collective-permute-done.4
  156.8 4.6 %collective-permute-start.5 = (f32[32,512]{1,0:T(8,128)S(1)}, f32[32,512]{1,0:T(8,128)S(1)}, u32[]{:S(2)}, u32[]{:S(2)}) collective-permute-start(f32[32,512]{1,0:T(8,128)S(1)} %dynamic-slice_add_fusion.4), channel_id=1, source_target_pairs={{0,16},{1,17},{2,18},{3,19},{4,20},{5,21},{6,22},{7,23},{8,24},{9,... | collective-permute-start | bytes 196616 | tf_op jit(solution)/shard_map/ppermute | solution.py:110
  161.5 1.9 collective-permute-done.5
  163.4 4.6 %collective-permute-start.6 = (f32[64,512]{1,0:T(8,128)S(1)}, f32[64,512]{1,0:T(8,128)S(1)}, u32[]{:S(2)}, u32[]{:S(2)}) collective-permute-start(f32[64,512]{1,0:T(8,128)S(1)} %pad_maximum_fusion.3), channel_id=1, source_target_pairs={{0,4},{1,5},{2,6},{3,7},{4,0},{5,1},{6,2},{7,3},{8,12},{9,13},{10,... | collective-permute-start | bytes 393224 | tf_op jit(solution)/shard_map/ppermute | solution.py:110
  168.0 2.6 collective-permute-done.6
  170.7 3.1 %collective-permute-start.7 = (f32[128,512]{1,0:T(8,128)S(1)}, f32[128,512]{1,0:T(8,128)S(1)}, u32[]{:S(2)}, u32[]{:S(2)}) collective-permute-start(f32[128,512]{1,0:T(8,128)S(1)} %pad_maximum_fusion.2), channel_id=1, source_target_pairs={{0,8},{1,9},{2,10},{3,11},{4,12},{5,13},{6,14},{7,15},{8,0},{9,1},... | collective-permute-start | bytes 786440 | tf_op jit(solution)/shard_map/ppermute | solution.py:110
  173.7 9.9 %collective-permute-done.7 = f32[128,512]{1,0:T(8,128)S(1)} collective-permute-done((f32[128,512]{1,0:T(8,128)S(1)}, f32[128,512]{1,0:T(8,128)S(1)}, u32[]{:S(2)}, u32[]{:S(2)}) %collective-permute-start.7) | collective-permute-done | bytes 262176 | tf_op jit(solution)/shard_map/ppermute | solution.py:110
  183.7 3.1 %collective-permute-start.8 = (f32[256,512]{1,0:T(8,128)S(1)}, f32[256,512]{1,0:T(8,128)S(1)}, u32[]{:S(2)}, u32[]{:S(2)}) collective-permute-start(f32[256,512]{1,0:T(8,128)S(1)} %pad_maximum_fusion.1), channel_id=1, source_target_pairs={{0,2},{1,3},{2,0},{3,1},{4,6},{5,7},{6,4},{7,5},{8,10},{9,11},{10,... | collective-permute-start | bytes 1572872 | tf_op jit(solution)/shard_map/ppermute | solution.py:110
  186.8 20.8 %collective-permute-done.8 = f32[256,512]{1,0:T(8,128)S(1)} collective-permute-done((f32[256,512]{1,0:T(8,128)S(1)}, f32[256,512]{1,0:T(8,128)S(1)}, u32[]{:S(2)}, u32[]{:S(2)}) %collective-permute-start.8) | collective-permute-done | bytes 524320 | tf_op jit(solution)/shard_map/ppermute | solution.py:110
  207.6 0.1 broadcast_select_fusion.3
  207.7 0.1 pad_maximum_fusion
  207.8 7.7 %collective-permute-start.9 = (f32[512,512]{1,0:T(8,128)S(1)}, f32[512,512]{1,0:T(8,128)S(1)}, u32[]{:S(2)}, u32[]{:S(2)}) collective-permute-start(f32[512,512]{1,0:T(8,128)S(1)} %pad_maximum_fusion), channel_id=1, source_target_pairs={{0,1},{1,0},{2,3},{3,2},{4,5},{5,4},{6,7},{7,6},{8,9},{9,8},{10,11... | collective-permute-start | bytes 3145736 | tf_op jit(solution)/shard_map/ppermute | solution.py:110
  215.5 2.0 collective-permute-done.9
  217.6 0.2 broadcast_select_fusion.1
  217.8 0.2 maximum_multiply_fusion
  218.1 0.5 slice.26
  219.2 1.1 slice_add_fusion.a_ref
  220.3 65.0 %shard_map.30 = (f32[512,512]{1,0:T(8,128)}, f32[512,512]{1,0:T(8,128)}) custom-call(f32[512,512]{1,0:T(8,128)} %slice_add_fusion.a_ref), custom_call_target="tpu_custom_call" | custom-call | flops 268435456 | bytes 3145728 | tf_op jit(solution)/shard_map/pallas_call | solution.py:80
  285.3 2.4 fusion.5
  287.7 0.0 copy-start.2
  287.7 0.0 reduce-scatter.2.cloned.1.call-done
  287.8 1.2 broadcast_multiply_fusion
  289.0 2.2 fusion.7
  291.2 1.2 convolution_subtract_fusion
  292.4 0.0 copy-done.2
  (19 shorter events, 0.4 us)
Async XLA Ops:
  7.2 78.2 %all-gather.2.cloned.1.call-start = ((), (), s32[]{:S(2)}) async-start(), calls=%async_computation.1 | async-start | bytes 4456448 | tf_op jit(solution)/shard_map/all_gather | solution.py:129
  7.9 279.9 %reduce-scatter.2.cloned.1.call-start = ((), (), s32[]{:S(2)}) async-start(), calls=%async_computation.2 | async-start | bytes 12976128 | tf_op jit(solution)/shard_map/reduce_scatter | solution.py:148
  85.3 3.4 %copy-start = (bf16[4096,512]{1,0:T(8,128)(2,1)S(1)}, bf16[4096,512]{1,0:T(8,128)(2,1)}, u32[]{:S(2)}) copy-start(bf16[4096,512]{1,0:T(8,128)(2,1)} %all-gather.2.cloned.1.call-done) | copy-start | bytes 12582916
  91.6 1.9 copy-start.1
  104.0 13.9 %collective-permute-start = (f32[512,512]{1,0:T(8,128)S(1)}, f32[512,512]{1,0:T(8,128)}, u32[]{:S(2)}, u32[]{:S(2)}) collective-permute-start(f32[512,512]{1,0:T(8,128)S(1)} %constant_dynamic-slice_fusion.4), channel_id=1, source_target_pairs={{0,1},{1,0},{2,3},{3,2},{4,5},{5,4},{6,7},{7,6},{8,9},{9,8},{10,11... | collective-permute-start | bytes 3145736 | tf_op jit(solution)/shard_map/ppermute | solution.py:106
  119.3 15.0 %collective-permute-start.1 = (f32[256,512]{1,0:T(8,128)S(1)}, f32[256,512]{1,0:T(8,128)S(1)}, u32[]{:S(2)}, u32[]{:S(2)}) collective-permute-start(f32[256,512]{1,0:T(8,128)S(1)} %constant_dynamic-slice_fusion.3), channel_id=1, source_target_pairs={{0,2},{1,3},{2,0},{3,1},{4,6},{5,7},{6,4},{7,5},{8,10},{9,11},{10,... | collective-permute-start | bytes 1572872 | tf_op jit(solution)/shard_map/ppermute | solution.py:106
  134.5 8.5 %collective-permute-start.2 = (f32[128,512]{1,0:T(8,128)S(1)}, f32[128,512]{1,0:T(8,128)S(1)}, u32[]{:S(2)}, u32[]{:S(2)}) collective-permute-start(f32[128,512]{1,0:T(8,128)S(1)} %constant_dynamic-slice_fusion.2), channel_id=1, source_target_pairs={{0,8},{1,9},{2,10},{3,11},{4,12},{5,13},{6,14},{7,15},{8,0},{9,1},... | collective-permute-start | bytes 786440 | tf_op jit(solution)/shard_map/ppermute | solution.py:106
  143.0 7.2 %collective-permute-start.3 = (f32[64,512]{1,0:T(8,128)S(1)}, f32[64,512]{1,0:T(8,128)S(1)}, u32[]{:S(2)}, u32[]{:S(2)}) collective-permute-start(f32[64,512]{1,0:T(8,128)S(1)} %constant_dynamic-slice_fusion.1), channel_id=1, source_target_pairs={{0,4},{1,5},{2,6},{3,7},{4,0},{5,1},{6,2},{7,3},{8,12},{9,13},{10,... | collective-permute-start | bytes 393224 | tf_op jit(solution)/shard_map/ppermute | solution.py:106
  150.3 6.5 %collective-permute-start.4 = (f32[32,512]{1,0:T(8,128)S(1)}, f32[32,512]{1,0:T(8,128)S(1)}, u32[]{:S(2)}, u32[]{:S(2)}) collective-permute-start(f32[32,512]{1,0:T(8,128)S(1)} %constant_dynamic-slice_fusion), channel_id=1, source_target_pairs={{0,16},{1,17},{2,18},{3,19},{4,20},{5,21},{6,22},{7,23},{8,24},{9,... | collective-permute-start | bytes 196616 | tf_op jit(solution)/shard_map/ppermute | solution.py:106
  156.8 6.5 %collective-permute-start.5 = (f32[32,512]{1,0:T(8,128)S(1)}, f32[32,512]{1,0:T(8,128)S(1)}, u32[]{:S(2)}, u32[]{:S(2)}) collective-permute-start(f32[32,512]{1,0:T(8,128)S(1)} %dynamic-slice_add_fusion.4), channel_id=1, source_target_pairs={{0,16},{1,17},{2,18},{3,19},{4,20},{5,21},{6,22},{7,23},{8,24},{9,... | collective-permute-start | bytes 196616 | tf_op jit(solution)/shard_map/ppermute | solution.py:110
  163.4 7.2 %collective-permute-start.6 = (f32[64,512]{1,0:T(8,128)S(1)}, f32[64,512]{1,0:T(8,128)S(1)}, u32[]{:S(2)}, u32[]{:S(2)}) collective-permute-start(f32[64,512]{1,0:T(8,128)S(1)} %pad_maximum_fusion.3), channel_id=1, source_target_pairs={{0,4},{1,5},{2,6},{3,7},{4,0},{5,1},{6,2},{7,3},{8,12},{9,13},{10,... | collective-permute-start | bytes 393224 | tf_op jit(solution)/shard_map/ppermute | solution.py:110
  170.7 13.0 %collective-permute-start.7 = (f32[128,512]{1,0:T(8,128)S(1)}, f32[128,512]{1,0:T(8,128)S(1)}, u32[]{:S(2)}, u32[]{:S(2)}) collective-permute-start(f32[128,512]{1,0:T(8,128)S(1)} %pad_maximum_fusion.2), channel_id=1, source_target_pairs={{0,8},{1,9},{2,10},{3,11},{4,12},{5,13},{6,14},{7,15},{8,0},{9,1},... | collective-permute-start | bytes 786440 | tf_op jit(solution)/shard_map/ppermute | solution.py:110
  183.7 23.9 %collective-permute-start.8 = (f32[256,512]{1,0:T(8,128)S(1)}, f32[256,512]{1,0:T(8,128)S(1)}, u32[]{:S(2)}, u32[]{:S(2)}) collective-permute-start(f32[256,512]{1,0:T(8,128)S(1)} %pad_maximum_fusion.1), channel_id=1, source_target_pairs={{0,2},{1,3},{2,0},{3,1},{4,6},{5,7},{6,4},{7,5},{8,10},{9,11},{10,... | collective-permute-start | bytes 1572872 | tf_op jit(solution)/shard_map/ppermute | solution.py:110
  207.8 9.8 %collective-permute-start.9 = (f32[512,512]{1,0:T(8,128)S(1)}, f32[512,512]{1,0:T(8,128)S(1)}, u32[]{:S(2)}, u32[]{:S(2)}) collective-permute-start(f32[512,512]{1,0:T(8,128)S(1)} %pad_maximum_fusion), channel_id=1, source_target_pairs={{0,1},{1,0},{2,3},{3,2},{4,5},{5,4},{6,7},{7,6},{8,9},{9,8},{10,11... | collective-permute-start | bytes 3145736 | tf_op jit(solution)/shard_map/ppermute | solution.py:110
  287.7 4.7 %copy-start.2 = (f32[256,512]{1,0:T(8,128)}, f32[256,512]{1,0:T(8,128)S(1)}, u32[]{:S(2)}) copy-start(f32[256,512]{1,0:T(8,128)S(1)} %fusion.5) | copy-start | bytes 1572868
Sparse Core Ops, SparseCore 0:
  10.1 75.2 all-gather.1
  100.1 142.8 reduce-scatter.1

commit v8 on v7

--- a/solution.py
+++ b/solution.py
@@ -37,7 +37,7 @@
             row = blk_a[pl.ds(j, 1), :]
             col = jnp.sum(jnp.where(cols == j, whole, 0.0), axis=1, keepdims=True)
             d = jnp.sum(jnp.where(lane == j, row, 0.0), axis=1, keepdims=True)
-            r = 1.0 / jnp.sqrt(d)
+            r = lax.rsqrt(d)
             v_row = jnp.where(lane >= j, row * r, 0.0)
             v_col = jnp.where(sub >= j, col * r, 0.0)
             blk_a[...] = whole - v_col * v_row

time: 300 us -> 296 us (0.987)
  Pallas kernels: 65 us -> 61.2 us
    pallas_call x1, Pallas kernels: 65 us -> 61.2 us  [chol_and_inverse(): pl.pallas_call(functools.partial(_chol_kernel, n=n, b=block), out_shape=(...]
  transfers between devices with their start and end apart: 12 -> 12, of which waited for: 11 -> 11; matrix products, arithmetic and copies ran while one was open for 3% -> 4% of each run, Pallas kernels for 22% -> 21%
where the time goes in v8:
time: 296 us; the launch traced here: 295 us
  waiting for transfers between devices  139 us (47%)
  Pallas kernels  61.2 us (21%)
  starting transfers between devices  50 us (17%)
  matrix products  15.2 us (5%)
  between operations  15.2 us (5%)
  other arithmetic  10.6 us (4%)
  local copies, waits for them, and re-layouts  3.77 us (1%)
    all_gather x1, waiting for transfers between devices, shards(): gathered = lax.all_gather(jacobian, 'smp', axis=0, tiled=True)  77.4 us
    pallas_call x1, Pallas kernels, chol_and_inverse(): pl.pallas_call(functools.partial(_chol_kernel, n=n, b=block), out_shape=(...  61.2 us
    ppermute x5, waiting for transfers between devices, reduce_by_halving(): other = lax.ppermute(x, axis, [(i, i ^ mask) for i in range(count)])  37.2 us
    ppermute x5, starting transfers between devices, reduce_by_halving(): x = keep + lax.ppermute(send, axis, [(i, i ^ mask) for i in range(count)])  26.9 us
    ppermute x5, waiting for transfers between devices, reduce_by_halving(): x = keep + lax.ppermute(send, axis, [(i, i ^ mask) for i in range(count)])  24 us
    ppermute x5, starting transfers between devices, reduce_by_halving(): other = lax.ppermute(x, axis, [(i, i ^ mask) for i in range(count)])  23.1 us
    dot_general x1, matrix products, shards(): big = lax.dot_general(lhs, centered, contract, preferred_element_type=f32)  6.39 us
  transfers between devices with their start and end apart: 12, of which 11 were waited for; matrix products, arithmetic and copies ran while one was open for 4% of the time, Pallas kernels for 21%

profile of v8, /device:TPU:1, one launch (start us, length us, event | category | flops | bytes accessed | tf_op | source)
XLA Modules:
  0.0 295.4 jit_solution(12407991540327175538)
XLA Ops:
  7.2 0.0 all-gather.2.cloned.1.call-start
  7.2 0.7 all-gather.2.cloned.1.call-update
  7.9 0.0 reduce-scatter.2.cloned.1.call-start
  7.9 77.4 %all-gather.2.cloned.1.call-done = bf16[4096,512]{1,0:T(8,128)(2,1)} async-done(((bf16[256,512]{1,0:T(8,128)(2,1)}), bf16[4096,512]{1,0:T(8,128)(2,1)}) %all-gather.2.cloned.1.call-update) | async-done | bytes 4194320 | tf_op jit(solution)/shard_map/all_gather | solution.py:129
  85.3 0.0 copy-start
  85.3 3.0 convert_reduce_fusion
  88.3 0.5 copy-done
  88.8 2.8 multiply_reduce_fusion
  91.6 0.0 copy-start.1
  91.7 1.9 copy-done.1
  93.5 6.4 %fusion.1 = f32[768,4096]{1,0:T(8,128)} fusion(bf16[4096,512]{1,0:T(8,128)(2,1)S(1)} %get-tuple-element.5, bf16[512,512]{1,0:T(8,128)(2,1)S(1)} %slice.24, bf16[256,512]{1,0:T(8,128)(2,1)S(1)} %constant_dynamic-slice_fusion.5), kind=kOutput, calls=%fused_computation.11 | convolution fusion | flops 3222798336 | bytes 17563648 | tf_op jit(solution)/shard_map/dot_general | solution.py:147
  99.9 0.0 reduce-scatter.2.cloned.1.call-update
  100.0 0.6 broadcast_in_dim.44
  100.6 1.4 fusion.20
  102.0 1.7 fusion.18
  103.7 0.2 maximum_maximum_fusion
  103.9 0.1 constant_dynamic-slice_fusion.4
  104.0 11.5 %collective-permute-start = (f32[512,512]{1,0:T(8,128)S(1)}, f32[512,512]{1,0:T(8,128)}, u32[]{:S(2)}, u32[]{:S(2)}) collective-permute-start(f32[512,512]{1,0:T(8,128)S(1)} %constant_dynamic-slice_fusion.4), channel_id=1, source_target_pairs={{0,1},{1,0},{2,3},{3,2},{4,5},{5,4},{6,7},{7,6},{8,9},{9,8},{10,11... | collective-permute-start | bytes 3145736 | tf_op jit(solution)/shard_map/ppermute | solution.py:106
  115.5 2.4 collective-permute-done
  117.9 1.4 dynamic-slice_add_fusion
  119.3 3.1 %collective-permute-start.1 = (f32[256,512]{1,0:T(8,128)S(1)}, f32[256,512]{1,0:T(8,128)S(1)}, u32[]{:S(2)}, u32[]{:S(2)}) collective-permute-start(f32[256,512]{1,0:T(8,128)S(1)} %constant_dynamic-slice_fusion.3), channel_id=1, source_target_pairs={{0,2},{1,3},{2,0},{3,1},{4,6},{5,7},{6,4},{7,5},{8,10},{9,11},{10,... | collective-permute-start | bytes 1572872 | tf_op jit(solution)/shard_map/ppermute | solution.py:106
  122.5 11.9 %collective-permute-done.1 = f32[256,512]{1,0:T(8,128)S(1)} collective-permute-done((f32[256,512]{1,0:T(8,128)S(1)}, f32[256,512]{1,0:T(8,128)S(1)}, u32[]{:S(2)}, u32[]{:S(2)}) %collective-permute-start.1) | collective-permute-done | bytes 524320 | tf_op jit(solution)/shard_map/ppermute | solution.py:106
  134.4 0.1 dynamic-slice_add_fusion.1
  134.5 3.1 %collective-permute-start.2 = (f32[128,512]{1,0:T(8,128)S(1)}, f32[128,512]{1,0:T(8,128)S(1)}, u32[]{:S(2)}, u32[]{:S(2)}) collective-permute-start(f32[128,512]{1,0:T(8,128)S(1)} %constant_dynamic-slice_fusion.2), channel_id=1, source_target_pairs={{0,8},{1,9},{2,10},{3,11},{4,12},{5,13},{6,14},{7,15},{8,0},{9,1},... | collective-permute-start | bytes 786440 | tf_op jit(solution)/shard_map/ppermute | solution.py:106
  137.6 5.4 %collective-permute-done.2 = f32[128,512]{1,0:T(8,128)S(1)} collective-permute-done((f32[128,512]{1,0:T(8,128)S(1)}, f32[128,512]{1,0:T(8,128)S(1)}, u32[]{:S(2)}, u32[]{:S(2)}) %collective-permute-start.2) | collective-permute-done | bytes 262176 | tf_op jit(solution)/shard_map/ppermute | solution.py:106
  143.0 4.6 %collective-permute-start.3 = (f32[64,512]{1,0:T(8,128)S(1)}, f32[64,512]{1,0:T(8,128)S(1)}, u32[]{:S(2)}, u32[]{:S(2)}) collective-permute-start(f32[64,512]{1,0:T(8,128)S(1)} %constant_dynamic-slice_fusion.1), channel_id=1, source_target_pairs={{0,4},{1,5},{2,6},{3,7},{4,0},{5,1},{6,2},{7,3},{8,12},{9,13},{10,... | collective-permute-start | bytes 393224 | tf_op jit(solution)/shard_map/ppermute | solution.py:106
  147.7 2.5 collective-permute-done.3
  150.3 4.6 %collective-permute-start.4 = (f32[32,512]{1,0:T(8,128)S(1)}, f32[32,512]{1,0:T(8,128)S(1)}, u32[]{:S(2)}, u32[]{:S(2)}) collective-permute-start(f32[32,512]{1,0:T(8,128)S(1)} %constant_dynamic-slice_fusion), channel_id=1, source_target_pairs={{0,16},{1,17},{2,18},{3,19},{4,20},{5,21},{6,22},{7,23},{8,24},{9,... | collective-permute-start | bytes 196616 | tf_op jit(solution)/shard_map/ppermute | solution.py:106
  154.9 1.9 collective-permute-done.4
  156.8 4.6 %collective-permute-start.5 = (f32[32,512]{1,0:T(8,128)S(1)}, f32[32,512]{1,0:T(8,128)S(1)}, u32[]{:S(2)}, u32[]{:S(2)}) collective-permute-start(f32[32,512]{1,0:T(8,128)S(1)} %dynamic-slice_add_fusion.4), channel_id=1, source_target_pairs={{0,16},{1,17},{2,18},{3,19},{4,20},{5,21},{6,22},{7,23},{8,24},{9,... | collective-permute-start | bytes 196616 | tf_op jit(solution)/shard_map/ppermute | solution.py:110
  161.5 1.9 collective-permute-done.5
  163.4 4.6 %collective-permute-start.6 = (f32[64,512]{1,0:T(8,128)S(1)}, f32[64,512]{1,0:T(8,128)S(1)}, u32[]{:S(2)}, u32[]{:S(2)}) collective-permute-start(f32[64,512]{1,0:T(8,128)S(1)} %pad_maximum_fusion.3), channel_id=1, source_target_pairs={{0,4},{1,5},{2,6},{3,7},{4,0},{5,1},{6,2},{7,3},{8,12},{9,13},{10,... | collective-permute-start | bytes 393224 | tf_op jit(solution)/shard_map/ppermute | solution.py:110
  168.0 2.6 collective-permute-done.6
  170.7 3.1 %collective-permute-start.7 = (f32[128,512]{1,0:T(8,128)S(1)}, f32[128,512]{1,0:T(8,128)S(1)}, u32[]{:S(2)}, u32[]{:S(2)}) collective-permute-start(f32[128,512]{1,0:T(8,128)S(1)} %pad_maximum_fusion.2), channel_id=1, source_target_pairs={{0,8},{1,9},{2,10},{3,11},{4,12},{5,13},{6,14},{7,15},{8,0},{9,1},... | collective-permute-start | bytes 786440 | tf_op jit(solution)/shard_map/ppermute | solution.py:110
  173.7 9.9 %collective-permute-done.7 = f32[128,512]{1,0:T(8,128)S(1)} collective-permute-done((f32[128,512]{1,0:T(8,128)S(1)}, f32[128,512]{1,0:T(8,128)S(1)}, u32[]{:S(2)}, u32[]{:S(2)}) %collective-permute-start.7) | collective-permute-done | bytes 262176 | tf_op jit(solution)/shard_map/ppermute | solution.py:110
  183.7 3.1 %collective-permute-start.8 = (f32[256,512]{1,0:T(8,128)S(1)}, f32[256,512]{1,0:T(8,128)S(1)}, u32[]{:S(2)}, u32[]{:S(2)}) collective-permute-start(f32[256,512]{1,0:T(8,128)S(1)} %pad_maximum_fusion.1), channel_id=1, source_target_pairs={{0,2},{1,3},{2,0},{3,1},{4,6},{5,7},{6,4},{7,5},{8,10},{9,11},{10,... | collective-permute-start | bytes 1572872 | tf_op jit(solution)/shard_map/ppermute | solution.py:110
  186.8 20.8 %collective-permute-done.8 = f32[256,512]{1,0:T(8,128)S(1)} collective-permute-done((f32[256,512]{1,0:T(8,128)S(1)}, f32[256,512]{1,0:T(8,128)S(1)}, u32[]{:S(2)}, u32[]{:S(2)}) %collective-permute-start.8) | collective-permute-done | bytes 524320 | tf_op jit(solution)/shard_map/ppermute | solution.py:110
  207.6 0.1 broadcast_select_fusion.3
  207.7 0.1 pad_maximum_fusion
  207.8 7.7 %collective-permute-start.9 = (f32[512,512]{1,0:T(8,128)S(1)}, f32[512,512]{1,0:T(8,128)S(1)}, u32[]{:S(2)}, u32[]{:S(2)}) collective-permute-start(f32[512,512]{1,0:T(8,128)S(1)} %pad_maximum_fusion), channel_id=1, source_target_pairs={{0,1},{1,0},{2,3},{3,2},{4,5},{5,4},{6,7},{7,6},{8,9},{9,8},{10,11... | collective-permute-start | bytes 3145736 | tf_op jit(solution)/shard_map/ppermute | solution.py:110
  215.5 2.0 collective-permute-done.9
  217.6 0.2 broadcast_select_fusion.1
  217.8 0.2 maximum_multiply_fusion
  218.1 0.5 slice.26
  219.2 1.1 slice_add_fusion.a_ref
  220.3 61.2 %shard_map.30 = (f32[512,512]{1,0:T(8,128)}, f32[512,512]{1,0:T(8,128)}) custom-call(f32[512,512]{1,0:T(8,128)} %slice_add_fusion.a_ref), custom_call_target="tpu_custom_call" | custom-call | flops 268435456 | bytes 3145728 | tf_op jit(solution)/shard_map/pallas_call | solution.py:80
  281.5 2.4 fusion.5
  283.9 0.0 copy-start.2
  283.9 0.0 reduce-scatter.2.cloned.1.call-done
  283.9 1.2 broadcast_multiply_fusion
  285.1 2.2 fusion.7
  287.3 1.2 convolution_subtract_fusion
  288.6 0.0 copy-done.2
  (19 shorter events, 0.4 us)
Async XLA Ops:
  7.2 78.2 %all-gather.2.cloned.1.call-start = ((), (), s32[]{:S(2)}) async-start(), calls=%async_computation.1 | async-start | bytes 4456448 | tf_op jit(solution)/shard_map/all_gather | solution.py:129
  7.9 276.0 %reduce-scatter.2.cloned.1.call-start = ((), (), s32[]{:S(2)}) async-start(), calls=%async_computation.2 | async-start | bytes 12976128 | tf_op jit(solution)/shard_map/reduce_scatter | solution.py:148
  85.3 3.4 %copy-start = (bf16[4096,512]{1,0:T(8,128)(2,1)S(1)}, bf16[4096,512]{1,0:T(8,128)(2,1)}, u32[]{:S(2)}) copy-start(bf16[4096,512]{1,0:T(8,128)(2,1)} %all-gather.2.cloned.1.call-done) | copy-start | bytes 12582916
  91.6 1.9 copy-start.1
  104.0 13.9 %collective-permute-start = (f32[512,512]{1,0:T(8,128)S(1)}, f32[512,512]{1,0:T(8,128)}, u32[]{:S(2)}, u32[]{:S(2)}) collective-permute-start(f32[512,512]{1,0:T(8,128)S(1)} %constant_dynamic-slice_fusion.4), channel_id=1, source_target_pairs={{0,1},{1,0},{2,3},{3,2},{4,5},{5,4},{6,7},{7,6},{8,9},{9,8},{10,11... | collective-permute-start | bytes 3145736 | tf_op jit(solution)/shard_map/ppermute | solution.py:106
  119.3 15.0 %collective-permute-start.1 = (f32[256,512]{1,0:T(8,128)S(1)}, f32[256,512]{1,0:T(8,128)S(1)}, u32[]{:S(2)}, u32[]{:S(2)}) collective-permute-start(f32[256,512]{1,0:T(8,128)S(1)} %constant_dynamic-slice_fusion.3), channel_id=1, source_target_pairs={{0,2},{1,3},{2,0},{3,1},{4,6},{5,7},{6,4},{7,5},{8,10},{9,11},{10,... | collective-permute-start | bytes 1572872 | tf_op jit(solution)/shard_map/ppermute | solution.py:106
  134.5 8.5 %collective-permute-start.2 = (f32[128,512]{1,0:T(8,128)S(1)}, f32[128,512]{1,0:T(8,128)S(1)}, u32[]{:S(2)}, u32[]{:S(2)}) collective-permute-start(f32[128,512]{1,0:T(8,128)S(1)} %constant_dynamic-slice_fusion.2), channel_id=1, source_target_pairs={{0,8},{1,9},{2,10},{3,11},{4,12},{5,13},{6,14},{7,15},{8,0},{9,1},... | collective-permute-start | bytes 786440 | tf_op jit(solution)/shard_map/ppermute | solution.py:106
  143.0 7.2 %collective-permute-start.3 = (f32[64,512]{1,0:T(8,128)S(1)}, f32[64,512]{1,0:T(8,128)S(1)}, u32[]{:S(2)}, u32[]{:S(2)}) collective-permute-start(f32[64,512]{1,0:T(8,128)S(1)} %constant_dynamic-slice_fusion.1), channel_id=1, source_target_pairs={{0,4},{1,5},{2,6},{3,7},{4,0},{5,1},{6,2},{7,3},{8,12},{9,13},{10,... | collective-permute-start | bytes 393224 | tf_op jit(solution)/shard_map/ppermute | solution.py:106
  150.3 6.5 %collective-permute-start.4 = (f32[32,512]{1,0:T(8,128)S(1)}, f32[32,512]{1,0:T(8,128)S(1)}, u32[]{:S(2)}, u32[]{:S(2)}) collective-permute-start(f32[32,512]{1,0:T(8,128)S(1)} %constant_dynamic-slice_fusion), channel_id=1, source_target_pairs={{0,16},{1,17},{2,18},{3,19},{4,20},{5,21},{6,22},{7,23},{8,24},{9,... | collective-permute-start | bytes 196616 | tf_op jit(solution)/shard_map/ppermute | solution.py:106
  156.8 6.5 %collective-permute-start.5 = (f32[32,512]{1,0:T(8,128)S(1)}, f32[32,512]{1,0:T(8,128)S(1)}, u32[]{:S(2)}, u32[]{:S(2)}) collective-permute-start(f32[32,512]{1,0:T(8,128)S(1)} %dynamic-slice_add_fusion.4), channel_id=1, source_target_pairs={{0,16},{1,17},{2,18},{3,19},{4,20},{5,21},{6,22},{7,23},{8,24},{9,... | collective-permute-start | bytes 196616 | tf_op jit(solution)/shard_map/ppermute | solution.py:110
  163.4 7.2 %collective-permute-start.6 = (f32[64,512]{1,0:T(8,128)S(1)}, f32[64,512]{1,0:T(8,128)S(1)}, u32[]{:S(2)}, u32[]{:S(2)}) collective-permute-start(f32[64,512]{1,0:T(8,128)S(1)} %pad_maximum_fusion.3), channel_id=1, source_target_pairs={{0,4},{1,5},{2,6},{3,7},{4,0},{5,1},{6,2},{7,3},{8,12},{9,13},{10,... | collective-permute-start | bytes 393224 | tf_op jit(solution)/shard_map/ppermute | solution.py:110
  170.7 13.0 %collective-permute-start.7 = (f32[128,512]{1,0:T(8,128)S(1)}, f32[128,512]{1,0:T(8,128)S(1)}, u32[]{:S(2)}, u32[]{:S(2)}) collective-permute-start(f32[128,512]{1,0:T(8,128)S(1)} %pad_maximum_fusion.2), channel_id=1, source_target_pairs={{0,8},{1,9},{2,10},{3,11},{4,12},{5,13},{6,14},{7,15},{8,0},{9,1},... | collective-permute-start | bytes 786440 | tf_op jit(solution)/shard_map/ppermute | solution.py:110
  183.7 23.9 %collective-permute-start.8 = (f32[256,512]{1,0:T(8,128)S(1)}, f32[256,512]{1,0:T(8,128)S(1)}, u32[]{:S(2)}, u32[]{:S(2)}) collective-permute-start(f32[256,512]{1,0:T(8,128)S(1)} %pad_maximum_fusion.1), channel_id=1, source_target_pairs={{0,2},{1,3},{2,0},{3,1},{4,6},{5,7},{6,4},{7,5},{8,10},{9,11},{10,... | collective-permute-start | bytes 1572872 | tf_op jit(solution)/shard_map/ppermute | solution.py:110
  207.8 9.8 %collective-permute-start.9 = (f32[512,512]{1,0:T(8,128)S(1)}, f32[512,512]{1,0:T(8,128)S(1)}, u32[]{:S(2)}, u32[]{:S(2)}) collective-permute-start(f32[512,512]{1,0:T(8,128)S(1)} %pad_maximum_fusion), channel_id=1, source_target_pairs={{0,1},{1,0},{2,3},{3,2},{4,5},{5,4},{6,7},{7,6},{8,9},{9,8},{10,11... | collective-permute-start | bytes 3145736 | tf_op jit(solution)/shard_map/ppermute | solution.py:110
  283.9 4.7 %copy-start.2 = (f32[256,512]{1,0:T(8,128)}, f32[256,512]{1,0:T(8,128)S(1)}, u32[]{:S(2)}) copy-start(f32[256,512]{1,0:T(8,128)S(1)} %fusion.5) | copy-start | bytes 1572868
Sparse Core Ops, SparseCore 0:
  10.1 75.2 all-gather.1
  100.1 142.8 reduce-scatter.1

commit v9 on v8

--- a/solution.py
+++ b/solution.py
@@ -95,19 +95,27 @@
 
 def reduce_by_halving(x, axis, count):
     index = lax.axis_index(axis)
-    masks = [1 << k for k in range(count.bit_length() - 1)]
-    masks = masks[:2] + masks[3:4] + masks[2:3] + masks[4:]
+    core = index % 2
+    rounds = [(1, 1), (2, 8), (8, 2), (4, 16), (16, 4)]
     size = x.shape[0]
-    for mask in masks:
+
+    def partners(pair):
+        return [(i, i ^ pair[i % 2]) for i in range(count)]
+
+    def bit_of(pair):
+        mask = jnp.where(core == 0, pair[0], pair[1])
+        return (index // mask) % 2
+
+    for pair in rounds:
         half = size // 2
-        bit = (index // mask) % 2
+        bit = bit_of(pair)
         keep = lax.dynamic_slice_in_dim(x, bit * half, half, 0)
         send = lax.dynamic_slice_in_dim(x, (1 - bit) * half, half, 0)
-        x = keep + lax.ppermute(send, axis, [(i, i ^ mask) for i in range(count)])
+        x = keep + lax.ppermute(send, axis, partners(pair))
         size = half
-    for mask in reversed(masks):
-        bit = (index // mask) % 2
-        other = lax.ppermute(x, axis, [(i, i ^ mask) for i in range(count)])
+    for pair in reversed(rounds):
+        bit = bit_of(pair)
+        other = lax.ppermute(x, axis, partners(pair))
         low = jnp.where(bit == 0, x, other)
         high = jnp.where(bit == 0, other, x)
         x = jnp.concatenate([low, high], axis=0)

time: 296 us -> 291 us (0.983)
  waiting for transfers between devices: 139 us -> 129 us
  starting transfers between devices: 50 us -> 55.3 us
    ppermute x10, waiting for transfers between devices: 61.2 us -> 50.9 us  [the longest x5 32.8 us: reduce_by_halving(): other = lax.ppermute(x, axis, partners(pair))]
    ppermute x10, starting transfers between devices: 50 us -> 55.2 us  [the longest x5 28.3 us: reduce_by_halving(): other = lax.ppermute(x, axis, partners(pair))]
where the time goes in v9:
time: 291 us; the launch traced here: 290 us
  waiting for transfers between devices  129 us (44%)
  Pallas kernels  61.2 us (21%)
  starting transfers between devices  55.3 us (19%)
  between operations  15.3 us (5%)
  matrix products  15.2 us (5%)
  other arithmetic  10.6 us (4%)
  local copies, waits for them, and re-layouts  3.77 us (1%)
    all_gather x1, waiting for transfers between devices, shards(): gathered = lax.all_gather(jacobian, 'smp', axis=0, tiled=True)  77.4 us
    pallas_call x1, Pallas kernels, chol_and_inverse(): pl.pallas_call(functools.partial(_chol_kernel, n=n, b=block), out_shape=(...  61.2 us
    ppermute x5, waiting for transfers between devices, reduce_by_halving(): other = lax.ppermute(x, axis, partners(pair))  32.8 us
    ppermute x5, starting transfers between devices, reduce_by_halving(): other = lax.ppermute(x, axis, partners(pair))  28.3 us
    ppermute x5, starting transfers between devices, reduce_by_halving(): x = keep + lax.ppermute(send, axis, partners(pair))  26.9 us
    ppermute x5, waiting for transfers between devices, reduce_by_halving(): x = keep + lax.ppermute(send, axis, partners(pair))  18 us
    dot_general x1, matrix products, shards(): big = lax.dot_general(lhs, centered, contract, preferred_element_type=f32)  6.39 us
  transfers between devices with their start and end apart: 12, of which 11 were waited for; matrix products, arithmetic and copies ran while one was open for 4% of the time, Pallas kernels for 21%

profile of v9, /device:TPU:1, one launch (start us, length us, event | category | flops | bytes accessed | tf_op | source)
XLA Modules:
  0.0 290.4 jit_solution(6785040032093342389)
XLA Ops:
  7.2 0.0 all-gather.2.cloned.1.call-start
  7.2 0.7 all-gather.2.cloned.1.call-update
  7.9 0.0 reduce-scatter.2.cloned.1.call-start
  7.9 77.4 %all-gather.2.cloned.1.call-done = bf16[4096,512]{1,0:T(8,128)(2,1)} async-done(((bf16[256,512]{1,0:T(8,128)(2,1)}), bf16[4096,512]{1,0:T(8,128)(2,1)}) %all-gather.2.cloned.1.call-update) | async-done | bytes 4194320 | tf_op jit(solution)/shard_map/all_gather | solution.py:137
  85.3 0.0 copy-start
  85.3 3.0 %convert_reduce_fusion = f32[512]{0:T(512)S(1)} fusion(bf16[4096,512]{1,0:T(8,128)(2,1)} %all-gather.2.cloned.1.call-done), kind=kLoop, calls=%fused_computation.1 | loop fusion | flops 4193792 | bytes 4196352 | tf_op jit(solution)/shard_map/reduce_sum | solution.py:139
  88.3 0.5 copy-done
  88.8 2.8 multiply_reduce_fusion
  91.6 0.0 copy-start.1
  91.7 1.9 copy-done.1
  93.5 6.4 %fusion.1 = f32[768,4096]{1,0:T(8,128)} fusion(bf16[4096,512]{1,0:T(8,128)(2,1)S(1)} %get-tuple-element.5, bf16[512,512]{1,0:T(8,128)(2,1)S(1)} %slice.24, bf16[256,512]{1,0:T(8,128)(2,1)S(1)} %constant_dynamic-slice_fusion.5), kind=kOutput, calls=%fused_computation.11 | convolution fusion | flops 3222798336 | bytes 17563648 | tf_op jit(solution)/shard_map/dot_general | solution.py:155
  99.9 0.0 reduce-scatter.2.cloned.1.call-update
  100.0 0.6 broadcast_in_dim.44
  100.6 1.4 fusion.20
  102.0 1.7 fusion.18
  103.7 0.2 maximum_maximum_fusion
  103.9 0.1 constant_dynamic-slice_fusion.4
  104.0 11.5 %collective-permute-start = (f32[512,512]{1,0:T(8,128)S(1)}, f32[512,512]{1,0:T(8,128)}, u32[]{:S(2)}, u32[]{:S(2)}) collective-permute-start(f32[512,512]{1,0:T(8,128)S(1)} %constant_dynamic-slice_fusion.4), channel_id=1, source_target_pairs={{0,1},{1,0},{2,3},{3,2},{4,5},{5,4},{6,7},{7,6},{8,9},{9,8},{10,11... | collective-permute-start | bytes 3145736 | tf_op jit(solution)/shard_map/ppermute | solution.py:114
  115.5 2.3 collective-permute-done
  117.8 1.4 dynamic-slice_add_fusion
  119.3 3.1 %collective-permute-start.1 = (f32[256,512]{1,0:T(8,128)S(1)}, f32[256,512]{1,0:T(8,128)S(1)}, u32[]{:S(2)}, u32[]{:S(2)}) collective-permute-start(f32[256,512]{1,0:T(8,128)S(1)} %constant_dynamic-slice_fusion.3), channel_id=1, source_target_pairs={{0,2},{1,9},{2,0},{3,11},{4,6},{5,13},{6,4},{7,15},{8,10},{9,1},{1... | collective-permute-start | bytes 1572872 | tf_op jit(solution)/shard_map/ppermute | solution.py:114
  122.5 7.1 %collective-permute-done.1 = f32[256,512]{1,0:T(8,128)S(1)} collective-permute-done((f32[256,512]{1,0:T(8,128)S(1)}, f32[256,512]{1,0:T(8,128)S(1)}, u32[]{:S(2)}, u32[]{:S(2)}) %collective-permute-start.1) | collective-permute-done | bytes 524320 | tf_op jit(solution)/shard_map/ppermute | solution.py:114
  129.6 0.1 dynamic-slice_add_fusion.1
  129.7 3.1 %collective-permute-start.2 = (f32[128,512]{1,0:T(8,128)S(1)}, f32[128,512]{1,0:T(8,128)S(1)}, u32[]{:S(2)}, u32[]{:S(2)}) collective-permute-start(f32[128,512]{1,0:T(8,128)S(1)} %constant_dynamic-slice_fusion.2), channel_id=1, source_target_pairs={{0,8},{1,3},{2,10},{3,1},{4,12},{5,7},{6,14},{7,5},{8,0},{9,11},{1... | collective-permute-start | bytes 786440 | tf_op jit(solution)/shard_map/ppermute | solution.py:114
  132.9 4.2 %collective-permute-done.2 = f32[128,512]{1,0:T(8,128)S(1)} collective-permute-done((f32[128,512]{1,0:T(8,128)S(1)}, f32[128,512]{1,0:T(8,128)S(1)}, u32[]{:S(2)}, u32[]{:S(2)}) %collective-permute-start.2) | collective-permute-done | bytes 262176 | tf_op jit(solution)/shard_map/ppermute | solution.py:114
  137.2 4.6 %collective-permute-start.3 = (f32[64,512]{1,0:T(8,128)S(1)}, f32[64,512]{1,0:T(8,128)S(1)}, u32[]{:S(2)}, u32[]{:S(2)}) collective-permute-start(f32[64,512]{1,0:T(8,128)S(1)} %constant_dynamic-slice_fusion.1), channel_id=1, source_target_pairs={{0,4},{1,17},{2,6},{3,19},{4,0},{5,21},{6,2},{7,23},{8,12},{9,25},... | collective-permute-start | bytes 393224 | tf_op jit(solution)/shard_map/ppermute | solution.py:114
  141.8 2.5 collective-permute-done.3
  144.4 4.6 %collective-permute-start.4 = (f32[32,512]{1,0:T(8,128)S(1)}, f32[32,512]{1,0:T(8,128)S(1)}, u32[]{:S(2)}, u32[]{:S(2)}) collective-permute-start(f32[32,512]{1,0:T(8,128)S(1)} %constant_dynamic-slice_fusion), channel_id=1, source_target_pairs={{0,16},{1,5},{2,18},{3,7},{4,20},{5,1},{6,22},{7,3},{8,24},{9,13},... | collective-permute-start | bytes 196616 | tf_op jit(solution)/shard_map/ppermute | solution.py:114
  149.1 1.9 collective-permute-done.4
  150.9 4.6 %collective-permute-start.5 = (f32[32,512]{1,0:T(8,128)S(1)}, f32[32,512]{1,0:T(8,128)S(1)}, u32[]{:S(2)}, u32[]{:S(2)}) collective-permute-start(f32[32,512]{1,0:T(8,128)S(1)} %dynamic-slice_add_fusion.4), channel_id=1, source_target_pairs={{0,16},{1,5},{2,18},{3,7},{4,20},{5,1},{6,22},{7,3},{8,24},{9,13},... | collective-permute-start | bytes 196616 | tf_op jit(solution)/shard_map/ppermute | solution.py:118
  155.6 1.9 collective-permute-done.5
  157.5 4.6 %collective-permute-start.6 = (f32[64,512]{1,0:T(8,128)S(1)}, f32[64,512]{1,0:T(8,128)S(1)}, u32[]{:S(2)}, u32[]{:S(2)}) collective-permute-start(f32[64,512]{1,0:T(8,128)S(1)} %pad_maximum_fusion.3), channel_id=1, source_target_pairs={{0,4},{1,17},{2,6},{3,19},{4,0},{5,21},{6,2},{7,23},{8,12},{9,25},... | collective-permute-start | bytes 393224 | tf_op jit(solution)/shard_map/ppermute | solution.py:118
  162.1 2.6 collective-permute-done.6
  164.8 3.1 %collective-permute-start.7 = (f32[128,512]{1,0:T(8,128)S(1)}, f32[128,512]{1,0:T(8,128)S(1)}, u32[]{:S(2)}, u32[]{:S(2)}) collective-permute-start(f32[128,512]{1,0:T(8,128)S(1)} %pad_maximum_fusion.2), channel_id=1, source_target_pairs={{0,8},{1,3},{2,10},{3,1},{4,12},{5,7},{6,14},{7,5},{8,0},{9,11},{1... | collective-permute-start | bytes 786440 | tf_op jit(solution)/shard_map/ppermute | solution.py:118
  167.9 5.4 %collective-permute-done.7 = f32[128,512]{1,0:T(8,128)S(1)} collective-permute-done((f32[128,512]{1,0:T(8,128)S(1)}, f32[128,512]{1,0:T(8,128)S(1)}, u32[]{:S(2)}, u32[]{:S(2)}) %collective-permute-start.7) | collective-permute-done | bytes 262176 | tf_op jit(solution)/shard_map/ppermute | solution.py:118
  173.4 3.1 %collective-permute-start.8 = (f32[256,512]{1,0:T(8,128)S(1)}, f32[256,512]{1,0:T(8,128)S(1)}, u32[]{:S(2)}, u32[]{:S(2)}) collective-permute-start(f32[256,512]{1,0:T(8,128)S(1)} %pad_maximum_fusion.1), channel_id=1, source_target_pairs={{0,2},{1,9},{2,0},{3,11},{4,6},{5,13},{6,4},{7,15},{8,10},{9,1},{1... | collective-permute-start | bytes 1572872 | tf_op jit(solution)/shard_map/ppermute | solution.py:118
  176.5 20.9 %collective-permute-done.8 = f32[256,512]{1,0:T(8,128)S(1)} collective-permute-done((f32[256,512]{1,0:T(8,128)S(1)}, f32[256,512]{1,0:T(8,128)S(1)}, u32[]{:S(2)}, u32[]{:S(2)}) %collective-permute-start.8) | collective-permute-done | bytes 524320 | tf_op jit(solution)/shard_map/ppermute | solution.py:118
  197.4 0.1 broadcast_select_fusion.3
  197.5 0.1 pad_maximum_fusion
  197.6 12.9 %collective-permute-start.9 = (f32[512,512]{1,0:T(8,128)S(1)}, f32[512,512]{1,0:T(8,128)S(1)}, u32[]{:S(2)}, u32[]{:S(2)}) collective-permute-start(f32[512,512]{1,0:T(8,128)S(1)} %pad_maximum_fusion), channel_id=1, source_target_pairs={{0,1},{1,0},{2,3},{3,2},{4,5},{5,4},{6,7},{7,6},{8,9},{9,8},{10,11... | collective-permute-start | bytes 3145736 | tf_op jit(solution)/shard_map/ppermute | solution.py:118
  210.5 2.1 collective-permute-done.9
  212.6 0.2 broadcast_select_fusion.1
  212.8 0.2 maximum_multiply_fusion
  213.0 0.5 slice.26
  214.2 1.1 slice_add_fusion.a_ref
  215.3 61.2 %shard_map.30 = (f32[512,512]{1,0:T(8,128)}, f32[512,512]{1,0:T(8,128)}) custom-call(f32[512,512]{1,0:T(8,128)} %slice_add_fusion.a_ref), custom_call_target="tpu_custom_call" | custom-call | flops 268435456 | bytes 3145728 | tf_op jit(solution)/shard_map/pallas_call | solution.py:80
  276.5 2.4 fusion.5
  278.8 0.0 copy-start.2
  278.9 0.0 reduce-scatter.2.cloned.1.call-done
  278.9 1.2 broadcast_multiply_fusion
  280.1 2.2 fusion.7
  282.3 1.2 convolution_subtract_fusion
  283.5 0.0 copy-done.2
  (19 shorter events, 0.4 us)
Async XLA Ops:
  7.2 78.2 %all-gather.2.cloned.1.call-start = ((), (), s32[]{:S(2)}) async-start(), calls=%async_computation.1 | async-start | bytes 4456448 | tf_op jit(solution)/shard_map/all_gather | solution.py:137
  7.9 271.0 %reduce-scatter.2.cloned.1.call-start = ((), (), s32[]{:S(2)}) async-start(), calls=%async_computation.2 | async-start | bytes 12976128 | tf_op jit(solution)/shard_map/reduce_scatter | solution.py:156
  85.3 3.4 %copy-start = (bf16[4096,512]{1,0:T(8,128)(2,1)S(1)}, bf16[4096,512]{1,0:T(8,128)(2,1)}, u32[]{:S(2)}) copy-start(bf16[4096,512]{1,0:T(8,128)(2,1)} %all-gather.2.cloned.1.call-done) | copy-start | bytes 12582916
  91.6 1.9 copy-start.1
  104.0 13.9 %collective-permute-start = (f32[512,512]{1,0:T(8,128)S(1)}, f32[512,512]{1,0:T(8,128)}, u32[]{:S(2)}, u32[]{:S(2)}) collective-permute-start(f32[512,512]{1,0:T(8,128)S(1)} %constant_dynamic-slice_fusion.4), channel_id=1, source_target_pairs={{0,1},{1,0},{2,3},{3,2},{4,5},{5,4},{6,7},{7,6},{8,9},{9,8},{10,11... | collective-permute-start | bytes 3145736 | tf_op jit(solution)/shard_map/ppermute | solution.py:114
  119.3 10.2 %collective-permute-start.1 = (f32[256,512]{1,0:T(8,128)S(1)}, f32[256,512]{1,0:T(8,128)S(1)}, u32[]{:S(2)}, u32[]{:S(2)}) collective-permute-start(f32[256,512]{1,0:T(8,128)S(1)} %constant_dynamic-slice_fusion.3), channel_id=1, source_target_pairs={{0,2},{1,9},{2,0},{3,11},{4,6},{5,13},{6,4},{7,15},{8,10},{9,1},{1... | collective-permute-start | bytes 1572872 | tf_op jit(solution)/shard_map/ppermute | solution.py:114
  129.7 7.4 %collective-permute-start.2 = (f32[128,512]{1,0:T(8,128)S(1)}, f32[128,512]{1,0:T(8,128)S(1)}, u32[]{:S(2)}, u32[]{:S(2)}) collective-permute-start(f32[128,512]{1,0:T(8,128)S(1)} %constant_dynamic-slice_fusion.2), channel_id=1, source_target_pairs={{0,8},{1,3},{2,10},{3,1},{4,12},{5,7},{6,14},{7,5},{8,0},{9,11},{1... | collective-permute-start | bytes 786440 | tf_op jit(solution)/shard_map/ppermute | solution.py:114
  137.2 7.2 %collective-permute-start.3 = (f32[64,512]{1,0:T(8,128)S(1)}, f32[64,512]{1,0:T(8,128)S(1)}, u32[]{:S(2)}, u32[]{:S(2)}) collective-permute-start(f32[64,512]{1,0:T(8,128)S(1)} %constant_dynamic-slice_fusion.1), channel_id=1, source_target_pairs={{0,4},{1,17},{2,6},{3,19},{4,0},{5,21},{6,2},{7,23},{8,12},{9,25},... | collective-permute-start | bytes 393224 | tf_op jit(solution)/shard_map/ppermute | solution.py:114
  144.4 6.5 %collective-permute-start.4 = (f32[32,512]{1,0:T(8,128)S(1)}, f32[32,512]{1,0:T(8,128)S(1)}, u32[]{:S(2)}, u32[]{:S(2)}) collective-permute-start(f32[32,512]{1,0:T(8,128)S(1)} %constant_dynamic-slice_fusion), channel_id=1, source_target_pairs={{0,16},{1,5},{2,18},{3,7},{4,20},{5,1},{6,22},{7,3},{8,24},{9,13},... | collective-permute-start | bytes 196616 | tf_op jit(solution)/shard_map/ppermute | solution.py:114
  150.9 6.5 %collective-permute-start.5 = (f32[32,512]{1,0:T(8,128)S(1)}, f32[32,512]{1,0:T(8,128)S(1)}, u32[]{:S(2)}, u32[]{:S(2)}) collective-permute-start(f32[32,512]{1,0:T(8,128)S(1)} %dynamic-slice_add_fusion.4), channel_id=1, source_target_pairs={{0,16},{1,5},{2,18},{3,7},{4,20},{5,1},{6,22},{7,3},{8,24},{9,13},... | collective-permute-start | bytes 196616 | tf_op jit(solution)/shard_map/ppermute | solution.py:118
  157.5 7.2 %collective-permute-start.6 = (f32[64,512]{1,0:T(8,128)S(1)}, f32[64,512]{1,0:T(8,128)S(1)}, u32[]{:S(2)}, u32[]{:S(2)}) collective-permute-start(f32[64,512]{1,0:T(8,128)S(1)} %pad_maximum_fusion.3), channel_id=1, source_target_pairs={{0,4},{1,17},{2,6},{3,19},{4,0},{5,21},{6,2},{7,23},{8,12},{9,25},... | collective-permute-start | bytes 393224 | tf_op jit(solution)/shard_map/ppermute | solution.py:118
  164.8 8.5 %collective-permute-start.7 = (f32[128,512]{1,0:T(8,128)S(1)}, f32[128,512]{1,0:T(8,128)S(1)}, u32[]{:S(2)}, u32[]{:S(2)}) collective-permute-start(f32[128,512]{1,0:T(8,128)S(1)} %pad_maximum_fusion.2), channel_id=1, source_target_pairs={{0,8},{1,3},{2,10},{3,1},{4,12},{5,7},{6,14},{7,5},{8,0},{9,11},{1... | collective-permute-start | bytes 786440 | tf_op jit(solution)/shard_map/ppermute | solution.py:118
  173.4 24.0 %collective-permute-start.8 = (f32[256,512]{1,0:T(8,128)S(1)}, f32[256,512]{1,0:T(8,128)S(1)}, u32[]{:S(2)}, u32[]{:S(2)}) collective-permute-start(f32[256,512]{1,0:T(8,128)S(1)} %pad_maximum_fusion.1), channel_id=1, source_target_pairs={{0,2},{1,9},{2,0},{3,11},{4,6},{5,13},{6,4},{7,15},{8,10},{9,1},{1... | collective-permute-start | bytes 1572872 | tf_op jit(solution)/shard_map/ppermute | solution.py:118
  197.6 15.0 %collective-permute-start.9 = (f32[512,512]{1,0:T(8,128)S(1)}, f32[512,512]{1,0:T(8,128)S(1)}, u32[]{:S(2)}, u32[]{:S(2)}) collective-permute-start(f32[512,512]{1,0:T(8,128)S(1)} %pad_maximum_fusion), channel_id=1, source_target_pairs={{0,1},{1,0},{2,3},{3,2},{4,5},{5,4},{6,7},{7,6},{8,9},{9,8},{10,11... | collective-permute-start | bytes 3145736 | tf_op jit(solution)/shard_map/ppermute | solution.py:118
  278.8 4.7 %copy-start.2 = (f32[256,512]{1,0:T(8,128)}, f32[256,512]{1,0:T(8,128)S(1)}, u32[]{:S(2)}) copy-start(f32[256,512]{1,0:T(8,128)S(1)} %fusion.5) | copy-start | bytes 1572868
Sparse Core Ops, SparseCore 0:
  10.1 75.2 all-gather.1
  100.1 138.2 reduce-scatter.1

commit v10 on v9

--- a/solution.py
+++ b/solution.py
@@ -20,7 +20,9 @@
 def _chol_kernel(a_ref, l_ref, w_ref, s_ref, blk_a, blk_b, blk_lt, blk_w, *, n, b):
     nb = n // b
     f32 = jnp.float32
-    s_ref[...] = a_ref[...]
+    whole = a_ref[...]
+    lower = lax.broadcasted_iota(jnp.int32, (n, n), 0) >= lax.broadcasted_iota(jnp.int32, (n, n), 1)
+    s_ref[...] = jnp.where(lower, whole, jnp.transpose(whole))
     l_ref[...] = jnp.zeros((n, n), f32)
     w_ref[...] = jnp.zeros((n, n), f32)
     rows = lax.broadcasted_iota(jnp.int32, (b, b), 0)
@@ -147,8 +149,9 @@
     sq = centered.astype(f32)
     sumsq = jnp.sum(sq * sq)
 
-    fill = jnp.broadcast_to(sumsq, (row_count, PANEL))
-    panel_in = jnp.concatenate([main_t, square, fill], axis=0)
+    corner = (jnp.arange(PANEL)[:, None] == 0) & (jnp.arange(PANEL)[None, :] == PANEL - 1)
+    square = jnp.where(corner, sumsq, square)
+    panel_in = jnp.concatenate([main_t, square], axis=0)
     shared = reduce_by_halving(panel_in, "par", par_count) / param_total
 
     lhs = jnp.concatenate([mine, head], axis=0)
@@ -159,7 +162,7 @@
 
     panel_g = shared[:row_count]
     square_g = shared[row_count : row_count + PANEL]
-    trace_total = shared[row_count + PANEL, 0]
+    trace_total = shared[row_count, PANEL - 1]
     shift_value = shift_scale * trace_total / sample_total
 
     eye = jnp.arange(PANEL, dtype=jnp.int32)

time: 291 us -> 279 us (0.959)
  waiting for transfers between devices: 129 us -> 116 us
    ppermute x5, waiting for transfers between devices: 32.8 us -> 22.7 us  [reduce_by_halving(): other = lax.ppermute(x, axis, partners(pair))]
    ppermute x5, waiting for transfers between devices: 18 us -> 14.9 us  [reduce_by_halving(): x = keep + lax.ppermute(send, axis, partners(pair))]
  transfers between devices with their start and end apart: 12 -> 12, of which waited for: 11 -> 11; matrix products, arithmetic and copies ran while one was open for 4% -> 3% of each run, Pallas kernels for 21% -> 22%
where the time goes in v10:
time: 279 us; the launch traced here: 278 us
  waiting for transfers between devices  116 us (42%)
  Pallas kernels  61.4 us (22%)
  starting transfers between devices  57.1 us (20%)
  matrix products  15.9 us (6%)
  between operations  15.3 us (5%)
  other arithmetic  9.13 us (3%)
  local copies, waits for them, and re-layouts  3.08 us (1%)
    all_gather x1, waiting for transfers between devices, shards(): gathered = lax.all_gather(jacobian, 'smp', axis=0, tiled=True)  77.4 us
    pallas_call x1, Pallas kernels, chol_and_inverse(): pl.pallas_call(functools.partial(_chol_kernel, n=n, b=block), out_shape=(...  61.4 us
    ppermute x5, starting transfers between devices, reduce_by_halving(): other = lax.ppermute(x, axis, partners(pair))  30.1 us
    ppermute x5, starting transfers between devices, reduce_by_halving(): x = keep + lax.ppermute(send, axis, partners(pair))  26.9 us
    ppermute x5, waiting for transfers between devices, reduce_by_halving(): other = lax.ppermute(x, axis, partners(pair))  22.7 us
    ppermute x5, waiting for transfers between devices, reduce_by_halving(): x = keep + lax.ppermute(send, axis, partners(pair))  14.9 us
    dot_general x1, matrix products, shards(): big = lax.dot_general(lhs, centered, contract, preferred_element_type=f32)  6.41 us
  transfers between devices with their start and end apart: 12, of which 11 were waited for; matrix products, arithmetic and copies ran while one was open for 3% of the time, Pallas kernels for 22%

profile of v10, /device:TPU:1, one launch (start us, length us, event | category | flops | bytes accessed | tf_op | source)
XLA Modules:
  0.0 277.6 jit_solution(7149061382167654406)
XLA Ops:
  7.2 0.0 all-gather.2.cloned.1.call-start
  7.2 0.7 all-gather.2.cloned.1.call-update
  7.9 0.0 reduce-scatter.2.cloned.1.call-start
  7.9 77.4 %all-gather.2.cloned.1.call-done = bf16[4096,512]{1,0:T(8,128)(2,1)} async-done(((bf16[256,512]{1,0:T(8,128)(2,1)}), bf16[4096,512]{1,0:T(8,128)(2,1)}) %all-gather.2.cloned.1.call-update) | async-done | bytes 4194320 | tf_op jit(solution)/shard_map/all_gather | solution.py:139
  85.3 0.0 copy-start
  85.3 3.0 %convert_reduce_fusion = f32[512]{0:T(512)S(1)} fusion(bf16[4096,512]{1,0:T(8,128)(2,1)} %all-gather.2.cloned.1.call-done), kind=kLoop, calls=%fused_computation.1 | loop fusion | flops 4193792 | bytes 4196352 | tf_op jit(solution)/shard_map/reduce_sum | solution.py:141
  88.3 0.5 copy-done
  88.8 2.8 %multiply_reduce_fusion = (f32[]{:T(128)}, bf16[4096,512]{1,0:T(8,128)(2,1)S(1)}) fusion(f32[512]{0:T(512)S(1)} %broadcast_multiply_fusion.1, bf16[4096,512]{1,0:T(8,128)(2,1)S(1)} %copy-done), kind=kLoop, calls=%fused_computation.3 | loop fusion | flops 12582911 | bytes 8390660 | tf_op jit(solution)/shard_map/reduce_sum | solution.py:150
  91.6 0.0 copy-start.1
  91.7 1.9 copy-done.1
  93.5 6.4 %fusion.4 = f32[768,4096]{1,0:T(8,128)} fusion(bf16[4096,512]{1,0:T(8,128)(2,1)S(1)} %get-tuple-element.5, bf16[512,512]{1,0:T(8,128)(2,1)S(1)} %slice.24, bf16[256,512]{1,0:T(8,128)(2,1)S(1)} %constant_dynamic-slice_fusion.4), kind=kOutput, calls=%fused_computation.17 | convolution fusion | flops 3222798336 | bytes 17563648 | tf_op jit(solution)/shard_map/dot_general | solution.py:158
  99.9 0.0 reduce-scatter.2.cloned.1.call-update
  100.0 1.4 fusion.22
  101.4 2.3 convolution_select_fusion
  103.7 0.2 fusion.1
  103.9 11.5 %collective-permute-start = (f32[384,512]{1,0:T(8,128)S(1)}, f32[384,512]{1,0:T(8,128)S(1)}, u32[]{:S(2)}, u32[]{:S(2)}) collective-permute-start(f32[384,512]{1,0:T(8,128)S(1)} %fusion.1), channel_id=1, source_target_pairs={{0,1},{1,0},{2,3},{3,2},{4,5},{5,4},{6,7},{7,6},{8,9},{9,8},{10,11... | collective-permute-start | bytes 2359304 | tf_op jit(solution)/shard_map/ppermute | solution.py:116
  115.4 1.8 collective-permute-done
  117.2 0.2 fusion.3
  117.5 3.1 %collective-permute-start.1 = (f32[192,512]{1,0:T(8,128)S(1)}, f32[192,512]{1,0:T(8,128)S(1)}, u32[]{:S(2)}, u32[]{:S(2)}) collective-permute-start(f32[192,512]{1,0:T(8,128)S(1)} %constant_dynamic-slice_fusion.3), channel_id=1, source_target_pairs={{0,2},{1,9},{2,0},{3,11},{4,6},{5,13},{6,4},{7,15},{8,10},{9,1},{1... | collective-permute-start | bytes 1179656 | tf_op jit(solution)/shard_map/ppermute | solution.py:116
  120.6 5.7 %collective-permute-done.1 = f32[192,512]{1,0:T(8,128)S(1)} collective-permute-done((f32[192,512]{1,0:T(8,128)S(1)}, f32[192,512]{1,0:T(8,128)S(1)}, u32[]{:S(2)}, u32[]{:S(2)}) %collective-permute-start.1) | collective-permute-done | bytes 393248 | tf_op jit(solution)/shard_map/ppermute | solution.py:116
  126.3 0.1 dynamic-slice_add_fusion
  126.4 3.1 %collective-permute-start.2 = (f32[96,512]{1,0:T(8,128)S(1)}, f32[96,512]{1,0:T(8,128)S(1)}, u32[]{:S(2)}, u32[]{:S(2)}) collective-permute-start(f32[96,512]{1,0:T(8,128)S(1)} %constant_dynamic-slice_fusion.2), channel_id=1, source_target_pairs={{0,8},{1,3},{2,10},{3,1},{4,12},{5,7},{6,14},{7,5},{8,0},{9,11},{1... | collective-permute-start | bytes 589832 | tf_op jit(solution)/shard_map/ppermute | solution.py:116
  129.6 3.5 %collective-permute-done.2 = f32[96,512]{1,0:T(8,128)S(1)} collective-permute-done((f32[96,512]{1,0:T(8,128)S(1)}, f32[96,512]{1,0:T(8,128)S(1)}, u32[]{:S(2)}, u32[]{:S(2)}) %collective-permute-start.2) | collective-permute-done | bytes 196640 | tf_op jit(solution)/shard_map/ppermute | solution.py:116
  133.2 4.6 %collective-permute-start.3 = (f32[48,512]{1,0:T(8,128)S(1)}, f32[48,512]{1,0:T(8,128)S(1)}, u32[]{:S(2)}, u32[]{:S(2)}) collective-permute-start(f32[48,512]{1,0:T(8,128)S(1)} %constant_dynamic-slice_fusion.1), channel_id=1, source_target_pairs={{0,4},{1,17},{2,6},{3,19},{4,0},{5,21},{6,2},{7,23},{8,12},{9,25},... | collective-permute-start | bytes 294920 | tf_op jit(solution)/shard_map/ppermute | solution.py:116
  137.9 2.2 collective-permute-done.3
  140.1 4.6 %collective-permute-start.4 = (f32[24,512]{1,0:T(8,128)S(1)}, f32[24,512]{1,0:T(8,128)S(1)}, u32[]{:S(2)}, u32[]{:S(2)}) collective-permute-start(f32[24,512]{1,0:T(8,128)S(1)} %constant_dynamic-slice_fusion), channel_id=1, source_target_pairs={{0,16},{1,5},{2,18},{3,7},{4,20},{5,1},{6,22},{7,3},{8,24},{9,13},... | collective-permute-start | bytes 147464 | tf_op jit(solution)/shard_map/ppermute | solution.py:116
  144.7 1.7 collective-permute-done.4
  146.4 4.6 %collective-permute-start.5 = (f32[24,512]{1,0:T(8,128)S(1)}, f32[24,512]{1,0:T(8,128)S(1)}, u32[]{:S(2)}, u32[]{:S(2)}) collective-permute-start(f32[24,512]{1,0:T(8,128)S(1)} %dynamic-slice_add_fusion.3), channel_id=1, source_target_pairs={{0,16},{1,5},{2,18},{3,7},{4,20},{5,1},{6,22},{7,3},{8,24},{9,13},... | collective-permute-start | bytes 147464 | tf_op jit(solution)/shard_map/ppermute | solution.py:120
  151.1 1.7 collective-permute-done.5
  152.8 4.6 %collective-permute-start.6 = (f32[48,512]{1,0:T(8,128)S(1)}, f32[48,512]{1,0:T(8,128)S(1)}, u32[]{:S(2)}, u32[]{:S(2)}) collective-permute-start(f32[48,512]{1,0:T(8,128)S(1)} %pad_maximum_fusion.3), channel_id=1, source_target_pairs={{0,4},{1,17},{2,6},{3,19},{4,0},{5,21},{6,2},{7,23},{8,12},{9,25},... | collective-permute-start | bytes 294920 | tf_op jit(solution)/shard_map/ppermute | solution.py:120
  157.4 2.2 collective-permute-done.6
  159.7 3.1 %collective-permute-start.7 = (f32[96,512]{1,0:T(8,128)S(1)}, f32[96,512]{1,0:T(8,128)S(1)}, u32[]{:S(2)}, u32[]{:S(2)}) collective-permute-start(f32[96,512]{1,0:T(8,128)S(1)} %pad_maximum_fusion.2), channel_id=1, source_target_pairs={{0,8},{1,3},{2,10},{3,1},{4,12},{5,7},{6,14},{7,5},{8,0},{9,11},{1... | collective-permute-start | bytes 589832 | tf_op jit(solution)/shard_map/ppermute | solution.py:120
  162.8 4.3 %collective-permute-done.7 = f32[96,512]{1,0:T(8,128)S(1)} collective-permute-done((f32[96,512]{1,0:T(8,128)S(1)}, f32[96,512]{1,0:T(8,128)S(1)}, u32[]{:S(2)}, u32[]{:S(2)}) %collective-permute-start.7) | collective-permute-done | bytes 196640 | tf_op jit(solution)/shard_map/ppermute | solution.py:120
  167.2 3.1 %collective-permute-start.8 = (f32[192,512]{1,0:T(8,128)S(1)}, f32[192,512]{1,0:T(8,128)S(1)}, u32[]{:S(2)}, u32[]{:S(2)}) collective-permute-start(f32[192,512]{1,0:T(8,128)S(1)} %pad_maximum_fusion.1), channel_id=1, source_target_pairs={{0,2},{1,9},{2,0},{3,11},{4,6},{5,13},{6,4},{7,15},{8,10},{9,1},{1... | collective-permute-start | bytes 1179656 | tf_op jit(solution)/shard_map/ppermute | solution.py:120
  170.3 12.7 %collective-permute-done.8 = f32[192,512]{1,0:T(8,128)S(1)} collective-permute-done((f32[192,512]{1,0:T(8,128)S(1)}, f32[192,512]{1,0:T(8,128)S(1)}, u32[]{:S(2)}, u32[]{:S(2)}) %collective-permute-start.8) | collective-permute-done | bytes 393248 | tf_op jit(solution)/shard_map/ppermute | solution.py:120
  183.1 0.1 broadcast_select_fusion.3
  183.2 0.1 pad_maximum_fusion
  183.2 14.7 %collective-permute-start.9 = (f32[384,512]{1,0:T(8,128)S(1)}, f32[384,512]{1,0:T(8,128)S(1)}, u32[]{:S(2)}, u32[]{:S(2)}) collective-permute-start(f32[384,512]{1,0:T(8,128)S(1)} %pad_maximum_fusion), channel_id=1, source_target_pairs={{0,1},{1,0},{2,3},{3,2},{4,5},{5,4},{6,7},{7,6},{8,9},{9,8},{10,11... | collective-permute-start | bytes 2359304 | tf_op jit(solution)/shard_map/ppermute | solution.py:120
  198.0 1.7 collective-permute-done.9
  199.6 0.2 broadcast_select_fusion.1
  199.8 0.2 maximum_multiply_fusion
  200.0 0.6 slice.26
  201.2 1.1 slice_add_fusion.a_ref
  202.3 61.4 %shard_map.30 = (f32[512,512]{1,0:T(8,128)}, f32[512,512]{1,0:T(8,128)}) custom-call(f32[512,512]{1,0:T(8,128)} %slice_add_fusion.a_ref), custom_call_target="tpu_custom_call" | custom-call | flops 268435456 | bytes 3145728 | tf_op jit(solution)/shard_map/pallas_call | solution.py:82
  263.7 2.4 fusion.8
  266.0 0.0 copy-start.2
  266.0 0.0 reduce-scatter.2.cloned.1.call-done
  266.1 1.2 broadcast_multiply_fusion
  267.3 2.2 fusion.10
  269.5 1.2 convolution_subtract_fusion
  270.7 0.0 copy-done.2
  (19 shorter events, 0.3 us)
Async XLA Ops:
  7.2 78.2 %all-gather.2.cloned.1.call-start = ((), (), s32[]{:S(2)}) async-start(), calls=%async_computation.1 | async-start | bytes 4456448 | tf_op jit(solution)/shard_map/all_gather | solution.py:139
  7.9 258.2 %reduce-scatter.2.cloned.1.call-start = ((), (), s32[]{:S(2)}) async-start(), calls=%async_computation.2 | async-start | bytes 12976128 | tf_op jit(solution)/shard_map/reduce_scatter | solution.py:159
  85.3 3.4 %copy-start = (bf16[4096,512]{1,0:T(8,128)(2,1)S(1)}, bf16[4096,512]{1,0:T(8,128)(2,1)}, u32[]{:S(2)}) copy-start(bf16[4096,512]{1,0:T(8,128)(2,1)} %all-gather.2.cloned.1.call-done) | copy-start | bytes 12582916
  91.6 1.9 copy-start.1
  103.9 13.4 %collective-permute-start = (f32[384,512]{1,0:T(8,128)S(1)}, f32[384,512]{1,0:T(8,128)S(1)}, u32[]{:S(2)}, u32[]{:S(2)}) collective-permute-start(f32[384,512]{1,0:T(8,128)S(1)} %fusion.1), channel_id=1, source_target_pairs={{0,1},{1,0},{2,3},{3,2},{4,5},{5,4},{6,7},{7,6},{8,9},{9,8},{10,11... | collective-permute-start | bytes 2359304 | tf_op jit(solution)/shard_map/ppermute | solution.py:116
  117.5 8.8 %collective-permute-start.1 = (f32[192,512]{1,0:T(8,128)S(1)}, f32[192,512]{1,0:T(8,128)S(1)}, u32[]{:S(2)}, u32[]{:S(2)}) collective-permute-start(f32[192,512]{1,0:T(8,128)S(1)} %constant_dynamic-slice_fusion.3), channel_id=1, source_target_pairs={{0,2},{1,9},{2,0},{3,11},{4,6},{5,13},{6,4},{7,15},{8,10},{9,1},{1... | collective-permute-start | bytes 1179656 | tf_op jit(solution)/shard_map/ppermute | solution.py:116
  126.4 6.7 %collective-permute-start.2 = (f32[96,512]{1,0:T(8,128)S(1)}, f32[96,512]{1,0:T(8,128)S(1)}, u32[]{:S(2)}, u32[]{:S(2)}) collective-permute-start(f32[96,512]{1,0:T(8,128)S(1)} %constant_dynamic-slice_fusion.2), channel_id=1, source_target_pairs={{0,8},{1,3},{2,10},{3,1},{4,12},{5,7},{6,14},{7,5},{8,0},{9,11},{1... | collective-permute-start | bytes 589832 | tf_op jit(solution)/shard_map/ppermute | solution.py:116
  133.2 6.9 %collective-permute-start.3 = (f32[48,512]{1,0:T(8,128)S(1)}, f32[48,512]{1,0:T(8,128)S(1)}, u32[]{:S(2)}, u32[]{:S(2)}) collective-permute-start(f32[48,512]{1,0:T(8,128)S(1)} %constant_dynamic-slice_fusion.1), channel_id=1, source_target_pairs={{0,4},{1,17},{2,6},{3,19},{4,0},{5,21},{6,2},{7,23},{8,12},{9,25},... | collective-permute-start | bytes 294920 | tf_op jit(solution)/shard_map/ppermute | solution.py:116
  140.1 6.3 %collective-permute-start.4 = (f32[24,512]{1,0:T(8,128)S(1)}, f32[24,512]{1,0:T(8,128)S(1)}, u32[]{:S(2)}, u32[]{:S(2)}) collective-permute-start(f32[24,512]{1,0:T(8,128)S(1)} %constant_dynamic-slice_fusion), channel_id=1, source_target_pairs={{0,16},{1,5},{2,18},{3,7},{4,20},{5,1},{6,22},{7,3},{8,24},{9,13},... | collective-permute-start | bytes 147464 | tf_op jit(solution)/shard_map/ppermute | solution.py:116
  146.4 6.3 %collective-permute-start.5 = (f32[24,512]{1,0:T(8,128)S(1)}, f32[24,512]{1,0:T(8,128)S(1)}, u32[]{:S(2)}, u32[]{:S(2)}) collective-permute-start(f32[24,512]{1,0:T(8,128)S(1)} %dynamic-slice_add_fusion.3), channel_id=1, source_target_pairs={{0,16},{1,5},{2,18},{3,7},{4,20},{5,1},{6,22},{7,3},{8,24},{9,13},... | collective-permute-start | bytes 147464 | tf_op jit(solution)/shard_map/ppermute | solution.py:120
  152.8 6.9 %collective-permute-start.6 = (f32[48,512]{1,0:T(8,128)S(1)}, f32[48,512]{1,0:T(8,128)S(1)}, u32[]{:S(2)}, u32[]{:S(2)}) collective-permute-start(f32[48,512]{1,0:T(8,128)S(1)} %pad_maximum_fusion.3), channel_id=1, source_target_pairs={{0,4},{1,17},{2,6},{3,19},{4,0},{5,21},{6,2},{7,23},{8,12},{9,25},... | collective-permute-start | bytes 294920 | tf_op jit(solution)/shard_map/ppermute | solution.py:120
  159.7 7.5 %collective-permute-start.7 = (f32[96,512]{1,0:T(8,128)S(1)}, f32[96,512]{1,0:T(8,128)S(1)}, u32[]{:S(2)}, u32[]{:S(2)}) collective-permute-start(f32[96,512]{1,0:T(8,128)S(1)} %pad_maximum_fusion.2), channel_id=1, source_target_pairs={{0,8},{1,3},{2,10},{3,1},{4,12},{5,7},{6,14},{7,5},{8,0},{9,11},{1... | collective-permute-start | bytes 589832 | tf_op jit(solution)/shard_map/ppermute | solution.py:120
  167.2 15.8 %collective-permute-start.8 = (f32[192,512]{1,0:T(8,128)S(1)}, f32[192,512]{1,0:T(8,128)S(1)}, u32[]{:S(2)}, u32[]{:S(2)}) collective-permute-start(f32[192,512]{1,0:T(8,128)S(1)} %pad_maximum_fusion.1), channel_id=1, source_target_pairs={{0,2},{1,9},{2,0},{3,11},{4,6},{5,13},{6,4},{7,15},{8,10},{9,1},{1... | collective-permute-start | bytes 1179656 | tf_op jit(solution)/shard_map/ppermute | solution.py:120
  183.2 16.4 %collective-permute-start.9 = (f32[384,512]{1,0:T(8,128)S(1)}, f32[384,512]{1,0:T(8,128)S(1)}, u32[]{:S(2)}, u32[]{:S(2)}) collective-permute-start(f32[384,512]{1,0:T(8,128)S(1)} %pad_maximum_fusion), channel_id=1, source_target_pairs={{0,1},{1,0},{2,3},{3,2},{4,5},{5,4},{6,7},{7,6},{8,9},{9,8},{10,11... | collective-permute-start | bytes 2359304 | tf_op jit(solution)/shard_map/ppermute | solution.py:120
  266.0 4.7 %copy-start.2 = (f32[256,512]{1,0:T(8,128)}, f32[256,512]{1,0:T(8,128)S(1)}, u32[]{:S(2)}) copy-start(f32[256,512]{1,0:T(8,128)S(1)} %fusion.8) | copy-start | bytes 1572868
Sparse Core Ops, SparseCore 0:
  10.1 75.2 all-gather.1
  100.1 135.8 reduce-scatter.1

commit v11 on v10

--- a/solution.py
+++ b/solution.py
@@ -98,7 +98,8 @@
 def reduce_by_halving(x, axis, count):
     index = lax.axis_index(axis)
     core = index % 2
-    rounds = [(1, 1), (2, 8), (8, 2), (4, 16), (16, 4)]
+    halving = [(1, 1), (2, 8)]
+    doubling = [(8, 2), (4, 16), (16, 4)]
     size = x.shape[0]
 
     def partners(pair):
@@ -108,14 +109,16 @@
         mask = jnp.where(core == 0, pair[0], pair[1])
         return (index // mask) % 2
 
-    for pair in rounds:
+    for pair in halving:
         half = size // 2
         bit = bit_of(pair)
         keep = lax.dynamic_slice_in_dim(x, bit * half, half, 0)
         send = lax.dynamic_slice_in_dim(x, (1 - bit) * half, half, 0)
         x = keep + lax.ppermute(send, axis, partners(pair))
         size = half
-    for pair in reversed(rounds):
+    for pair in doubling:
+        x = x + lax.ppermute(x, axis, partners(pair))
+    for pair in reversed(halving):
         bit = bit_of(pair)
         other = lax.ppermute(x, axis, partners(pair))
         low = jnp.where(bit == 0, x, other)

time: 279 us -> 252 us (0.903)
  starting transfers between devices: 57.1 us -> 36.5 us
  waiting for transfers between devices: 116 us -> 110 us
    ppermute x5 -> x2, starting transfers between devices: 30.1 us -> 9.81 us  [reduce_by_halving(): other = lax.ppermute(x, axis, partners(pair))]
    ppermute x0 -> x3, waiting for transfers between devices: none -> 17.4 us  [reduce_by_halving(): x = x + lax.ppermute(x, axis, partners(pair))]
    ppermute x5 -> x2, waiting for transfers between devices: 22.7 us -> 7.41 us  [reduce_by_halving(): other = lax.ppermute(x, axis, partners(pair))]
    ppermute x5 -> x2, starting transfers between devices: 26.9 us -> 14.5 us  [reduce_by_halving(): x = keep + lax.ppermute(send, axis, partners(pair))]
    ppermute x0 -> x3, starting transfers between devices: none -> 12.1 us  [reduce_by_halving(): x = x + lax.ppermute(x, axis, partners(pair))]
    ppermute x5 -> x2, waiting for transfers between devices: 14.9 us -> 7.55 us  [reduce_by_halving(): x = keep + lax.ppermute(send, axis, partners(pair))]
  transfers between devices with their start and end apart: 12 -> 9, of which waited for: 11 -> 8; matrix products, arithmetic and copies ran while one was open for 3% -> 4% of each run, Pallas kernels for 22% -> 24%
where the time goes in v11:
time: 252 us; the launch traced here: 251 us
  waiting for transfers between devices  110 us (44%)
  Pallas kernels  61.4 us (24%)
  starting transfers between devices  36.5 us (14%)
  matrix products  15.9 us (6%)
  between operations  15 us (6%)
  other arithmetic  9.14 us (4%)
  local copies, waits for them, and re-layouts  3.02 us (1%)
    all_gather x1, waiting for transfers between devices, shards(): gathered = lax.all_gather(jacobian, 'smp', axis=0, tiled=True)  77.4 us
    pallas_call x1, Pallas kernels, chol_and_inverse(): pl.pallas_call(functools.partial(_chol_kernel, n=n, b=block), out_shape=(...  61.4 us
    ppermute x3, waiting for transfers between devices, reduce_by_halving(): x = x + lax.ppermute(x, axis, partners(pair))  17.4 us
    ppermute x2, starting transfers between devices, reduce_by_halving(): x = keep + lax.ppermute(send, axis, partners(pair))  14.5 us
    ppermute x3, starting transfers between devices, reduce_by_halving(): x = x + lax.ppermute(x, axis, partners(pair))  12.1 us
    ppermute x2, starting transfers between devices, reduce_by_halving(): other = lax.ppermute(x, axis, partners(pair))  9.81 us
    ppermute x2, waiting for transfers between devices, reduce_by_halving(): x = keep + lax.ppermute(send, axis, partners(pair))  7.55 us
    ppermute x2, waiting for transfers between devices, reduce_by_halving(): other = lax.ppermute(x, axis, partners(pair))  7.41 us
  transfers between devices with their start and end apart: 9, of which 8 were waited for; matrix products, arithmetic and copies ran while one was open for 4% of the time, Pallas kernels for 24%

profile of v11, /device:TPU:1, one launch (start us, length us, event | category | flops | bytes accessed | tf_op | source)
XLA Modules:
  0.0 251.4 jit_solution(11884530132837293413)
XLA Ops:
  7.2 0.0 all-gather.2.cloned.1.call-start
  7.2 0.7 all-gather.2.cloned.1.call-update
  7.9 0.0 reduce-scatter.2.cloned.1.call-start
  7.9 77.4 %all-gather.2.cloned.1.call-done = bf16[4096,512]{1,0:T(8,128)(2,1)} async-done(((bf16[256,512]{1,0:T(8,128)(2,1)}), bf16[4096,512]{1,0:T(8,128)(2,1)}) %all-gather.2.cloned.1.call-update) | async-done | bytes 4194320 | tf_op jit(solution)/shard_map/all_gather | solution.py:142
  85.3 0.0 copy-start
  85.3 3.0 %convert_reduce_fusion = f32[512]{0:T(512)S(1)} fusion(bf16[4096,512]{1,0:T(8,128)(2,1)} %all-gather.2.cloned.1.call-done), kind=kLoop, calls=%fused_computation.1 | loop fusion | flops 4193792 | bytes 4196352 | tf_op jit(solution)/shard_map/reduce_sum | solution.py:144
  88.3 0.5 copy-done
  88.8 2.8 %multiply_reduce_fusion = (f32[]{:T(128)}, bf16[4096,512]{1,0:T(8,128)(2,1)S(1)}) fusion(f32[512]{0:T(512)S(1)} %broadcast_multiply_fusion.1, bf16[4096,512]{1,0:T(8,128)(2,1)S(1)} %copy-done), kind=kLoop, calls=%fused_computation.3 | loop fusion | flops 12582911 | bytes 8390660 | tf_op jit(solution)/shard_map/reduce_sum | solution.py:153
  91.6 0.0 copy-start.1
  91.7 1.8 copy-done.1
  93.5 6.4 %fusion.4 = f32[768,4096]{1,0:T(8,128)} fusion(bf16[4096,512]{1,0:T(8,128)(2,1)S(1)} %get-tuple-element.5, bf16[512,512]{1,0:T(8,128)(2,1)S(1)} %slice.24, bf16[256,512]{1,0:T(8,128)(2,1)S(1)} %constant_dynamic-slice_fusion.1), kind=kOutput, calls=%fused_computation.17 | convolution fusion | flops 3222798336 | bytes 17563648 | tf_op jit(solution)/shard_map/dot_general | solution.py:161
  99.9 0.0 reduce-scatter.2.cloned.1.call-update
  100.0 1.4 fusion.22
  101.3 2.4 convolution_select_fusion
  103.7 0.2 fusion.1
  103.9 11.5 %collective-permute-start = (f32[384,512]{1,0:T(8,128)S(1)}, f32[384,512]{1,0:T(8,128)S(1)}, u32[]{:S(2)}, u32[]{:S(2)}) collective-permute-start(f32[384,512]{1,0:T(8,128)S(1)} %fusion.1), channel_id=1, source_target_pairs={{0,1},{1,0},{2,3},{3,2},{4,5},{5,4},{6,7},{7,6},{8,9},{9,8},{10,11... | collective-permute-start | bytes 2359304 | tf_op jit(solution)/shard_map/ppermute | solution.py:117
  115.4 1.8 collective-permute-done
  117.2 0.2 fusion.3
  117.5 3.1 %collective-permute-start.1 = (f32[192,512]{1,0:T(8,128)S(1)}, f32[192,512]{1,0:T(8,128)S(1)}, u32[]{:S(2)}, u32[]{:S(2)}) collective-permute-start(f32[192,512]{1,0:T(8,128)S(1)} %constant_dynamic-slice_fusion), channel_id=1, source_target_pairs={{0,2},{1,9},{2,0},{3,11},{4,6},{5,13},{6,4},{7,15},{8,10},{9,1},{1... | collective-permute-start | bytes 1179656 | tf_op jit(solution)/shard_map/ppermute | solution.py:117
  120.6 5.7 %collective-permute-done.1 = f32[192,512]{1,0:T(8,128)S(1)} collective-permute-done((f32[192,512]{1,0:T(8,128)S(1)}, f32[192,512]{1,0:T(8,128)S(1)}, u32[]{:S(2)}, u32[]{:S(2)}) %collective-permute-start.1) | collective-permute-done | bytes 393248 | tf_op jit(solution)/shard_map/ppermute | solution.py:117
  126.3 0.1 dynamic-slice_add_fusion
  126.4 3.1 %collective-permute-start.2 = (f32[192,512]{1,0:T(8,128)S(1)}, f32[192,512]{1,0:T(8,128)S(1)}, u32[]{:S(2)}, u32[]{:S(2)}) collective-permute-start(f32[192,512]{1,0:T(8,128)S(1)} %dynamic-slice_add_fusion), channel_id=1, source_target_pairs={{0,8},{1,3},{2,10},{3,1},{4,12},{5,7},{6,14},{7,5},{8,0},{9,11},{1... | collective-permute-start | bytes 1179656 | tf_op jit(solution)/shard_map/ppermute | solution.py:120
  129.5 5.7 %collective-permute-done.2 = f32[192,512]{1,0:T(8,128)S(1)} collective-permute-done((f32[192,512]{1,0:T(8,128)S(1)}, f32[192,512]{1,0:T(8,128)S(1)}, u32[]{:S(2)}, u32[]{:S(2)}) %collective-permute-start.2) | collective-permute-done | bytes 393248 | tf_op jit(solution)/shard_map/ppermute | solution.py:120
  135.2 0.1 add.85
  135.2 4.6 %collective-permute-start.3 = (f32[192,512]{1,0:T(8,128)S(1)}, f32[192,512]{1,0:T(8,128)S(1)}, u32[]{:S(2)}, u32[]{:S(2)}) collective-permute-start(f32[192,512]{1,0:T(8,128)S(1)} %add.85), channel_id=1, source_target_pairs={{0,4},{1,17},{2,6},{3,19},{4,0},{5,21},{6,2},{7,23},{8,12},{9,25},... | collective-permute-start | bytes 1179656 | tf_op jit(solution)/shard_map/ppermute | solution.py:120
  139.9 5.7 %collective-permute-done.3 = f32[192,512]{1,0:T(8,128)S(1)} collective-permute-done((f32[192,512]{1,0:T(8,128)S(1)}, f32[192,512]{1,0:T(8,128)S(1)}, u32[]{:S(2)}, u32[]{:S(2)}) %collective-permute-start.3) | collective-permute-done | bytes 393248 | tf_op jit(solution)/shard_map/ppermute | solution.py:120
  145.6 0.1 add.86
  145.6 4.3 %collective-permute-start.4 = (f32[192,512]{1,0:T(8,128)S(1)}, f32[192,512]{1,0:T(8,128)S(1)}, u32[]{:S(2)}, u32[]{:S(2)}) collective-permute-start(f32[192,512]{1,0:T(8,128)S(1)} %add.86), channel_id=1, source_target_pairs={{0,16},{1,5},{2,18},{3,7},{4,20},{5,1},{6,22},{7,3},{8,24},{9,13},... | collective-permute-start | bytes 1179656 | tf_op jit(solution)/shard_map/ppermute | solution.py:120
  150.0 6.0 %collective-permute-done.4 = f32[192,512]{1,0:T(8,128)S(1)} collective-permute-done((f32[192,512]{1,0:T(8,128)S(1)}, f32[192,512]{1,0:T(8,128)S(1)}, u32[]{:S(2)}, u32[]{:S(2)}) %collective-permute-start.4) | collective-permute-done | bytes 393248 | tf_op jit(solution)/shard_map/ppermute | solution.py:120
  155.9 0.1 add.87
  156.0 2.8 %collective-permute-start.5 = (f32[192,512]{1,0:T(8,128)S(1)}, f32[192,512]{1,0:T(8,128)S(1)}, u32[]{:S(2)}, u32[]{:S(2)}) collective-permute-start(f32[192,512]{1,0:T(8,128)S(1)} %add.87), channel_id=1, source_target_pairs={{0,2},{1,9},{2,0},{3,11},{4,6},{5,13},{6,4},{7,15},{8,10},{9,1},{1... | collective-permute-start | bytes 1179656 | tf_op jit(solution)/shard_map/ppermute | solution.py:123
  158.8 5.7 %collective-permute-done.5 = f32[192,512]{1,0:T(8,128)S(1)} collective-permute-done((f32[192,512]{1,0:T(8,128)S(1)}, f32[192,512]{1,0:T(8,128)S(1)}, u32[]{:S(2)}, u32[]{:S(2)}) %collective-permute-start.5) | collective-permute-done | bytes 393248 | tf_op jit(solution)/shard_map/ppermute | solution.py:123
  164.5 0.1 broadcast_select_fusion.3
  164.6 0.1 pad_maximum_fusion
  164.7 7.0 %collective-permute-start.6 = (f32[384,512]{1,0:T(8,128)S(1)}, f32[384,512]{1,0:T(8,128)S(1)}, u32[]{:S(2)}, u32[]{:S(2)}) collective-permute-start(f32[384,512]{1,0:T(8,128)S(1)} %pad_maximum_fusion), channel_id=1, source_target_pairs={{0,1},{1,0},{2,3},{3,2},{4,5},{5,4},{6,7},{7,6},{8,9},{9,8},{10,11... | collective-permute-start | bytes 2359304 | tf_op jit(solution)/shard_map/ppermute | solution.py:123
  171.7 1.7 collective-permute-done.6
  173.4 0.2 broadcast_select_fusion.1
  173.6 0.2 maximum_multiply_fusion
  173.8 0.6 slice.26
  175.0 1.1 slice_add_fusion.a_ref
  176.1 61.4 %shard_map.30 = (f32[512,512]{1,0:T(8,128)}, f32[512,512]{1,0:T(8,128)}) custom-call(f32[512,512]{1,0:T(8,128)} %slice_add_fusion.a_ref), custom_call_target="tpu_custom_call" | custom-call | flops 268435456 | bytes 3145728 | tf_op jit(solution)/shard_map/pallas_call | solution.py:82
  237.5 2.4 fusion.8
  239.8 0.0 copy-start.2
  239.8 0.0 reduce-scatter.2.cloned.1.call-done
  239.9 1.2 broadcast_multiply_fusion
  241.1 2.2 fusion.10
  243.3 1.2 convolution_subtract_fusion
  244.5 0.0 copy-done.2
  (7 shorter events, 0.1 us)
Async XLA Ops:
  7.2 78.2 %all-gather.2.cloned.1.call-start = ((), (), s32[]{:S(2)}) async-start(), calls=%async_computation.1 | async-start | bytes 4456448 | tf_op jit(solution)/shard_map/all_gather | solution.py:142
  7.9 232.0 %reduce-scatter.2.cloned.1.call-start = ((), (), s32[]{:S(2)}) async-start(), calls=%async_computation.2 | async-start | bytes 12976128 | tf_op jit(solution)/shard_map/reduce_scatter | solution.py:162
  85.3 3.4 %copy-start = (bf16[4096,512]{1,0:T(8,128)(2,1)S(1)}, bf16[4096,512]{1,0:T(8,128)(2,1)}, u32[]{:S(2)}) copy-start(bf16[4096,512]{1,0:T(8,128)(2,1)} %all-gather.2.cloned.1.call-done) | copy-start | bytes 12582916
  91.6 1.9 copy-start.1
  103.9 13.4 %collective-permute-start = (f32[384,512]{1,0:T(8,128)S(1)}, f32[384,512]{1,0:T(8,128)S(1)}, u32[]{:S(2)}, u32[]{:S(2)}) collective-permute-start(f32[384,512]{1,0:T(8,128)S(1)} %fusion.1), channel_id=1, source_target_pairs={{0,1},{1,0},{2,3},{3,2},{4,5},{5,4},{6,7},{7,6},{8,9},{9,8},{10,11... | collective-permute-start | bytes 2359304 | tf_op jit(solution)/shard_map/ppermute | solution.py:117
  117.5 8.8 %collective-permute-start.1 = (f32[192,512]{1,0:T(8,128)S(1)}, f32[192,512]{1,0:T(8,128)S(1)}, u32[]{:S(2)}, u32[]{:S(2)}) collective-permute-start(f32[192,512]{1,0:T(8,128)S(1)} %constant_dynamic-slice_fusion), channel_id=1, source_target_pairs={{0,2},{1,9},{2,0},{3,11},{4,6},{5,13},{6,4},{7,15},{8,10},{9,1},{1... | collective-permute-start | bytes 1179656 | tf_op jit(solution)/shard_map/ppermute | solution.py:117
  126.4 8.8 %collective-permute-start.2 = (f32[192,512]{1,0:T(8,128)S(1)}, f32[192,512]{1,0:T(8,128)S(1)}, u32[]{:S(2)}, u32[]{:S(2)}) collective-permute-start(f32[192,512]{1,0:T(8,128)S(1)} %dynamic-slice_add_fusion), channel_id=1, source_target_pairs={{0,8},{1,3},{2,10},{3,1},{4,12},{5,7},{6,14},{7,5},{8,0},{9,11},{1... | collective-permute-start | bytes 1179656 | tf_op jit(solution)/shard_map/ppermute | solution.py:120
  135.2 10.3 %collective-permute-start.3 = (f32[192,512]{1,0:T(8,128)S(1)}, f32[192,512]{1,0:T(8,128)S(1)}, u32[]{:S(2)}, u32[]{:S(2)}) collective-permute-start(f32[192,512]{1,0:T(8,128)S(1)} %add.85), channel_id=1, source_target_pairs={{0,4},{1,17},{2,6},{3,19},{4,0},{5,21},{6,2},{7,23},{8,12},{9,25},... | collective-permute-start | bytes 1179656 | tf_op jit(solution)/shard_map/ppermute | solution.py:120
  145.6 10.3 %collective-permute-start.4 = (f32[192,512]{1,0:T(8,128)S(1)}, f32[192,512]{1,0:T(8,128)S(1)}, u32[]{:S(2)}, u32[]{:S(2)}) collective-permute-start(f32[192,512]{1,0:T(8,128)S(1)} %add.86), channel_id=1, source_target_pairs={{0,16},{1,5},{2,18},{3,7},{4,20},{5,1},{6,22},{7,3},{8,24},{9,13},... | collective-permute-start | bytes 1179656 | tf_op jit(solution)/shard_map/ppermute | solution.py:120
  156.0 8.5 %collective-permute-start.5 = (f32[192,512]{1,0:T(8,128)S(1)}, f32[192,512]{1,0:T(8,128)S(1)}, u32[]{:S(2)}, u32[]{:S(2)}) collective-permute-start(f32[192,512]{1,0:T(8,128)S(1)} %add.87), channel_id=1, source_target_pairs={{0,2},{1,9},{2,0},{3,11},{4,6},{5,13},{6,4},{7,15},{8,10},{9,1},{1... | collective-permute-start | bytes 1179656 | tf_op jit(solution)/shard_map/ppermute | solution.py:123
  164.7 8.7 %collective-permute-start.6 = (f32[384,512]{1,0:T(8,128)S(1)}, f32[384,512]{1,0:T(8,128)S(1)}, u32[]{:S(2)}, u32[]{:S(2)}) collective-permute-start(f32[384,512]{1,0:T(8,128)S(1)} %pad_maximum_fusion), channel_id=1, source_target_pairs={{0,1},{1,0},{2,3},{3,2},{4,5},{5,4},{6,7},{7,6},{8,9},{9,8},{10,11... | collective-permute-start | bytes 2359304 | tf_op jit(solution)/shard_map/ppermute | solution.py:123
  239.8 4.7 %copy-start.2 = (f32[256,512]{1,0:T(8,128)}, f32[256,512]{1,0:T(8,128)S(1)}, u32[]{:S(2)}) copy-start(f32[256,512]{1,0:T(8,128)S(1)} %fusion.8) | copy-start | bytes 1572868
Sparse Core Ops, SparseCore 0:
  10.1 75.2 all-gather.1
  100.1 131.8 reduce-scatter.1

commit v12 on v11

--- a/solution.py
+++ b/solution.py
@@ -17,7 +17,7 @@
 NT = (((1,), (1,)), ((), ()))
 
 
-def _chol_kernel(a_ref, l_ref, w_ref, s_ref, blk_a, blk_b, blk_lt, blk_w, *, n, b):
+def _chol_kernel(a_ref, p_ref, po_ref, p2_ref, l_ref, w_ref, s_ref, blk_a, blk_b, blk_lt, blk_w, *, n, b):
     nb = n // b
     f32 = jnp.float32
     whole = a_ref[...]
@@ -74,25 +74,34 @@
             w_ref[pl.ds(i * b, b), pl.ds(j * b, b)] = -jnp.dot(
                 w_ii, acc, precision=HI, preferred_element_type=f32
             )
-
-
-def chol_and_inverse(a, block=128):
+    inverse = w_ref[...]
+    panel_out = lax.dot_general(p_ref[...], inverse, NT, precision=HI, preferred_element_type=f32)
+    po_ref[...] = panel_out
+    p2_ref[...] = jnp.dot(panel_out, inverse, precision=HI, preferred_element_type=f32)
+
+
+def chol_and_inverse(a, panel, block=128):
     n = a.shape[0]
     f32 = jnp.float32
+    vmem = pl.BlockSpec(memory_space=pltpu.VMEM)
     return pl.pallas_call(
         functools.partial(_chol_kernel, n=n, b=block),
-        out_shape=(jax.ShapeDtypeStruct((n, n), f32), jax.ShapeDtypeStruct((n, n), f32)),
-        in_specs=[pl.BlockSpec(memory_space=pltpu.VMEM)],
-        out_specs=(pl.BlockSpec(memory_space=pltpu.VMEM), pl.BlockSpec(memory_space=pltpu.VMEM)),
+        out_shape=(jax.ShapeDtypeStruct(panel.shape, f32), jax.ShapeDtypeStruct(panel.shape, f32)),
+        in_specs=[vmem, vmem],
+        out_specs=(vmem, vmem),
         scratch_shapes=[
             pltpu.VMEM((n, n), f32),
+            pltpu.VMEM((n, n), f32),
+            pltpu.VMEM((n, n), f32),
             pltpu.VMEM((block, block), f32),
             pltpu.VMEM((block, block), f32),
             pltpu.VMEM((block, block), f32),
             pltpu.VMEM((block, block), f32),
         ],
-        cost_estimate=pl.CostEstimate(flops=2 * n * n * n, bytes_accessed=3 * n * n * 4, transcendentals=n),
-    )(a)
+        cost_estimate=pl.CostEstimate(
+            flops=2 * n * n * n + 4 * panel.shape[0] * n * n, bytes_accessed=5 * n * n * 4, transcendentals=n
+        ),
+    )(a, panel)
 
 
 def reduce_by_halving(x, axis, count):
@@ -176,10 +185,8 @@
     band_s = band_t + jnp.where(eye[:, None] == global_cols[None, :], shift_value, 0.0)
     tile_s = tile + jnp.where(global_rows[:, None] == global_cols[None, :], shift_value, 0.0)
 
-    _, inverse = chol_and_inverse(square_s)
-    panel_out = lax.dot_general(panel_s, inverse, NT, precision=HI, preferred_element_type=f32)
-    band_factor = jnp.dot(inverse, band_s, precision=HI, preferred_element_type=f32)
-    schur_tile = tile_s - jnp.dot(panel_out, band_factor, precision=lax.Precision.HIGHEST)
+    panel_out, projected = chol_and_inverse(square_s, panel_s)
+    schur_tile = tile_s - jnp.dot(projected, band_s, precision=HI, preferred_element_type=f32)
     return (panel_out, schur_tile)
 
 

time: 252 us -> 250 us (level)
  matrix products: 15.9 us -> 12.4 us
    dot_general x3 -> x1, matrix products: 5.82 us -> 2.3 us  [shards(): jnp.dot(projected, band_s, precision=HI, preferred_element_type=f32)]
  transfers between devices with their start and end apart: 9 -> 9, of which waited for: 8 -> 8; matrix products, arithmetic and copies ran while one was open for 4% -> 3% of each run, Pallas kernels for 24% -> 25%
where the time goes in v12:
time: 250 us
  waiting for transfers between devices  110 us (44%)
  Pallas kernels  62.7 us (25%)
  starting transfers between devices  36.5 us (15%)
  between operations  15 us (6%)
  matrix products  12.4 us (5%)
  other arithmetic  9.96 us (4%)
  local copies, waits for them, and re-layouts  3.02 us (1%)
    all_gather x1, waiting for transfers between devices, shards(): gathered = lax.all_gather(jacobian, 'smp', axis=0, tiled=True)  77.4 us
    pallas_call x1, Pallas kernels, chol_and_inverse(): pl.pallas_call(functools.partial(_chol_kernel, n=n, b=block), out_shape=(...  62.7 us
    ppermute x3, waiting for transfers between devices, reduce_by_halving(): x = x + lax.ppermute(x, axis, partners(pair))  17.4 us
    ppermute x2, starting transfers between devices, reduce_by_halving(): x = keep + lax.ppermute(send, axis, partners(pair))  14.5 us
    ppermute x3, starting transfers between devices, reduce_by_halving(): x = x + lax.ppermute(x, axis, partners(pair))  12.1 us
    ppermute x2, starting transfers between devices, reduce_by_halving(): other = lax.ppermute(x, axis, partners(pair))  9.82 us
    ppermute x2, waiting for transfers between devices, reduce_by_halving(): x = keep + lax.ppermute(send, axis, partners(pair))  7.54 us
    ppermute x2, waiting for transfers between devices, reduce_by_halving(): other = lax.ppermute(x, axis, partners(pair))  7.4 us
  transfers between devices with their start and end apart: 9, of which 8 were waited for; matrix products, arithmetic and copies ran while one was open for 3% of the time, Pallas kernels for 25%

profile of v12, /device:TPU:1, one launch (start us, length us, event | category | flops | bytes accessed | tf_op | source)
XLA Modules:
  0.0 249.9 jit_solution(10066420156066573579)
XLA Ops:
  7.2 0.0 all-gather.2.cloned.1.call-start
  7.2 0.7 all-gather.2.cloned.1.call-update
  7.9 0.0 reduce-scatter.2.cloned.1.call-start
  7.9 77.4 %all-gather.2.cloned.1.call-done = bf16[4096,512]{1,0:T(8,128)(2,1)} async-done(((bf16[256,512]{1,0:T(8,128)(2,1)}), bf16[4096,512]{1,0:T(8,128)(2,1)}) %all-gather.2.cloned.1.call-update) | async-done | bytes 4194320 | tf_op jit(solution)/shard_map/all_gather | solution.py:151
  85.3 0.0 copy-start
  85.3 3.0 %convert_reduce_fusion = f32[512]{0:T(512)S(1)} fusion(bf16[4096,512]{1,0:T(8,128)(2,1)} %all-gather.2.cloned.1.call-done), kind=kLoop, calls=%fused_computation.1 | loop fusion | flops 4193792 | bytes 4196352 | tf_op jit(solution)/shard_map/reduce_sum | solution.py:153
  88.3 0.5 copy-done
  88.8 2.8 %multiply_reduce_fusion = (f32[]{:T(128)}, bf16[4096,512]{1,0:T(8,128)(2,1)S(1)}) fusion(f32[512]{0:T(512)S(1)} %broadcast_multiply_fusion.1, bf16[4096,512]{1,0:T(8,128)(2,1)S(1)} %copy-done), kind=kLoop, calls=%fused_computation.3 | loop fusion | flops 12582911 | bytes 8390660 | tf_op jit(solution)/shard_map/reduce_sum | solution.py:162
  91.6 0.0 copy-start.1
  91.7 1.8 copy-done.1
  93.5 6.4 %fusion.4 = f32[768,4096]{1,0:T(8,128)} fusion(bf16[4096,512]{1,0:T(8,128)(2,1)S(1)} %get-tuple-element.7, bf16[512,512]{1,0:T(8,128)(2,1)S(1)} %slice.24, bf16[256,512]{1,0:T(8,128)(2,1)S(1)} %constant_dynamic-slice_fusion.1), kind=kOutput, calls=%fused_computation.17 | convolution fusion | flops 3222798336 | bytes 17563648 | tf_op jit(solution)/shard_map/dot_general | solution.py:170
  99.9 0.0 reduce-scatter.2.cloned.1.call-update
  100.0 1.4 fusion.15
  101.4 2.3 convolution_select_fusion
  103.7 0.2 fusion.1
  103.9 11.5 %collective-permute-start = (f32[384,512]{1,0:T(8,128)S(1)}, f32[384,512]{1,0:T(8,128)S(1)}, u32[]{:S(2)}, u32[]{:S(2)}) collective-permute-start(f32[384,512]{1,0:T(8,128)S(1)} %fusion.1), channel_id=1, source_target_pairs={{0,1},{1,0},{2,3},{3,2},{4,5},{5,4},{6,7},{7,6},{8,9},{9,8},{10,11... | collective-permute-start | bytes 2359304 | tf_op jit(solution)/shard_map/ppermute | solution.py:126
  115.4 1.8 collective-permute-done
  117.2 0.2 fusion.3
  117.5 3.1 %collective-permute-start.1 = (f32[192,512]{1,0:T(8,128)S(1)}, f32[192,512]{1,0:T(8,128)S(1)}, u32[]{:S(2)}, u32[]{:S(2)}) collective-permute-start(f32[192,512]{1,0:T(8,128)S(1)} %constant_dynamic-slice_fusion), channel_id=1, source_target_pairs={{0,2},{1,9},{2,0},{3,11},{4,6},{5,13},{6,4},{7,15},{8,10},{9,1},{1... | collective-permute-start | bytes 1179656 | tf_op jit(solution)/shard_map/ppermute | solution.py:126
  120.6 5.7 %collective-permute-done.1 = f32[192,512]{1,0:T(8,128)S(1)} collective-permute-done((f32[192,512]{1,0:T(8,128)S(1)}, f32[192,512]{1,0:T(8,128)S(1)}, u32[]{:S(2)}, u32[]{:S(2)}) %collective-permute-start.1) | collective-permute-done | bytes 393248 | tf_op jit(solution)/shard_map/ppermute | solution.py:126
  126.3 0.1 dynamic-slice_add_fusion
  126.4 3.1 %collective-permute-start.2 = (f32[192,512]{1,0:T(8,128)S(1)}, f32[192,512]{1,0:T(8,128)S(1)}, u32[]{:S(2)}, u32[]{:S(2)}) collective-permute-start(f32[192,512]{1,0:T(8,128)S(1)} %dynamic-slice_add_fusion), channel_id=1, source_target_pairs={{0,8},{1,3},{2,10},{3,1},{4,12},{5,7},{6,14},{7,5},{8,0},{9,11},{1... | collective-permute-start | bytes 1179656 | tf_op jit(solution)/shard_map/ppermute | solution.py:129
  129.5 5.7 %collective-permute-done.2 = f32[192,512]{1,0:T(8,128)S(1)} collective-permute-done((f32[192,512]{1,0:T(8,128)S(1)}, f32[192,512]{1,0:T(8,128)S(1)}, u32[]{:S(2)}, u32[]{:S(2)}) %collective-permute-start.2) | collective-permute-done | bytes 393248 | tf_op jit(solution)/shard_map/ppermute | solution.py:129
  135.2 0.1 add.85
  135.3 4.6 %collective-permute-start.3 = (f32[192,512]{1,0:T(8,128)S(1)}, f32[192,512]{1,0:T(8,128)S(1)}, u32[]{:S(2)}, u32[]{:S(2)}) collective-permute-start(f32[192,512]{1,0:T(8,128)S(1)} %add.85), channel_id=1, source_target_pairs={{0,4},{1,17},{2,6},{3,19},{4,0},{5,21},{6,2},{7,23},{8,12},{9,25},... | collective-permute-start | bytes 1179656 | tf_op jit(solution)/shard_map/ppermute | solution.py:129
  139.9 5.7 %collective-permute-done.3 = f32[192,512]{1,0:T(8,128)S(1)} collective-permute-done((f32[192,512]{1,0:T(8,128)S(1)}, f32[192,512]{1,0:T(8,128)S(1)}, u32[]{:S(2)}, u32[]{:S(2)}) %collective-permute-start.3) | collective-permute-done | bytes 393248 | tf_op jit(solution)/shard_map/ppermute | solution.py:129
  145.6 0.1 add.86
  145.6 4.3 %collective-permute-start.4 = (f32[192,512]{1,0:T(8,128)S(1)}, f32[192,512]{1,0:T(8,128)S(1)}, u32[]{:S(2)}, u32[]{:S(2)}) collective-permute-start(f32[192,512]{1,0:T(8,128)S(1)} %add.86), channel_id=1, source_target_pairs={{0,16},{1,5},{2,18},{3,7},{4,20},{5,1},{6,22},{7,3},{8,24},{9,13},... | collective-permute-start | bytes 1179656 | tf_op jit(solution)/shard_map/ppermute | solution.py:129
  150.0 6.0 %collective-permute-done.4 = f32[192,512]{1,0:T(8,128)S(1)} collective-permute-done((f32[192,512]{1,0:T(8,128)S(1)}, f32[192,512]{1,0:T(8,128)S(1)}, u32[]{:S(2)}, u32[]{:S(2)}) %collective-permute-start.4) | collective-permute-done | bytes 393248 | tf_op jit(solution)/shard_map/ppermute | solution.py:129
  156.0 0.1 add.87
  156.0 2.8 %collective-permute-start.5 = (f32[192,512]{1,0:T(8,128)S(1)}, f32[192,512]{1,0:T(8,128)S(1)}, u32[]{:S(2)}, u32[]{:S(2)}) collective-permute-start(f32[192,512]{1,0:T(8,128)S(1)} %add.87), channel_id=1, source_target_pairs={{0,2},{1,9},{2,0},{3,11},{4,6},{5,13},{6,4},{7,15},{8,10},{9,1},{1... | collective-permute-start | bytes 1179656 | tf_op jit(solution)/shard_map/ppermute | solution.py:132
  158.8 5.7 %collective-permute-done.5 = f32[192,512]{1,0:T(8,128)S(1)} collective-permute-done((f32[192,512]{1,0:T(8,128)S(1)}, f32[192,512]{1,0:T(8,128)S(1)}, u32[]{:S(2)}, u32[]{:S(2)}) %collective-permute-start.5) | collective-permute-done | bytes 393248 | tf_op jit(solution)/shard_map/ppermute | solution.py:132
  164.5 0.1 broadcast_select_fusion.3
  164.6 0.1 pad_maximum_fusion
  164.7 7.0 %collective-permute-start.6 = (f32[384,512]{1,0:T(8,128)S(1)}, f32[384,512]{1,0:T(8,128)S(1)}, u32[]{:S(2)}, u32[]{:S(2)}) collective-permute-start(f32[384,512]{1,0:T(8,128)S(1)} %pad_maximum_fusion), channel_id=1, source_target_pairs={{0,1},{1,0},{2,3},{3,2},{4,5},{5,4},{6,7},{7,6},{8,9},{9,8},{10,11... | collective-permute-start | bytes 2359304 | tf_op jit(solution)/shard_map/ppermute | solution.py:132
  171.8 1.7 collective-permute-done.6
  173.4 0.2 broadcast_select_fusion.1
  173.6 0.2 maximum_multiply_fusion
  173.8 0.6 slice.26
  175.0 0.9 slice_add_fusion.1.p_ref
  175.9 1.2 slice_add_fusion.a_ref
  177.1 62.7 %shard_map.30 = (f32[256,512]{1,0:T(8,128)}, f32[256,512]{1,0:T(8,128)}) custom-call(f32[512,512]{1,0:T(8,128)} %slice_add_fusion.a_ref, f32[256,512]{1,0:T(8,128)} %slice_add_fusion.1.p_ref), custom_call_target="tpu_custom_call" | custom-call | flops 536870912 | bytes 5242880 | tf_op jit(solution)/shard_map/pallas_call | solution.py:87
  239.8 0.0 reduce-scatter.2.cloned.1.call-done
  239.8 1.0 broadcast_multiply_fusion
  240.8 2.3 convolution_subtract_fusion
  (7 shorter events, 0.1 us)
Async XLA Ops:
  7.2 78.2 %all-gather.2.cloned.1.call-start = ((), (), s32[]{:S(2)}) async-start(), calls=%async_computation.1 | async-start | bytes 4456448 | tf_op jit(solution)/shard_map/all_gather | solution.py:151
  7.9 231.9 %reduce-scatter.2.cloned.1.call-start = ((), (), s32[]{:S(2)}) async-start(), calls=%async_computation.2 | async-start | bytes 12976128 | tf_op jit(solution)/shard_map/reduce_scatter | solution.py:171
  85.3 3.4 %copy-start = (bf16[4096,512]{1,0:T(8,128)(2,1)S(1)}, bf16[4096,512]{1,0:T(8,128)(2,1)}, u32[]{:S(2)}) copy-start(bf16[4096,512]{1,0:T(8,128)(2,1)} %all-gather.2.cloned.1.call-done) | copy-start | bytes 12582916
  91.6 1.9 copy-start.1
  103.9 13.4 %collective-permute-start = (f32[384,512]{1,0:T(8,128)S(1)}, f32[384,512]{1,0:T(8,128)S(1)}, u32[]{:S(2)}, u32[]{:S(2)}) collective-permute-start(f32[384,512]{1,0:T(8,128)S(1)} %fusion.1), channel_id=1, source_target_pairs={{0,1},{1,0},{2,3},{3,2},{4,5},{5,4},{6,7},{7,6},{8,9},{9,8},{10,11... | collective-permute-start | bytes 2359304 | tf_op jit(solution)/shard_map/ppermute | solution.py:126
  117.5 8.8 %collective-permute-start.1 = (f32[192,512]{1,0:T(8,128)S(1)}, f32[192,512]{1,0:T(8,128)S(1)}, u32[]{:S(2)}, u32[]{:S(2)}) collective-permute-start(f32[192,512]{1,0:T(8,128)S(1)} %constant_dynamic-slice_fusion), channel_id=1, source_target_pairs={{0,2},{1,9},{2,0},{3,11},{4,6},{5,13},{6,4},{7,15},{8,10},{9,1},{1... | collective-permute-start | bytes 1179656 | tf_op jit(solution)/shard_map/ppermute | solution.py:126
  126.4 8.8 %collective-permute-start.2 = (f32[192,512]{1,0:T(8,128)S(1)}, f32[192,512]{1,0:T(8,128)S(1)}, u32[]{:S(2)}, u32[]{:S(2)}) collective-permute-start(f32[192,512]{1,0:T(8,128)S(1)} %dynamic-slice_add_fusion), channel_id=1, source_target_pairs={{0,8},{1,3},{2,10},{3,1},{4,12},{5,7},{6,14},{7,5},{8,0},{9,11},{1... | collective-permute-start | bytes 1179656 | tf_op jit(solution)/shard_map/ppermute | solution.py:129
  135.3 10.3 %collective-permute-start.3 = (f32[192,512]{1,0:T(8,128)S(1)}, f32[192,512]{1,0:T(8,128)S(1)}, u32[]{:S(2)}, u32[]{:S(2)}) collective-permute-start(f32[192,512]{1,0:T(8,128)S(1)} %add.85), channel_id=1, source_target_pairs={{0,4},{1,17},{2,6},{3,19},{4,0},{5,21},{6,2},{7,23},{8,12},{9,25},... | collective-permute-start | bytes 1179656 | tf_op jit(solution)/shard_map/ppermute | solution.py:129
  145.6 10.3 %collective-permute-start.4 = (f32[192,512]{1,0:T(8,128)S(1)}, f32[192,512]{1,0:T(8,128)S(1)}, u32[]{:S(2)}, u32[]{:S(2)}) collective-permute-start(f32[192,512]{1,0:T(8,128)S(1)} %add.86), channel_id=1, source_target_pairs={{0,16},{1,5},{2,18},{3,7},{4,20},{5,1},{6,22},{7,3},{8,24},{9,13},... | collective-permute-start | bytes 1179656 | tf_op jit(solution)/shard_map/ppermute | solution.py:129
  156.0 8.5 %collective-permute-start.5 = (f32[192,512]{1,0:T(8,128)S(1)}, f32[192,512]{1,0:T(8,128)S(1)}, u32[]{:S(2)}, u32[]{:S(2)}) collective-permute-start(f32[192,512]{1,0:T(8,128)S(1)} %add.87), channel_id=1, source_target_pairs={{0,2},{1,9},{2,0},{3,11},{4,6},{5,13},{6,4},{7,15},{8,10},{9,1},{1... | collective-permute-start | bytes 1179656 | tf_op jit(solution)/shard_map/ppermute | solution.py:132
  164.7 8.7 %collective-permute-start.6 = (f32[384,512]{1,0:T(8,128)S(1)}, f32[384,512]{1,0:T(8,128)S(1)}, u32[]{:S(2)}, u32[]{:S(2)}) collective-permute-start(f32[384,512]{1,0:T(8,128)S(1)} %pad_maximum_fusion), channel_id=1, source_target_pairs={{0,1},{1,0},{2,3},{3,2},{4,5},{5,4},{6,7},{7,6},{8,9},{9,8},{10,11... | collective-permute-start | bytes 2359304 | tf_op jit(solution)/shard_map/ppermute | solution.py:132
Sparse Core Ops, SparseCore 0:
  10.1 75.2 all-gather.1
  100.1 131.8 reduce-scatter.1

commit v13 on v12

--- a/solution.py
+++ b/solution.py
@@ -17,12 +17,23 @@
 NT = (((1,), (1,)), ((), ()))
 
 
+def lower_blocks(count):
+    return [(i, j) for i in range(count) for j in range(i + 1)]
+
+
 def _chol_kernel(a_ref, p_ref, po_ref, p2_ref, l_ref, w_ref, s_ref, blk_a, blk_b, blk_lt, blk_w, *, n, b):
     nb = n // b
     f32 = jnp.float32
-    whole = a_ref[...]
-    lower = lax.broadcasted_iota(jnp.int32, (n, n), 0) >= lax.broadcasted_iota(jnp.int32, (n, n), 1)
-    s_ref[...] = jnp.where(lower, whole, jnp.transpose(whole))
+    lower = lax.broadcasted_iota(jnp.int32, (b, b), 0) >= lax.broadcasted_iota(jnp.int32, (b, b), 1)
+    per_group = n // b
+    for idx, (i, j) in enumerate(lower_blocks(n // b)):
+        g, c = divmod(idx, per_group)
+        blk = a_ref[pl.ds(g * b, b), pl.ds(c * b, b)]
+        if i == j:
+            s_ref[pl.ds(i * b, b), pl.ds(i * b, b)] = jnp.where(lower, blk, jnp.transpose(blk))
+        else:
+            s_ref[pl.ds(i * b, b), pl.ds(j * b, b)] = blk
+            s_ref[pl.ds(j * b, b), pl.ds(i * b, b)] = jnp.transpose(blk)
     l_ref[...] = jnp.zeros((n, n), f32)
     w_ref[...] = jnp.zeros((n, n), f32)
     rows = lax.broadcasted_iota(jnp.int32, (b, b), 0)
@@ -81,7 +92,7 @@
 
 
 def chol_and_inverse(a, panel, block=128):
-    n = a.shape[0]
+    n = panel.shape[1]
     f32 = jnp.float32
     vmem = pl.BlockSpec(memory_space=pltpu.VMEM)
     return pl.pallas_call(
@@ -161,9 +172,19 @@
     sq = centered.astype(f32)
     sumsq = jnp.sum(sq * sq)
 
-    corner = (jnp.arange(PANEL)[:, None] == 0) & (jnp.arange(PANEL)[None, :] == PANEL - 1)
-    square = jnp.where(corner, sumsq, square)
-    panel_in = jnp.concatenate([main_t, square], axis=0)
+    block = 128
+    per_group = PANEL // block
+    pieces = [square[i * block : (i + 1) * block, j * block : (j + 1) * block] for i, j in lower_blocks(per_group)]
+    first_pad = len(pieces)
+    groups = -(-first_pad // per_group)
+    corner = (jnp.arange(block)[:, None] == 0) & (jnp.arange(block)[None, :] == 0)
+    pieces.append(jnp.where(corner, sumsq, 0.0))
+    while len(pieces) < groups * per_group:
+        pieces.append(jnp.zeros((block, block), f32))
+    packed = jnp.concatenate(
+        [jnp.concatenate(pieces[g * per_group : (g + 1) * per_group], axis=1) for g in range(groups)], axis=0
+    )
+    panel_in = jnp.concatenate([main_t, packed], axis=0)
     shared = reduce_by_halving(panel_in, "par", par_count) / param_total
 
     lhs = jnp.concatenate([mine, head], axis=0)
@@ -173,14 +194,22 @@
     band_t = big[row_count:]
 
     panel_g = shared[:row_count]
-    square_g = shared[row_count : row_count + PANEL]
-    trace_total = shared[row_count, PANEL - 1]
+    square_g = shared[row_count:]
+    pad_g, pad_c = divmod(first_pad, per_group)
+    trace_total = shared[row_count + pad_g * block, pad_c * block]
     shift_value = shift_scale * trace_total / sample_total
 
     eye = jnp.arange(PANEL, dtype=jnp.int32)
     global_rows = row_index * row_count + jnp.arange(row_count, dtype=jnp.int32)
     global_cols = col_index * col_width + jnp.arange(col_width, dtype=jnp.int32)
-    square_s = square_g + jnp.where(eye[:, None] == eye[None, :], shift_value, 0.0)
+    pr = jnp.arange(groups * block, dtype=jnp.int32)[:, None]
+    pc = jnp.arange(PANEL, dtype=jnp.int32)[None, :]
+    on_diag = jnp.zeros((groups * block, PANEL), bool)
+    for idx, (i, j) in enumerate(lower_blocks(per_group)):
+        if i == j:
+            g, c = divmod(idx, per_group)
+            on_diag = on_diag | ((pr // block == g) & (pc // block == c) & (pr % block == pc % block))
+    square_s = square_g + jnp.where(on_diag, shift_value, 0.0)
     panel_s = panel_g + jnp.where(global_rows[:, None] == eye[None, :], shift_value, 0.0)
     band_s = band_t + jnp.where(eye[:, None] == global_cols[None, :], shift_value, 0.0)
     tile_s = tile + jnp.where(global_rows[:, None] == global_cols[None, :], shift_value, 0.0)

time: 250 us -> 247 us (0.988)
  waiting for transfers between devices: 110 us -> 106 us
where the time goes in v13:
time: 247 us; the launch traced here: 246 us
  waiting for transfers between devices  106 us (43%)
  Pallas kernels  62.8 us (25%)
  starting transfers between devices  36.5 us (15%)
  between operations  15 us (6%)
  matrix products  11.7 us (5%)
  other arithmetic  10.8 us (4%)
  local copies, waits for them, and re-layouts  3.05 us (1%)
    all_gather x1, waiting for transfers between devices, shards(): gathered = lax.all_gather(jacobian, 'smp', axis=0, tiled=True)  77.4 us
    pallas_call x1, Pallas kernels, chol_and_inverse(): pl.pallas_call(functools.partial(_chol_kernel, n=n, b=block), out_shape=(...  62.8 us
    ppermute x3, waiting for transfers between devices, reduce_by_halving(): x = x + lax.ppermute(x, axis, partners(pair))  15.3 us
    ppermute x2, starting transfers between devices, reduce_by_halving(): x = keep + lax.ppermute(send, axis, partners(pair))  14.5 us
    ppermute x3, starting transfers between devices, reduce_by_halving(): x = x + lax.ppermute(x, axis, partners(pair))  12 us
    ppermute x2, starting transfers between devices, reduce_by_halving(): other = lax.ppermute(x, axis, partners(pair))  9.81 us
    ppermute x2, waiting for transfers between devices, reduce_by_halving(): x = keep + lax.ppermute(send, axis, partners(pair))  6.67 us
    ppermute x2, waiting for transfers between devices, reduce_by_halving(): other = lax.ppermute(x, axis, partners(pair))  6.45 us
  transfers between devices with their start and end apart: 9, of which 8 were waited for; matrix products, arithmetic and copies ran while one was open for 3% of the time, Pallas kernels for 25%

profile of v13, /device:TPU:1, one launch (start us, length us, event | category | flops | bytes accessed | tf_op | source)
XLA Modules:
  0.0 246.2 jit_solution(1592325833498887240)
XLA Ops:
  7.2 0.0 all-gather.2.cloned.1.call-start
  7.2 0.7 all-gather.2.cloned.1.call-update
  7.9 0.0 reduce-scatter.2.cloned.1.call-start
  7.9 77.4 %all-gather.2.cloned.1.call-done = bf16[4096,512]{1,0:T(8,128)(2,1)} async-done(((bf16[256,512]{1,0:T(8,128)(2,1)}), bf16[4096,512]{1,0:T(8,128)(2,1)}) %all-gather.2.cloned.1.call-update) | async-done | bytes 4194320 | tf_op jit(solution)/shard_map/all_gather | solution.py:162
  85.3 0.0 copy-start
  85.3 3.0 %convert_reduce_fusion = f32[512]{0:T(512)S(1)} fusion(bf16[4096,512]{1,0:T(8,128)(2,1)} %all-gather.2.cloned.1.call-done), kind=kLoop, calls=%fused_computation.1 | loop fusion | flops 4193792 | bytes 4196352 | tf_op jit(solution)/shard_map/reduce_sum | solution.py:164
  88.3 0.5 copy-done
  88.8 2.8 %multiply_reduce_fusion = (f32[]{:T(128)}, bf16[4096,512]{1,0:T(8,128)(2,1)S(1)}) fusion(f32[512]{0:T(512)S(1)} %broadcast_multiply_fusion.1, bf16[4096,512]{1,0:T(8,128)(2,1)S(1)} %copy-done), kind=kLoop, calls=%fused_computation.3 | loop fusion | flops 12582911 | bytes 8390660 | tf_op jit(solution)/shard_map/reduce_sum | solution.py:173
  91.6 0.0 copy-start.1
  91.7 1.9 copy-done.1
  93.5 6.4 %fusion.1 = f32[768,4096]{1,0:T(8,128)} fusion(bf16[4096,512]{1,0:T(8,128)(2,1)S(1)} %get-tuple-element.7, bf16[512,512]{1,0:T(8,128)(2,1)S(1)} %slice.56, bf16[256,512]{1,0:T(8,128)(2,1)S(1)} %constant_dynamic-slice_fusion.2), kind=kOutput, calls=%fused_computation.12 | convolution fusion | flops 3222798336 | bytes 17563648 | tf_op jit(solution)/shard_map/dot_general | solution.py:191
  99.9 0.0 reduce-scatter.2.cloned.1.call-update
  99.9 1.7 fusion.34
  101.6 0.7 fusion.39
  102.4 1.4 fusion.36
  103.8 0.1 maximum_maximum_fusion
  103.9 0.1 constant_dynamic-slice_fusion.1
  104.0 11.5 %collective-permute-start = (f32[320,512]{1,0:T(8,128)S(1)}, f32[320,512]{1,0:T(8,128)S(1)}, u32[]{:S(2)}, u32[]{:S(2)}) collective-permute-start(f32[320,512]{1,0:T(8,128)S(1)} %constant_dynamic-slice_fusion.1), channel_id=1, source_target_pairs={{0,1},{1,0},{2,3},{3,2},{4,5},{5,4},{6,7},{7,6},{8,9},{9,8},{10,11... | collective-permute-start | bytes 1966088 | tf_op jit(solution)/shard_map/ppermute | solution.py:137
  115.5 1.6 collective-permute-done
  117.2 0.1 dynamic-slice_add_fusion
  117.3 3.1 %collective-permute-start.1 = (f32[160,512]{1,0:T(8,128)S(1)}, f32[160,512]{1,0:T(8,128)S(1)}, u32[]{:S(2)}, u32[]{:S(2)}) collective-permute-start(f32[160,512]{1,0:T(8,128)S(1)} %constant_dynamic-slice_fusion), channel_id=1, source_target_pairs={{0,2},{1,9},{2,0},{3,11},{4,6},{5,13},{6,4},{7,15},{8,10},{9,1},{1... | collective-permute-start | bytes 983048 | tf_op jit(solution)/shard_map/ppermute | solution.py:137
  120.4 5.0 %collective-permute-done.1 = f32[160,512]{1,0:T(8,128)S(1)} collective-permute-done((f32[160,512]{1,0:T(8,128)S(1)}, f32[160,512]{1,0:T(8,128)S(1)}, u32[]{:S(2)}, u32[]{:S(2)}) %collective-permute-start.1) | collective-permute-done | bytes 327712 | tf_op jit(solution)/shard_map/ppermute | solution.py:137
  125.5 3.1 %collective-permute-start.2 = (f32[160,512]{1,0:T(8,128)S(1)}, f32[160,512]{1,0:T(8,128)S(1)}, u32[]{:S(2)}, u32[]{:S(2)}) collective-permute-start(f32[160,512]{1,0:T(8,128)S(1)} %dynamic-slice_add_fusion.1), channel_id=1, source_target_pairs={{0,8},{1,3},{2,10},{3,1},{4,12},{5,7},{6,14},{7,5},{8,0},{9,11},{1... | collective-permute-start | bytes 983048 | tf_op jit(solution)/shard_map/ppermute | solution.py:140
  128.6 5.0 %collective-permute-done.2 = f32[160,512]{1,0:T(8,128)S(1)} collective-permute-done((f32[160,512]{1,0:T(8,128)S(1)}, f32[160,512]{1,0:T(8,128)S(1)}, u32[]{:S(2)}, u32[]{:S(2)}) %collective-permute-start.2) | collective-permute-done | bytes 327712 | tf_op jit(solution)/shard_map/ppermute | solution.py:140
  133.7 4.6 %collective-permute-start.3 = (f32[160,512]{1,0:T(8,128)S(1)}, f32[160,512]{1,0:T(8,128)S(1)}, u32[]{:S(2)}, u32[]{:S(2)}) collective-permute-start(f32[160,512]{1,0:T(8,128)S(1)} %add.143), channel_id=1, source_target_pairs={{0,4},{1,17},{2,6},{3,19},{4,0},{5,21},{6,2},{7,23},{8,12},{9,25},... | collective-permute-start | bytes 983048 | tf_op jit(solution)/shard_map/ppermute | solution.py:140
  138.3 5.0 %collective-permute-done.3 = f32[160,512]{1,0:T(8,128)S(1)} collective-permute-done((f32[160,512]{1,0:T(8,128)S(1)}, f32[160,512]{1,0:T(8,128)S(1)}, u32[]{:S(2)}, u32[]{:S(2)}) %collective-permute-start.3) | collective-permute-done | bytes 327712 | tf_op jit(solution)/shard_map/ppermute | solution.py:140
  143.3 4.3 %collective-permute-start.4 = (f32[160,512]{1,0:T(8,128)S(1)}, f32[160,512]{1,0:T(8,128)S(1)}, u32[]{:S(2)}, u32[]{:S(2)}) collective-permute-start(f32[160,512]{1,0:T(8,128)S(1)} %add.144), channel_id=1, source_target_pairs={{0,16},{1,5},{2,18},{3,7},{4,20},{5,1},{6,22},{7,3},{8,24},{9,13},... | collective-permute-start | bytes 983048 | tf_op jit(solution)/shard_map/ppermute | solution.py:140
  147.7 5.3 %collective-permute-done.4 = f32[160,512]{1,0:T(8,128)S(1)} collective-permute-done((f32[160,512]{1,0:T(8,128)S(1)}, f32[160,512]{1,0:T(8,128)S(1)}, u32[]{:S(2)}, u32[]{:S(2)}) %collective-permute-start.4) | collective-permute-done | bytes 327712 | tf_op jit(solution)/shard_map/ppermute | solution.py:140
  153.0 2.8 %collective-permute-start.5 = (f32[160,512]{1,0:T(8,128)S(1)}, f32[160,512]{1,0:T(8,128)S(1)}, u32[]{:S(2)}, u32[]{:S(2)}) collective-permute-start(f32[160,512]{1,0:T(8,128)S(1)} %add.145), channel_id=1, source_target_pairs={{0,2},{1,9},{2,0},{3,11},{4,6},{5,13},{6,4},{7,15},{8,10},{9,1},{1... | collective-permute-start | bytes 983048 | tf_op jit(solution)/shard_map/ppermute | solution.py:143
  155.8 5.0 %collective-permute-done.5 = f32[160,512]{1,0:T(8,128)S(1)} collective-permute-done((f32[160,512]{1,0:T(8,128)S(1)}, f32[160,512]{1,0:T(8,128)S(1)}, u32[]{:S(2)}, u32[]{:S(2)}) %collective-permute-start.5) | collective-permute-done | bytes 327712 | tf_op jit(solution)/shard_map/ppermute | solution.py:143
  160.8 0.1 broadcast_select_fusion.3
  160.9 7.0 %collective-permute-start.6 = (f32[320,512]{1,0:T(8,128)S(1)}, f32[320,512]{1,0:T(8,128)S(1)}, u32[]{:S(2)}, u32[]{:S(2)}) collective-permute-start(f32[320,512]{1,0:T(8,128)S(1)} %pad_maximum_fusion), channel_id=1, source_target_pairs={{0,1},{1,0},{2,3},{3,2},{4,5},{5,4},{6,7},{7,6},{8,9},{9,8},{10,11... | collective-permute-start | bytes 1966088 | tf_op jit(solution)/shard_map/ppermute | solution.py:143
  168.0 1.4 collective-permute-done.6
  169.5 0.1 broadcast_select_fusion.1
  169.6 0.1 maximum_multiply_fusion
  169.8 0.5 slice.64
  170.9 0.9 slice_add_fusion.1.p_ref
  171.8 1.5 slice_add_fusion.a_ref
  173.3 62.8 %shard_map.30 = (f32[256,512]{1,0:T(8,128)}, f32[256,512]{1,0:T(8,128)}) custom-call(f32[384,512]{1,0:T(8,128)} %slice_add_fusion.a_ref, f32[256,512]{1,0:T(8,128)} %slice_add_fusion.1.p_ref), custom_call_target="tpu_custom_call" | custom-call | flops 536870912 | bytes 5242880 | tf_op jit(solution)/shard_map/pallas_call | solution.py:98
  236.1 0.0 reduce-scatter.2.cloned.1.call-done
  236.1 1.0 broadcast_multiply_fusion
  237.1 2.3 convolution_subtract_fusion
  (20 shorter events, 0.4 us)
Async XLA Ops:
  7.2 78.2 %all-gather.2.cloned.1.call-start = ((), (), s32[]{:S(2)}) async-start(), calls=%async_computation.1 | async-start | bytes 4456448 | tf_op jit(solution)/shard_map/all_gather | solution.py:162
  7.9 228.2 %reduce-scatter.2.cloned.1.call-start = ((), (), s32[]{:S(2)}) async-start(), calls=%async_computation.2 | async-start | bytes 12976128 | tf_op jit(solution)/shard_map/reduce_scatter | solution.py:192
  85.3 3.4 %copy-start = (bf16[4096,512]{1,0:T(8,128)(2,1)S(1)}, bf16[4096,512]{1,0:T(8,128)(2,1)}, u32[]{:S(2)}) copy-start(bf16[4096,512]{1,0:T(8,128)(2,1)} %all-gather.2.cloned.1.call-done) | copy-start | bytes 12582916
  91.6 1.9 copy-start.1
  104.0 13.2 %collective-permute-start = (f32[320,512]{1,0:T(8,128)S(1)}, f32[320,512]{1,0:T(8,128)S(1)}, u32[]{:S(2)}, u32[]{:S(2)}) collective-permute-start(f32[320,512]{1,0:T(8,128)S(1)} %constant_dynamic-slice_fusion.1), channel_id=1, source_target_pairs={{0,1},{1,0},{2,3},{3,2},{4,5},{5,4},{6,7},{7,6},{8,9},{9,8},{10,11... | collective-permute-start | bytes 1966088 | tf_op jit(solution)/shard_map/ppermute | solution.py:137
  117.3 8.1 %collective-permute-start.1 = (f32[160,512]{1,0:T(8,128)S(1)}, f32[160,512]{1,0:T(8,128)S(1)}, u32[]{:S(2)}, u32[]{:S(2)}) collective-permute-start(f32[160,512]{1,0:T(8,128)S(1)} %constant_dynamic-slice_fusion), channel_id=1, source_target_pairs={{0,2},{1,9},{2,0},{3,11},{4,6},{5,13},{6,4},{7,15},{8,10},{9,1},{1... | collective-permute-start | bytes 983048 | tf_op jit(solution)/shard_map/ppermute | solution.py:137
  125.5 8.1 %collective-permute-start.2 = (f32[160,512]{1,0:T(8,128)S(1)}, f32[160,512]{1,0:T(8,128)S(1)}, u32[]{:S(2)}, u32[]{:S(2)}) collective-permute-start(f32[160,512]{1,0:T(8,128)S(1)} %dynamic-slice_add_fusion.1), channel_id=1, source_target_pairs={{0,8},{1,3},{2,10},{3,1},{4,12},{5,7},{6,14},{7,5},{8,0},{9,11},{1... | collective-permute-start | bytes 983048 | tf_op jit(solution)/shard_map/ppermute | solution.py:140
  133.7 9.6 %collective-permute-start.3 = (f32[160,512]{1,0:T(8,128)S(1)}, f32[160,512]{1,0:T(8,128)S(1)}, u32[]{:S(2)}, u32[]{:S(2)}) collective-permute-start(f32[160,512]{1,0:T(8,128)S(1)} %add.143), channel_id=1, source_target_pairs={{0,4},{1,17},{2,6},{3,19},{4,0},{5,21},{6,2},{7,23},{8,12},{9,25},... | collective-permute-start | bytes 983048 | tf_op jit(solution)/shard_map/ppermute | solution.py:140
  143.3 9.6 %collective-permute-start.4 = (f32[160,512]{1,0:T(8,128)S(1)}, f32[160,512]{1,0:T(8,128)S(1)}, u32[]{:S(2)}, u32[]{:S(2)}) collective-permute-start(f32[160,512]{1,0:T(8,128)S(1)} %add.144), channel_id=1, source_target_pairs={{0,16},{1,5},{2,18},{3,7},{4,20},{5,1},{6,22},{7,3},{8,24},{9,13},... | collective-permute-start | bytes 983048 | tf_op jit(solution)/shard_map/ppermute | solution.py:140
  153.0 7.8 %collective-permute-start.5 = (f32[160,512]{1,0:T(8,128)S(1)}, f32[160,512]{1,0:T(8,128)S(1)}, u32[]{:S(2)}, u32[]{:S(2)}) collective-permute-start(f32[160,512]{1,0:T(8,128)S(1)} %add.145), channel_id=1, source_target_pairs={{0,2},{1,9},{2,0},{3,11},{4,6},{5,13},{6,4},{7,15},{8,10},{9,1},{1... | collective-permute-start | bytes 983048 | tf_op jit(solution)/shard_map/ppermute | solution.py:143
  160.9 8.6 %collective-permute-start.6 = (f32[320,512]{1,0:T(8,128)S(1)}, f32[320,512]{1,0:T(8,128)S(1)}, u32[]{:S(2)}, u32[]{:S(2)}) collective-permute-start(f32[320,512]{1,0:T(8,128)S(1)} %pad_maximum_fusion), channel_id=1, source_target_pairs={{0,1},{1,0},{2,3},{3,2},{4,5},{5,4},{6,7},{7,6},{8,9},{9,8},{10,11... | collective-permute-start | bytes 1966088 | tf_op jit(solution)/shard_map/ppermute | solution.py:143
Sparse Core Ops, SparseCore 0:
  10.1 75.2 all-gather.1
  100.0 131.8 reduce-scatter.1

commit v14 on v13

--- a/solution.py
+++ b/solution.py
@@ -21,15 +21,23 @@
     return [(i, j) for i in range(count) for j in range(i + 1)]
 
 
-def _chol_kernel(a_ref, p_ref, po_ref, p2_ref, l_ref, w_ref, s_ref, blk_a, blk_b, blk_lt, blk_w, *, n, b):
+def _chol_kernel(
+    sh_ref, off_ref, po_ref, p2_ref, l_ref, w_ref, s_ref, blk_a, blk_b, blk_lt, blk_w, *, n, b, rows_p, pad, scale, shift
+):
     nb = n // b
     f32 = jnp.float32
     lower = lax.broadcasted_iota(jnp.int32, (b, b), 0) >= lax.broadcasted_iota(jnp.int32, (b, b), 1)
+    diag = lax.broadcasted_iota(jnp.int32, (b, b), 0) == lax.broadcasted_iota(jnp.int32, (b, b), 1)
+    first = lax.broadcasted_iota(jnp.int32, (1, b), 1) == 0
+    trace_row = sh_ref[pl.ds(rows_p + pad[0] * b, 1), pl.ds(pad[1] * b, b)] * scale
+    trace_total = jnp.sum(jnp.where(first, trace_row, 0.0), axis=1, keepdims=True)
+    delta = shift[0] * trace_total / shift[1]
     per_group = n // b
     for idx, (i, j) in enumerate(lower_blocks(n // b)):
         g, c = divmod(idx, per_group)
-        blk = a_ref[pl.ds(g * b, b), pl.ds(c * b, b)]
+        blk = sh_ref[pl.ds(rows_p + g * b, b), pl.ds(c * b, b)] * scale
         if i == j:
+            blk = blk + jnp.where(diag, delta, 0.0)
             s_ref[pl.ds(i * b, b), pl.ds(i * b, b)] = jnp.where(lower, blk, jnp.transpose(blk))
         else:
             s_ref[pl.ds(i * b, b), pl.ds(j * b, b)] = blk
@@ -86,17 +94,21 @@
                 w_ii, acc, precision=HI, preferred_element_type=f32
             )
     inverse = w_ref[...]
-    panel_out = lax.dot_general(p_ref[...], inverse, NT, precision=HI, preferred_element_type=f32)
+    p_rows = lax.broadcasted_iota(jnp.int32, (rows_p, n), 0).astype(f32) + off_ref[:, 0:1]
+    p_cols = lax.broadcasted_iota(jnp.int32, (rows_p, n), 1).astype(f32)
+    panel_s = sh_ref[pl.ds(0, rows_p), :] * scale + jnp.where(p_rows == p_cols, delta, 0.0)
+    panel_out = lax.dot_general(panel_s, inverse, NT, precision=HI, preferred_element_type=f32)
     po_ref[...] = panel_out
     p2_ref[...] = jnp.dot(panel_out, inverse, precision=HI, preferred_element_type=f32)
 
 
-def chol_and_inverse(a, panel, block=128):
-    n = panel.shape[1]
+def chol_and_inverse(shared, offset, rows_p, pad, scale, shift, block=128):
+    n = shared.shape[1]
+    panel = jax.ShapeDtypeStruct((rows_p, n), jnp.float32)
     f32 = jnp.float32
     vmem = pl.BlockSpec(memory_space=pltpu.VMEM)
     return pl.pallas_call(
-        functools.partial(_chol_kernel, n=n, b=block),
+        functools.partial(_chol_kernel, n=n, b=block, rows_p=rows_p, pad=pad, scale=scale, shift=shift),
         out_shape=(jax.ShapeDtypeStruct(panel.shape, f32), jax.ShapeDtypeStruct(panel.shape, f32)),
         in_specs=[vmem, vmem],
         out_specs=(vmem, vmem),
@@ -112,7 +124,7 @@
         cost_estimate=pl.CostEstimate(
             flops=2 * n * n * n + 4 * panel.shape[0] * n * n, bytes_accessed=5 * n * n * 4, transcendentals=n
         ),
-    )(a, panel)
+    )(shared, offset)
 
 
 def reduce_by_halving(x, axis, count):
@@ -185,7 +197,7 @@
         [jnp.concatenate(pieces[g * per_group : (g + 1) * per_group], axis=1) for g in range(groups)], axis=0
     )
     panel_in = jnp.concatenate([main_t, packed], axis=0)
-    shared = reduce_by_halving(panel_in, "par", par_count) / param_total
+    shared = reduce_by_halving(panel_in, "par", par_count)
 
     lhs = jnp.concatenate([mine, head], axis=0)
     big = lax.dot_general(lhs, centered, contract, preferred_element_type=f32)
@@ -193,28 +205,20 @@
     tile = big[:row_count]
     band_t = big[row_count:]
 
-    panel_g = shared[:row_count]
-    square_g = shared[row_count:]
     pad_g, pad_c = divmod(first_pad, per_group)
-    trace_total = shared[row_count + pad_g * block, pad_c * block]
+    trace_total = shared[row_count + pad_g * block, pad_c * block] / param_total
     shift_value = shift_scale * trace_total / sample_total
 
     eye = jnp.arange(PANEL, dtype=jnp.int32)
     global_rows = row_index * row_count + jnp.arange(row_count, dtype=jnp.int32)
     global_cols = col_index * col_width + jnp.arange(col_width, dtype=jnp.int32)
-    pr = jnp.arange(groups * block, dtype=jnp.int32)[:, None]
-    pc = jnp.arange(PANEL, dtype=jnp.int32)[None, :]
-    on_diag = jnp.zeros((groups * block, PANEL), bool)
-    for idx, (i, j) in enumerate(lower_blocks(per_group)):
-        if i == j:
-            g, c = divmod(idx, per_group)
-            on_diag = on_diag | ((pr // block == g) & (pc // block == c) & (pr % block == pc % block))
-    square_s = square_g + jnp.where(on_diag, shift_value, 0.0)
-    panel_s = panel_g + jnp.where(global_rows[:, None] == eye[None, :], shift_value, 0.0)
     band_s = band_t + jnp.where(eye[:, None] == global_cols[None, :], shift_value, 0.0)
     tile_s = tile + jnp.where(global_rows[:, None] == global_cols[None, :], shift_value, 0.0)
-
-    panel_out, projected = chol_and_inverse(square_s, panel_s)
+    offset = jnp.full((1, 128), row_index * row_count, f32)
+
+    panel_out, projected = chol_and_inverse(
+        shared, offset, row_count, (pad_g, pad_c), 1.0 / param_total, (shift_scale, float(sample_total))
+    )
     schur_tile = tile_s - jnp.dot(projected, band_s, precision=HI, preferred_element_type=f32)
     return (panel_out, schur_tile)
 

time: 247 us -> 246 us (level)
  transfers between devices with their start and end apart: 9 -> 9, of which waited for: 8 -> 8; matrix products, arithmetic and copies ran while one was open for 3% -> 3% of each run, Pallas kernels for 25% -> 26%
where the time goes in v14:
time: 246 us
  waiting for transfers between devices  107 us (43%)
  Pallas kernels  63.1 us (26%)
  starting transfers between devices  36.5 us (15%)
  between operations  15 us (6%)
  matrix products  11.7 us (5%)
  other arithmetic  9.43 us (4%)
  local copies, waits for them, and re-layouts  3.55 us (1%)
    all_gather x1, waiting for transfers between devices, shards(): gathered = lax.all_gather(jacobian, 'smp', axis=0, tiled=True)  77.4 us
    pallas_call x1, Pallas kernels, chol_and_inverse(): pl.pallas_call(functools.partial(_chol_kernel, n=n, b=block, rows_p=rows_...  63.1 us
    ppermute x3, waiting for transfers between devices, reduce_by_halving(): x = x + lax.ppermute(x, axis, partners(pair))  15.3 us
    ppermute x2, starting transfers between devices, reduce_by_halving(): x = keep + lax.ppermute(send, axis, partners(pair))  14.5 us
    ppermute x3, starting transfers between devices, reduce_by_halving(): x = x + lax.ppermute(x, axis, partners(pair))  12 us
    ppermute x2, starting transfers between devices, reduce_by_halving(): other = lax.ppermute(x, axis, partners(pair))  9.81 us
    ppermute x2, waiting for transfers between devices, reduce_by_halving(): x = keep + lax.ppermute(send, axis, partners(pair))  6.66 us
    ppermute x2, waiting for transfers between devices, reduce_by_halving(): other = lax.ppermute(x, axis, partners(pair))  6.52 us
  transfers between devices with their start and end apart: 9, of which 8 were waited for; matrix products, arithmetic and copies ran while one was open for 3% of the time, Pallas kernels for 26%

profile of v14, /device:TPU:1, one launch (start us, length us, event | category | flops | bytes accessed | tf_op | source)
XLA Modules:
  0.0 245.9 jit_solution(2880533695568204079)
XLA Ops:
  7.2 0.0 all-gather.2.cloned.1.call-start
  7.2 0.7 all-gather.2.cloned.1.call-update
  7.9 0.0 reduce-scatter.2.cloned.1.call-start
  7.9 77.4 %all-gather.2.cloned.1.call-done = bf16[4096,512]{1,0:T(8,128)(2,1)} async-done(((bf16[256,512]{1,0:T(8,128)(2,1)}), bf16[4096,512]{1,0:T(8,128)(2,1)}) %all-gather.2.cloned.1.call-update) | async-done | bytes 4194320 | tf_op jit(solution)/shard_map/all_gather | solution.py:174
  85.3 0.0 copy-start
  85.3 3.0 %convert_reduce_fusion = f32[512]{0:T(512)S(1)} fusion(bf16[4096,512]{1,0:T(8,128)(2,1)} %all-gather.2.cloned.1.call-done), kind=kLoop, calls=%fused_computation.1 | loop fusion | flops 4193792 | bytes 4196352 | tf_op jit(solution)/shard_map/reduce_sum | solution.py:176
  88.3 0.5 copy-done
  88.8 2.8 %multiply_reduce_fusion = (f32[]{:T(128)}, bf16[4096,512]{1,0:T(8,128)(2,1)S(1)}) fusion(f32[512]{0:T(512)S(1)} %broadcast_multiply_fusion.1, bf16[4096,512]{1,0:T(8,128)(2,1)S(1)} %copy-done), kind=kLoop, calls=%fused_computation.3 | loop fusion | flops 12582911 | bytes 8390660 | tf_op jit(solution)/shard_map/reduce_sum | solution.py:185
  91.6 0.0 copy-start.1
  91.7 1.8 copy-done.1
  93.5 6.4 %fusion.1 = f32[768,4096]{1,0:T(8,128)} fusion(bf16[4096,512]{1,0:T(8,128)(2,1)S(1)} %get-tuple-element.7, bf16[512,512]{1,0:T(8,128)(2,1)S(1)} %slice.48, bf16[256,512]{1,0:T(8,128)(2,1)S(1)} %constant_dynamic-slice_fusion.2), kind=kOutput, calls=%fused_computation.7 | convolution fusion | flops 3222798336 | bytes 17563648 | tf_op jit(solution)/shard_map/dot_general | solution.py:203
  99.9 0.0 reduce-scatter.2.cloned.1.call-update
  100.0 1.7 fusion.11
  101.7 0.7 fusion.16
  102.4 1.4 fusion.13
  103.8 0.1 maximum_maximum_fusion
  104.0 0.1 constant_dynamic-slice_fusion.1
  104.0 11.5 %collective-permute-start = (f32[320,512]{1,0:T(8,128)S(1)}, f32[320,512]{1,0:T(8,128)S(1)}, u32[]{:S(2)}, u32[]{:S(2)}) collective-permute-start(f32[320,512]{1,0:T(8,128)S(1)} %constant_dynamic-slice_fusion.1), channel_id=1, source_target_pairs={{0,1},{1,0},{2,3},{3,2},{4,5},{5,4},{6,7},{7,6},{8,9},{9,8},{10,11... | collective-permute-start | bytes 1966088 | tf_op jit(solution)/shard_map/ppermute | solution.py:149
  115.6 1.6 collective-permute-done
  117.2 0.1 dynamic-slice_add_fusion
  117.4 3.1 %collective-permute-start.1 = (f32[160,512]{1,0:T(8,128)S(1)}, f32[160,512]{1,0:T(8,128)S(1)}, u32[]{:S(2)}, u32[]{:S(2)}) collective-permute-start(f32[160,512]{1,0:T(8,128)S(1)} %constant_dynamic-slice_fusion), channel_id=1, source_target_pairs={{0,2},{1,9},{2,0},{3,11},{4,6},{5,13},{6,4},{7,15},{8,10},{9,1},{1... | collective-permute-start | bytes 983048 | tf_op jit(solution)/shard_map/ppermute | solution.py:149
  120.5 5.0 %collective-permute-done.1 = f32[160,512]{1,0:T(8,128)S(1)} collective-permute-done((f32[160,512]{1,0:T(8,128)S(1)}, f32[160,512]{1,0:T(8,128)S(1)}, u32[]{:S(2)}, u32[]{:S(2)}) %collective-permute-start.1) | collective-permute-done | bytes 327712 | tf_op jit(solution)/shard_map/ppermute | solution.py:149
  125.5 3.1 %collective-permute-start.2 = (f32[160,512]{1,0:T(8,128)S(1)}, f32[160,512]{1,0:T(8,128)S(1)}, u32[]{:S(2)}, u32[]{:S(2)}) collective-permute-start(f32[160,512]{1,0:T(8,128)S(1)} %dynamic-slice_add_fusion.1), channel_id=1, source_target_pairs={{0,8},{1,3},{2,10},{3,1},{4,12},{5,7},{6,14},{7,5},{8,0},{9,11},{1... | collective-permute-start | bytes 983048 | tf_op jit(solution)/shard_map/ppermute | solution.py:152
  128.7 5.0 %collective-permute-done.2 = f32[160,512]{1,0:T(8,128)S(1)} collective-permute-done((f32[160,512]{1,0:T(8,128)S(1)}, f32[160,512]{1,0:T(8,128)S(1)}, u32[]{:S(2)}, u32[]{:S(2)}) %collective-permute-start.2) | collective-permute-done | bytes 327712 | tf_op jit(solution)/shard_map/ppermute | solution.py:152
  133.7 4.6 %collective-permute-start.3 = (f32[160,512]{1,0:T(8,128)S(1)}, f32[160,512]{1,0:T(8,128)S(1)}, u32[]{:S(2)}, u32[]{:S(2)}) collective-permute-start(f32[160,512]{1,0:T(8,128)S(1)} %add.79), channel_id=1, source_target_pairs={{0,4},{1,17},{2,6},{3,19},{4,0},{5,21},{6,2},{7,23},{8,12},{9,25},... | collective-permute-start | bytes 983048 | tf_op jit(solution)/shard_map/ppermute | solution.py:152
  138.3 5.0 %collective-permute-done.3 = f32[160,512]{1,0:T(8,128)S(1)} collective-permute-done((f32[160,512]{1,0:T(8,128)S(1)}, f32[160,512]{1,0:T(8,128)S(1)}, u32[]{:S(2)}, u32[]{:S(2)}) %collective-permute-start.3) | collective-permute-done | bytes 327712 | tf_op jit(solution)/shard_map/ppermute | solution.py:152
  143.4 4.3 %collective-permute-start.4 = (f32[160,512]{1,0:T(8,128)S(1)}, f32[160,512]{1,0:T(8,128)S(1)}, u32[]{:S(2)}, u32[]{:S(2)}) collective-permute-start(f32[160,512]{1,0:T(8,128)S(1)} %add.80), channel_id=1, source_target_pairs={{0,16},{1,5},{2,18},{3,7},{4,20},{5,1},{6,22},{7,3},{8,24},{9,13},... | collective-permute-start | bytes 983048 | tf_op jit(solution)/shard_map/ppermute | solution.py:152
  147.7 5.3 %collective-permute-done.4 = f32[160,512]{1,0:T(8,128)S(1)} collective-permute-done((f32[160,512]{1,0:T(8,128)S(1)}, f32[160,512]{1,0:T(8,128)S(1)}, u32[]{:S(2)}, u32[]{:S(2)}) %collective-permute-start.4) | collective-permute-done | bytes 327712 | tf_op jit(solution)/shard_map/ppermute | solution.py:152
  153.0 2.8 %collective-permute-start.5 = (f32[160,512]{1,0:T(8,128)S(1)}, f32[160,512]{1,0:T(8,128)S(1)}, u32[]{:S(2)}, u32[]{:S(2)}) collective-permute-start(f32[160,512]{1,0:T(8,128)S(1)} %add.81), channel_id=1, source_target_pairs={{0,2},{1,9},{2,0},{3,11},{4,6},{5,13},{6,4},{7,15},{8,10},{9,1},{1... | collective-permute-start | bytes 983048 | tf_op jit(solution)/shard_map/ppermute | solution.py:155
  155.8 5.0 %collective-permute-done.5 = f32[160,512]{1,0:T(8,128)S(1)} collective-permute-done((f32[160,512]{1,0:T(8,128)S(1)}, f32[160,512]{1,0:T(8,128)S(1)}, u32[]{:S(2)}, u32[]{:S(2)}) %collective-permute-start.5) | collective-permute-done | bytes 327712 | tf_op jit(solution)/shard_map/ppermute | solution.py:155
  160.9 0.1 broadcast_select_fusion.3
  161.0 7.0 %collective-permute-start.6 = (f32[320,512]{1,0:T(8,128)S(1)}, f32[320,512]{1,0:T(8,128)S(1)}, u32[]{:S(2)}, u32[]{:S(2)}) collective-permute-start(f32[320,512]{1,0:T(8,128)S(1)} %pad_maximum_fusion.1), channel_id=1, source_target_pairs={{0,1},{1,0},{2,3},{3,2},{4,5},{5,4},{6,7},{7,6},{8,9},{9,8},{10,11... | collective-permute-start | bytes 1966088 | tf_op jit(solution)/shard_map/ppermute | solution.py:155
  168.0 1.5 collective-permute-done.6
  169.5 0.1 broadcast_select_fusion.1
  169.7 0.5 slice.56
  170.8 1.2 pad_maximum_fusion.sh_ref
  172.1 0.5 broadcast_in_dim.37.off_ref
  172.6 63.1 %shard_map.30 = (f32[256,512]{1,0:T(8,128)}, f32[256,512]{1,0:T(8,128)}) custom-call(f32[640,512]{1,0:T(8,128)} %pad_maximum_fusion.sh_ref, f32[1,128]{1,0:T(1,128)} %broadcast_in_dim.37.off_ref), custom_call_target="tpu_custom_call" | custom-call | flops 536870912 | bytes 5242880 | tf_op jit(solution)/shard_map/pallas_call | solution.py:110
  235.7 0.0 reduce-scatter.2.cloned.1.call-done
  235.7 1.0 broadcast_multiply_fusion
  236.7 2.3 convolution_subtract_fusion
  (14 shorter events, 0.4 us)
Async XLA Ops:
  7.2 78.2 %all-gather.2.cloned.1.call-start = ((), (), s32[]{:S(2)}) async-start(), calls=%async_computation.1 | async-start | bytes 4456448 | tf_op jit(solution)/shard_map/all_gather | solution.py:174
  7.9 227.8 %reduce-scatter.2.cloned.1.call-start = ((), (), s32[]{:S(2)}) async-start(), calls=%async_computation.2 | async-start | bytes 12976128 | tf_op jit(solution)/shard_map/reduce_scatter | solution.py:204
  85.3 3.4 %copy-start = (bf16[4096,512]{1,0:T(8,128)(2,1)S(1)}, bf16[4096,512]{1,0:T(8,128)(2,1)}, u32[]{:S(2)}) copy-start(bf16[4096,512]{1,0:T(8,128)(2,1)} %all-gather.2.cloned.1.call-done) | copy-start | bytes 12582916
  91.6 1.9 copy-start.1
  104.0 13.2 %collective-permute-start = (f32[320,512]{1,0:T(8,128)S(1)}, f32[320,512]{1,0:T(8,128)S(1)}, u32[]{:S(2)}, u32[]{:S(2)}) collective-permute-start(f32[320,512]{1,0:T(8,128)S(1)} %constant_dynamic-slice_fusion.1), channel_id=1, source_target_pairs={{0,1},{1,0},{2,3},{3,2},{4,5},{5,4},{6,7},{7,6},{8,9},{9,8},{10,11... | collective-permute-start | bytes 1966088 | tf_op jit(solution)/shard_map/ppermute | solution.py:149
  117.4 8.1 %collective-permute-start.1 = (f32[160,512]{1,0:T(8,128)S(1)}, f32[160,512]{1,0:T(8,128)S(1)}, u32[]{:S(2)}, u32[]{:S(2)}) collective-permute-start(f32[160,512]{1,0:T(8,128)S(1)} %constant_dynamic-slice_fusion), channel_id=1, source_target_pairs={{0,2},{1,9},{2,0},{3,11},{4,6},{5,13},{6,4},{7,15},{8,10},{9,1},{1... | collective-permute-start | bytes 983048 | tf_op jit(solution)/shard_map/ppermute | solution.py:149
  125.5 8.1 %collective-permute-start.2 = (f32[160,512]{1,0:T(8,128)S(1)}, f32[160,512]{1,0:T(8,128)S(1)}, u32[]{:S(2)}, u32[]{:S(2)}) collective-permute-start(f32[160,512]{1,0:T(8,128)S(1)} %dynamic-slice_add_fusion.1), channel_id=1, source_target_pairs={{0,8},{1,3},{2,10},{3,1},{4,12},{5,7},{6,14},{7,5},{8,0},{9,11},{1... | collective-permute-start | bytes 983048 | tf_op jit(solution)/shard_map/ppermute | solution.py:152
  133.7 9.6 %collective-permute-start.3 = (f32[160,512]{1,0:T(8,128)S(1)}, f32[160,512]{1,0:T(8,128)S(1)}, u32[]{:S(2)}, u32[]{:S(2)}) collective-permute-start(f32[160,512]{1,0:T(8,128)S(1)} %add.79), channel_id=1, source_target_pairs={{0,4},{1,17},{2,6},{3,19},{4,0},{5,21},{6,2},{7,23},{8,12},{9,25},... | collective-permute-start | bytes 983048 | tf_op jit(solution)/shard_map/ppermute | solution.py:152
  143.4 9.6 %collective-permute-start.4 = (f32[160,512]{1,0:T(8,128)S(1)}, f32[160,512]{1,0:T(8,128)S(1)}, u32[]{:S(2)}, u32[]{:S(2)}) collective-permute-start(f32[160,512]{1,0:T(8,128)S(1)} %add.80), channel_id=1, source_target_pairs={{0,16},{1,5},{2,18},{3,7},{4,20},{5,1},{6,22},{7,3},{8,24},{9,13},... | collective-permute-start | bytes 983048 | tf_op jit(solution)/shard_map/ppermute | solution.py:152
  153.0 7.8 %collective-permute-start.5 = (f32[160,512]{1,0:T(8,128)S(1)}, f32[160,512]{1,0:T(8,128)S(1)}, u32[]{:S(2)}, u32[]{:S(2)}) collective-permute-start(f32[160,512]{1,0:T(8,128)S(1)} %add.81), channel_id=1, source_target_pairs={{0,2},{1,9},{2,0},{3,11},{4,6},{5,13},{6,4},{7,15},{8,10},{9,1},{1... | collective-permute-start | bytes 983048 | tf_op jit(solution)/shard_map/ppermute | solution.py:155
  161.0 8.6 %collective-permute-start.6 = (f32[320,512]{1,0:T(8,128)S(1)}, f32[320,512]{1,0:T(8,128)S(1)}, u32[]{:S(2)}, u32[]{:S(2)}) collective-permute-start(f32[320,512]{1,0:T(8,128)S(1)} %pad_maximum_fusion.1), channel_id=1, source_target_pairs={{0,1},{1,0},{2,3},{3,2},{4,5},{5,4},{6,7},{7,6},{8,9},{9,8},{10,11... | collective-permute-start | bytes 1966088 | tf_op jit(solution)/shard_map/ppermute | solution.py:155
Sparse Core Ops, SparseCore 0:
  10.1 75.2 all-gather.1
  100.1 131.9 reduce-scatter.1

commit v15 on v14

--- a/solution.py
+++ b/solution.py
@@ -173,7 +173,8 @@
 
     gathered = lax.all_gather(jacobian, "smp", axis=0, tiled=True)
     widened = gathered.astype(f32)
-    col_mean = jnp.sum(widened, axis=0) / sample_total
+    ones = jnp.ones((8, sample_total), jnp.bfloat16)
+    col_mean = jnp.dot(ones, gathered, preferred_element_type=f32)[0] / sample_total
     centered = (widened - col_mean).astype(jnp.bfloat16)
     mine = lax.dynamic_slice_in_dim(centered, row_index * row_count, row_count, 0)
     head = centered[:PANEL]

time: 246 us -> 246 us (level)
  matrix products: 11.7 us -> 14.7 us
  other arithmetic: 9.43 us -> 6.46 us
    dot_general x0 -> x1, matrix products: none -> 2.98 us  [shards(): jnp.dot(ones, gathered, preferred_element_type=f32)[0] / sample_total]
    reduce_sum x1 -> x0, other arithmetic: 2.95 us -> none  [shards(): col_mean = jnp.sum(widened, axis=0) / sample_total]
where the time goes in v15:
time: 246 us
  waiting for transfers between devices  107 us (43%)
  Pallas kernels  63.1 us (26%)
  starting transfers between devices  36.5 us (15%)
  between operations  15 us (6%)
  matrix products  14.7 us (6%)
  other arithmetic  6.46 us (3%)
  local copies, waits for them, and re-layouts  3.53 us (1%)
    all_gather x1, waiting for transfers between devices, shards(): gathered = lax.all_gather(jacobian, 'smp', axis=0, tiled=True)  77.4 us
    pallas_call x1, Pallas kernels, chol_and_inverse(): pl.pallas_call(functools.partial(_chol_kernel, n=n, b=block, rows_p=rows_...  63.1 us
    ppermute x3, waiting for transfers between devices, reduce_by_halving(): x = x + lax.ppermute(x, axis, partners(pair))  15.3 us
    ppermute x2, starting transfers between devices, reduce_by_halving(): x = keep + lax.ppermute(send, axis, partners(pair))  14.5 us
    ppermute x3, starting transfers between devices, reduce_by_halving(): x = x + lax.ppermute(x, axis, partners(pair))  12 us
    ppermute x2, starting transfers between devices, reduce_by_halving(): other = lax.ppermute(x, axis, partners(pair))  9.81 us
    ppermute x2, waiting for transfers between devices, reduce_by_halving(): x = keep + lax.ppermute(send, axis, partners(pair))  6.66 us
    ppermute x2, waiting for transfers between devices, reduce_by_halving(): other = lax.ppermute(x, axis, partners(pair))  6.52 us
  transfers between devices with their start and end apart: 9, of which 8 were waited for; matrix products, arithmetic and copies ran while one was open for 3% of the time, Pallas kernels for 26%

profile of v15, /device:TPU:1, one launch (start us, length us, event | category | flops | bytes accessed | tf_op | source)
XLA Modules:
  0.0 245.8 jit_solution(17114133257751644797)
XLA Ops:
  7.2 0.0 all-gather.2.cloned.1.call-start
  7.2 0.7 all-gather.2.cloned.1.call-update
  7.9 0.0 reduce-scatter.2.cloned.1.call-start
  7.9 77.4 %all-gather.2.cloned.1.call-done = bf16[4096,512]{1,0:T(8,128)(2,1)} async-done(((bf16[256,512]{1,0:T(8,128)(2,1)}), bf16[4096,512]{1,0:T(8,128)(2,1)}) %all-gather.2.cloned.1.call-update) | async-done | bytes 4194320 | tf_op jit(solution)/shard_map/all_gather | solution.py:174
  85.3 0.0 copy-start
  85.3 3.0 %convolution_multiply_fusion = f32[1,512]{1,0:T(1,128)S(1)} fusion(bf16[4096,512]{1,0:T(8,128)(2,1)} %all-gather.2.cloned.1.call-done), kind=kOutput, calls=%fused_computation.5 | convolution fusion | flops 4194816 | bytes 4196352 | tf_op jit(solution)/shard_map/dot_general | solution.py:177
  88.3 0.5 copy-done
  88.8 2.8 %multiply_reduce_fusion = (f32[]{:T(128)}, bf16[4096,512]{1,0:T(8,128)(2,1)S(1)}) fusion(f32[512]{0:T(512)S(1)} %bitcast.6, bf16[4096,512]{1,0:T(8,128)(2,1)S(1)} %copy-done), kind=kLoop, calls=%fused_computation | loop fusion | flops 12582911 | bytes 8390660 | tf_op jit(solution)/shard_map/reduce_sum | solution.py:186
  91.6 0.0 copy-start.1
  91.7 1.8 copy-done.1
  93.5 6.4 %fusion = f32[768,4096]{1,0:T(8,128)} fusion(bf16[4096,512]{1,0:T(8,128)(2,1)S(1)} %get-tuple-element.7, bf16[512,512]{1,0:T(8,128)(2,1)S(1)} %slice.54, bf16[256,512]{1,0:T(8,128)(2,1)S(1)} %constant_dynamic-slice_fusion.2), kind=kOutput, calls=%fused_computation.6 | convolution fusion | flops 3222798336 | bytes 17563648 | tf_op jit(solution)/shard_map/dot_general | solution.py:204
  99.9 0.0 reduce-scatter.2.cloned.1.call-update
  99.9 1.7 fusion.12
  101.6 0.7 fusion.16
  102.4 1.4 fusion.14
  103.8 0.1 maximum_maximum_fusion
  103.9 0.1 constant_dynamic-slice_fusion.1
  104.0 11.5 %collective-permute-start = (f32[320,512]{1,0:T(8,128)S(1)}, f32[320,512]{1,0:T(8,128)S(1)}, u32[]{:S(2)}, u32[]{:S(2)}) collective-permute-start(f32[320,512]{1,0:T(8,128)S(1)} %constant_dynamic-slice_fusion.1), channel_id=1, source_target_pairs={{0,1},{1,0},{2,3},{3,2},{4,5},{5,4},{6,7},{7,6},{8,9},{9,8},{10,11... | collective-permute-start | bytes 1966088 | tf_op jit(solution)/shard_map/ppermute | solution.py:149
  115.5 1.6 collective-permute-done
  117.2 0.1 dynamic-slice_add_fusion
  117.3 3.1 %collective-permute-start.1 = (f32[160,512]{1,0:T(8,128)S(1)}, f32[160,512]{1,0:T(8,128)S(1)}, u32[]{:S(2)}, u32[]{:S(2)}) collective-permute-start(f32[160,512]{1,0:T(8,128)S(1)} %constant_dynamic-slice_fusion), channel_id=1, source_target_pairs={{0,2},{1,9},{2,0},{3,11},{4,6},{5,13},{6,4},{7,15},{8,10},{9,1},{1... | collective-permute-start | bytes 983048 | tf_op jit(solution)/shard_map/ppermute | solution.py:149
  120.4 5.0 %collective-permute-done.1 = f32[160,512]{1,0:T(8,128)S(1)} collective-permute-done((f32[160,512]{1,0:T(8,128)S(1)}, f32[160,512]{1,0:T(8,128)S(1)}, u32[]{:S(2)}, u32[]{:S(2)}) %collective-permute-start.1) | collective-permute-done | bytes 327712 | tf_op jit(solution)/shard_map/ppermute | solution.py:149
  125.5 3.1 %collective-permute-start.2 = (f32[160,512]{1,0:T(8,128)S(1)}, f32[160,512]{1,0:T(8,128)S(1)}, u32[]{:S(2)}, u32[]{:S(2)}) collective-permute-start(f32[160,512]{1,0:T(8,128)S(1)} %dynamic-slice_add_fusion.1), channel_id=1, source_target_pairs={{0,8},{1,3},{2,10},{3,1},{4,12},{5,7},{6,14},{7,5},{8,0},{9,11},{1... | collective-permute-start | bytes 983048 | tf_op jit(solution)/shard_map/ppermute | solution.py:152
  128.6 5.0 %collective-permute-done.2 = f32[160,512]{1,0:T(8,128)S(1)} collective-permute-done((f32[160,512]{1,0:T(8,128)S(1)}, f32[160,512]{1,0:T(8,128)S(1)}, u32[]{:S(2)}, u32[]{:S(2)}) %collective-permute-start.2) | collective-permute-done | bytes 327712 | tf_op jit(solution)/shard_map/ppermute | solution.py:152
  133.6 4.6 %collective-permute-start.3 = (f32[160,512]{1,0:T(8,128)S(1)}, f32[160,512]{1,0:T(8,128)S(1)}, u32[]{:S(2)}, u32[]{:S(2)}) collective-permute-start(f32[160,512]{1,0:T(8,128)S(1)} %add.79), channel_id=1, source_target_pairs={{0,4},{1,17},{2,6},{3,19},{4,0},{5,21},{6,2},{7,23},{8,12},{9,25},... | collective-permute-start | bytes 983048 | tf_op jit(solution)/shard_map/ppermute | solution.py:152
  138.3 5.0 %collective-permute-done.3 = f32[160,512]{1,0:T(8,128)S(1)} collective-permute-done((f32[160,512]{1,0:T(8,128)S(1)}, f32[160,512]{1,0:T(8,128)S(1)}, u32[]{:S(2)}, u32[]{:S(2)}) %collective-permute-start.3) | collective-permute-done | bytes 327712 | tf_op jit(solution)/shard_map/ppermute | solution.py:152
  143.3 4.3 %collective-permute-start.4 = (f32[160,512]{1,0:T(8,128)S(1)}, f32[160,512]{1,0:T(8,128)S(1)}, u32[]{:S(2)}, u32[]{:S(2)}) collective-permute-start(f32[160,512]{1,0:T(8,128)S(1)} %add.80), channel_id=1, source_target_pairs={{0,16},{1,5},{2,18},{3,7},{4,20},{5,1},{6,22},{7,3},{8,24},{9,13},... | collective-permute-start | bytes 983048 | tf_op jit(solution)/shard_map/ppermute | solution.py:152
  147.6 5.3 %collective-permute-done.4 = f32[160,512]{1,0:T(8,128)S(1)} collective-permute-done((f32[160,512]{1,0:T(8,128)S(1)}, f32[160,512]{1,0:T(8,128)S(1)}, u32[]{:S(2)}, u32[]{:S(2)}) %collective-permute-start.4) | collective-permute-done | bytes 327712 | tf_op jit(solution)/shard_map/ppermute | solution.py:152
  153.0 2.8 %collective-permute-start.5 = (f32[160,512]{1,0:T(8,128)S(1)}, f32[160,512]{1,0:T(8,128)S(1)}, u32[]{:S(2)}, u32[]{:S(2)}) collective-permute-start(f32[160,512]{1,0:T(8,128)S(1)} %add.81), channel_id=1, source_target_pairs={{0,2},{1,9},{2,0},{3,11},{4,6},{5,13},{6,4},{7,15},{8,10},{9,1},{1... | collective-permute-start | bytes 983048 | tf_op jit(solution)/shard_map/ppermute | solution.py:155
  155.8 5.0 %collective-permute-done.5 = f32[160,512]{1,0:T(8,128)S(1)} collective-permute-done((f32[160,512]{1,0:T(8,128)S(1)}, f32[160,512]{1,0:T(8,128)S(1)}, u32[]{:S(2)}, u32[]{:S(2)}) %collective-permute-start.5) | collective-permute-done | bytes 327712 | tf_op jit(solution)/shard_map/ppermute | solution.py:155
  160.8 0.1 broadcast_select_fusion.3
  160.9 7.0 %collective-permute-start.6 = (f32[320,512]{1,0:T(8,128)S(1)}, f32[320,512]{1,0:T(8,128)S(1)}, u32[]{:S(2)}, u32[]{:S(2)}) collective-permute-start(f32[320,512]{1,0:T(8,128)S(1)} %pad_maximum_fusion.1), channel_id=1, source_target_pairs={{0,1},{1,0},{2,3},{3,2},{4,5},{5,4},{6,7},{7,6},{8,9},{9,8},{10,11... | collective-permute-start | bytes 1966088 | tf_op jit(solution)/shard_map/ppermute | solution.py:155
  168.0 1.5 collective-permute-done.6
  169.5 0.1 broadcast_select_fusion.1
  169.6 0.5 slice.62
  170.8 1.2 pad_maximum_fusion.sh_ref
  172.0 0.5 broadcast_in_dim.41.off_ref
  172.5 63.1 %shard_map.30 = (f32[256,512]{1,0:T(8,128)}, f32[256,512]{1,0:T(8,128)}) custom-call(f32[640,512]{1,0:T(8,128)} %pad_maximum_fusion.sh_ref, f32[1,128]{1,0:T(1,128)} %broadcast_in_dim.41.off_ref), custom_call_target="tpu_custom_call" | custom-call | flops 536870912 | bytes 5242880 | tf_op jit(solution)/shard_map/pallas_call | solution.py:110
  235.6 0.0 reduce-scatter.2.cloned.1.call-done
  235.6 1.0 broadcast_multiply_fusion
  236.6 2.3 convolution_subtract_fusion
  (13 shorter events, 0.4 us)
Async XLA Ops:
  7.2 78.2 %all-gather.2.cloned.1.call-start = ((), (), s32[]{:S(2)}) async-start(), calls=%async_computation.1 | async-start | bytes 4456448 | tf_op jit(solution)/shard_map/all_gather | solution.py:174
  7.9 227.7 %reduce-scatter.2.cloned.1.call-start = ((), (), s32[]{:S(2)}) async-start(), calls=%async_computation.2 | async-start | bytes 12976128 | tf_op jit(solution)/shard_map/reduce_scatter | solution.py:205
  85.3 3.4 %copy-start = (bf16[4096,512]{1,0:T(8,128)(2,1)S(1)}, bf16[4096,512]{1,0:T(8,128)(2,1)}, u32[]{:S(2)}) copy-start(bf16[4096,512]{1,0:T(8,128)(2,1)} %all-gather.2.cloned.1.call-done) | copy-start | bytes 12582916
  91.6 1.9 copy-start.1
  104.0 13.2 %collective-permute-start = (f32[320,512]{1,0:T(8,128)S(1)}, f32[320,512]{1,0:T(8,128)S(1)}, u32[]{:S(2)}, u32[]{:S(2)}) collective-permute-start(f32[320,512]{1,0:T(8,128)S(1)} %constant_dynamic-slice_fusion.1), channel_id=1, source_target_pairs={{0,1},{1,0},{2,3},{3,2},{4,5},{5,4},{6,7},{7,6},{8,9},{9,8},{10,11... | collective-permute-start | bytes 1966088 | tf_op jit(solution)/shard_map/ppermute | solution.py:149
  117.3 8.1 %collective-permute-start.1 = (f32[160,512]{1,0:T(8,128)S(1)}, f32[160,512]{1,0:T(8,128)S(1)}, u32[]{:S(2)}, u32[]{:S(2)}) collective-permute-start(f32[160,512]{1,0:T(8,128)S(1)} %constant_dynamic-slice_fusion), channel_id=1, source_target_pairs={{0,2},{1,9},{2,0},{3,11},{4,6},{5,13},{6,4},{7,15},{8,10},{9,1},{1... | collective-permute-start | bytes 983048 | tf_op jit(solution)/shard_map/ppermute | solution.py:149
  125.5 8.1 %collective-permute-start.2 = (f32[160,512]{1,0:T(8,128)S(1)}, f32[160,512]{1,0:T(8,128)S(1)}, u32[]{:S(2)}, u32[]{:S(2)}) collective-permute-start(f32[160,512]{1,0:T(8,128)S(1)} %dynamic-slice_add_fusion.1), channel_id=1, source_target_pairs={{0,8},{1,3},{2,10},{3,1},{4,12},{5,7},{6,14},{7,5},{8,0},{9,11},{1... | collective-permute-start | bytes 983048 | tf_op jit(solution)/shard_map/ppermute | solution.py:152
  133.6 9.6 %collective-permute-start.3 = (f32[160,512]{1,0:T(8,128)S(1)}, f32[160,512]{1,0:T(8,128)S(1)}, u32[]{:S(2)}, u32[]{:S(2)}) collective-permute-start(f32[160,512]{1,0:T(8,128)S(1)} %add.79), channel_id=1, source_target_pairs={{0,4},{1,17},{2,6},{3,19},{4,0},{5,21},{6,2},{7,23},{8,12},{9,25},... | collective-permute-start | bytes 983048 | tf_op jit(solution)/shard_map/ppermute | solution.py:152
  143.3 9.6 %collective-permute-start.4 = (f32[160,512]{1,0:T(8,128)S(1)}, f32[160,512]{1,0:T(8,128)S(1)}, u32[]{:S(2)}, u32[]{:S(2)}) collective-permute-start(f32[160,512]{1,0:T(8,128)S(1)} %add.80), channel_id=1, source_target_pairs={{0,16},{1,5},{2,18},{3,7},{4,20},{5,1},{6,22},{7,3},{8,24},{9,13},... | collective-permute-start | bytes 983048 | tf_op jit(solution)/shard_map/ppermute | solution.py:152
  153.0 7.8 %collective-permute-start.5 = (f32[160,512]{1,0:T(8,128)S(1)}, f32[160,512]{1,0:T(8,128)S(1)}, u32[]{:S(2)}, u32[]{:S(2)}) collective-permute-start(f32[160,512]{1,0:T(8,128)S(1)} %add.81), channel_id=1, source_target_pairs={{0,2},{1,9},{2,0},{3,11},{4,6},{5,13},{6,4},{7,15},{8,10},{9,1},{1... | collective-permute-start | bytes 983048 | tf_op jit(solution)/shard_map/ppermute | solution.py:155
  160.9 8.6 %collective-permute-start.6 = (f32[320,512]{1,0:T(8,128)S(1)}, f32[320,512]{1,0:T(8,128)S(1)}, u32[]{:S(2)}, u32[]{:S(2)}) collective-permute-start(f32[320,512]{1,0:T(8,128)S(1)} %pad_maximum_fusion.1), channel_id=1, source_target_pairs={{0,1},{1,0},{2,3},{3,2},{4,5},{5,4},{6,7},{7,6},{8,9},{9,8},{10,11... | collective-permute-start | bytes 1966088 | tf_op jit(solution)/shard_map/ppermute | solution.py:155
Sparse Core Ops, SparseCore 0:
  10.1 75.2 all-gather.1
  100.0 131.9 reduce-scatter.1
